TPU v7x, 32 devices: a whole 2x2x4 slice. The times are simulated.
32 devices in a mesh: groups: 2 (over x), inst: 2 (over core), section: 8 (over z, y).
Axes of the slice: x: 2, y: 2, z: 4, core: 2. Of those that a mesh axis runs over, the one named last changes fastest.
Arguments:
- tokens: bfloat16 [4, 4, 8, 8192], P(('groups', 'inst')), parts along dimension 0, may hold values from -8 to 8
- kv_pool: bfloat16 [4, 8, 16, 2, 8, 128, 128], P(('groups', 'inst'), 'section'), parts along dimension 0, may hold values from -7.125 to 7.125
- page_table: int32 [4, 8, 2], P(('groups', 'inst')), parts along dimension 0, may hold values from 0 to 15, as said below
- lengths: int32 [4, 8], P(('groups', 'inst')), parts along dimension 0, may hold values from 1 to 256, 1280 in all within a row
- migrate_ids: int32 [4, 2], P(('groups', 'inst')), parts along dimension 0, may hold values from 0 to 7, as said below
- norm_gain: float32 [8, 8192], P('section'), may hold values from 0.5 to 1.5
- out_scale: float32 [8, 8192], P('section'), may hold values from 0.5 to 3
Outputs:
- section_rows: bfloat16 [4, 8, 4, 8, 8192], P(('groups', 'inst'), 'section'), parts along dimension 0
- arrived: bfloat16 [4, 8, 2, 2, 2, 8, 128, 128], P(('groups', 'inst'), 'section'), parts along dimension 0
There are 2 independent parts, one for each index of `groups`. A program takes and returns all parts, laid end to end along the dimension named above; an argument that names none is the same for every part. Nothing has to cross between parts.
Inputs may be any that keep to these rules, and one draw needn't show every extreme that they name: `page_table`: each instance's table names each of its 16 pages exactly once. `migrate_ids`: the 2 requests of one instance are different.
All inputs are finite; a program needn't handle non-finite values.
Results may differ from a plain program's by a relative error of at most 0.0091.
Values may be sent and summed in bfloat16 or wider, within the bound.
No kernel may reach another device: no remote copies, remote signals or barrier semaphores. Data moves between devices by JAX's collectives and lax.ppermute only.
A program may use at most 128 MiB of HBM per device.

v0:
```python
import math

import jax
import jax.numpy as jnp
from jax import lax
from jax.sharding import PartitionSpec as P


def partner(block, axis, stride):
    count = lax.axis_size(axis)
    route = []
    for low in range(count):
        high = low | 1 << stride
        if high != low and high < count:
            route += [(low, high), (high, low)]
    return lax.ppermute(block, axis, route)


def passed_along(array, axis, by):
    peers = lax.axis_size(axis)
    pairs = [(i, i + by) for i in range(peers) if 0 <= i + by < peers]
    return lax.ppermute(array, axis, pairs)


def gather_slots(pool, table):
    picked = pool[table]
    count = picked.shape[0]
    picked = jnp.transpose(picked, (0, 2, 3, 1, 4, 5))
    return picked.reshape(
        count, 2, picked.shape[2], picked.shape[3] * picked.shape[4], picked.shape[5]
    )


def to_slots(pages):
    count = pages.shape[0]
    moved = jnp.transpose(pages, (0, 2, 3, 1, 4, 5))
    return moved.reshape(count, 2, moved.shape[2], moved.shape[3] * moved.shape[4], moved.shape[5])


def layer(hidden, caches, lens, fresh_buf, step, gain, scale):
    rows = hidden.shape[0]
    kv_heads = caches.shape[2]
    head = caches.shape[4]
    steps = fresh_buf.shape[0]
    wide = hidden.astype(jnp.float32)
    normed = wide * lax.rsqrt(jnp.mean(wide * wide, axis=-1, keepdims=True) + 1e-05) * gain
    heads = normed.reshape(rows, kv_heads, -1, head)
    query = heads.astype(jnp.bfloat16)
    fresh = jnp.mean(heads, axis=2).astype(jnp.bfloat16)
    fresh_buf = lax.dynamic_update_index_in_dim(fresh_buf, fresh, step, 0)
    factor = 1.0 / math.sqrt(head)
    keys = caches[:, 0]
    values = caches[:, 1]
    cache_scores = (
        jnp.einsum("rgqd,rgtd->rgqt", query, keys, preferred_element_type=jnp.float32) * factor
    )
    positions = jnp.arange(keys.shape[2])
    live = positions[None, :] < lens[:, None]
    cache_scores = jnp.where(live[:, None, None, :], cache_scores, -1e30)
    new_scores = (
        jnp.einsum("rgqd,jrgd->rgqj", query, fresh_buf, preferred_element_type=jnp.float32) * factor
    )
    done = jnp.arange(steps) <= step
    new_scores = jnp.where(done[None, None, None, :], new_scores, -1e30)
    top = jnp.maximum(
        jnp.max(cache_scores, axis=-1, keepdims=True), jnp.max(new_scores, axis=-1, keepdims=True)
    )
    cache_exp = jnp.exp(cache_scores - top)
    new_exp = jnp.exp(new_scores - top)
    total = jnp.sum(cache_exp, axis=-1, keepdims=True) + jnp.sum(new_exp, axis=-1, keepdims=True)
    cache_w = (cache_exp / total).astype(jnp.bfloat16)
    new_w = (new_exp / total).astype(jnp.bfloat16)
    attended = jnp.einsum("rgqt,rgtd->rgqd", cache_w, values, preferred_element_type=jnp.float32)
    attended = attended + jnp.einsum(
        "rgqj,jrgd->rgqd", new_w, fresh_buf, preferred_element_type=jnp.float32
    )
    result = (wide + scale * attended.reshape(rows, -1)).astype(jnp.bfloat16)
    return (result, fresh_buf)


def per_device(tokens, kv_pool, page_table, lengths, migrate_ids, norm_gain, out_scale):
    inputs = tokens[0]
    pool = kv_pool[0, 0]
    table = page_table[0]
    lens = lengths[0]
    moving = migrate_ids[0]
    gain = norm_gain[0]
    scale = out_scale[0]
    steps, reqs, width = inputs.shape
    kv_heads = pool.shape[2]
    page_len = pool.shape[3]
    head = pool.shape[4]
    caches = gather_slots(pool, table)
    chosen = table[moving]
    outgoing = pool[chosen]
    spots = jnp.arange(chosen.shape[1])[:, None] * page_len + jnp.arange(page_len)[None, :]
    keep = spots[None, :, :] < lens[moving][:, None, None]
    outgoing = jnp.where(keep[:, :, None, None, :, None], outgoing, jnp.zeros((), jnp.bfloat16))
    lens_used = lens
    received, arrived_rows = partner((outgoing, inputs[:, moving]), "inst", 0)
    arrived_lens = partner(lens[moving], "inst", 0)
    caches = caches.at[moving].set(to_slots(received))
    lens_used = lens.at[moving].set(arrived_lens)
    inputs = inputs.at[:, moving].set(arrived_rows)
    section = lax.axis_index("section")
    count = lax.axis_size("section")
    parts = 1
    block = reqs // parts
    items = steps * parts

    def tick(k, carry):
        incoming, fresh_buf, finished = carry
        item = k - section
        live = jnp.logical_and(item >= 0, item < items)
        safe = jnp.clip(item, 0, items - 1)
        step = safe // parts
        start = safe % parts * block
        first = lax.dynamic_index_in_dim(inputs, step, 0, keepdims=False)
        rows = jnp.where(section == 0, first, incoming)
        part_buf = fresh_buf
        result, part_new = layer(rows, caches, lens_used, part_buf, step, gain, scale)
        part_new = jnp.where(live, part_new, part_buf)
        fresh_buf = part_new
        zero = jnp.zeros((), jnp.int32)
        previous = lax.dynamic_slice(finished, (step, start, zero), (1, block, width))
        finished = lax.dynamic_update_slice(
            finished, jnp.where(live, result[None], previous), (step, start, zero)
        )
        passed = passed_along(result, "section", 1)
        return (passed, fresh_buf, finished)

    start_carry = (
        jnp.zeros((block, width), jnp.bfloat16),
        jnp.zeros((steps, reqs, kv_heads, head), jnp.bfloat16),
        jnp.zeros((steps, reqs, width), jnp.bfloat16),
    )
    _, _, finished = lax.fori_loop(0, items + count - 1, tick, start_carry)
    return (finished[None, None], received[None, None])


def solution(mesh):
    in_specs = (
        P(("groups", "inst"), None, None, None),
        P(("groups", "inst"), "section", None, None, None, None, None),
        P(("groups", "inst"), None, None),
        P(("groups", "inst"), None),
        P(("groups", "inst"), None),
        P("section", None),
        P("section", None),
    )
    out_specs = (
        P(("groups", "inst"), "section", None, None, None),
        P(("groups", "inst"), "section", None, None, None, None, None, None),
    )
    return jax.shard_map(
        per_device, mesh=mesh, in_specs=in_specs, out_specs=out_specs, check_vma=False
    )
```

profile of v0, /device:TPU:26, one launch (start us, length us, event | category | flops | bytes accessed | tf_op | source)
XLA Modules:
  0.0 255.0 jit_solution(2838461762568867262)
XLA Ops:
  4.2 4.3 %gather_fusion.4 = bf16[4,2,8,128,128]{4,3,2,1,0:T(8,128)(2,1)S(1)} fusion(bf16[16,2,8,128,128]{4,3,2,1,0:T(8,128)(2,1)} %bitcast.93, s32[1024]{0:T(1024)S(1)} %pad_clamp_fusion), kind=kCustom, calls=%fused_computation.4 | custom fusion | bytes 4194320 | tf_op jit(solution)/shard_map/gather | solution.py:95
  12.0 8.1 %gather_fusion.2 = bf16[16,2,8,128,128]{4,3,2,1,0:T(8,128)(2,1)} fusion(bf16[16,2,8,128,128]{4,3,2,1,0:T(8,128)(2,1)} %bitcast.94, s32[1024]{0:T(1024)S(1)} %pad_clamp_fusion.1), kind=kCustom, calls=%fused_computation.2 | custom fusion | bytes 16777280 | tf_op jit(solution)/shard_map/gather | solution.py:26
  20.1 10.3 %copy.39 = bf16[8,2,2,8,128,128]{5,4,1,3,2,0:T(8,128)(2,1)} copy(bf16[8,2,2,8,128,128]{5,4,3,2,1,0:T(8,128)(2,1)} %bitcast.92) | data formatting | bytes 16777216 | tf_op jit(solution)/shard_map/gather | solution.py:26
  35.9 5.2 %scatter_fusion.2 = bf16[8,2,8,256,128]{4,3,2,1,0:T(8,128)(2,1)} fusion(bf16[8,2,8,256,128]{4,3,2,1,0:T(8,128)(2,1)} %bitcast.91, s32[2]{0:T(128)S(1)} %fusion.33, bf16[2,2,8,256,128]{4,3,2,1,0:T(8,128)(2,1)S(1)} %bitcast.96), kind=kCustom, calls=%fused_computation.7 | custom fusion | bytes 6291464 | tf_op jit(solution)/shard_map/scatter | solution.py:102
  41.1 7.7 %copy.43 = bf16[8,2,8,256,128]{4,3,2,0,1:T(8,128)(2,1)} copy(bf16[8,2,8,256,128]{4,3,2,1,0:T(8,128)(2,1)} %scatter_fusion.2) | data formatting | bytes 16777216
  49.7 204.0 %while.20 = (s32[]{:T(128)}, bf16[8,8192]{1,0:T(8,128)(2,1)S(1)}, bf16[4,8,8,128]{3,0,2,1:T(4,128)(2,1)S(1)}, bf16[4,8,8192]{2,1,0:T(8,128)(2,1)}, pred[]{:T(512...) while((s32[]{:T(128)}, bf16[8,8192]{1,0:T(8,128)(2,1)S(1)}, ...), condition=%wide.region_10.11_spmd.clone, body=%wide.region_3.10_spmd.clone.sunk | while | flops 70312976 | bytes 14496192 | solution.py:137
  51.7 3.5 %fusion.59 = (f32[8,8,8]{2,1,0:T(8,128)S(1)}, f32[8,8,8,256]{3,2,1,0:T(8,128)S(1)}) fusion(bf16[8,2,8,256,128]{4,3,2,0,1:T(8,128)(2,1)} %get-tuple-element.490, bf16[8,8,8,128]{3,0,2,1:T(8,128)(2,1)S(1)} %convert_element_type.107, pred[8,256]{1,0:T(8,128)(4,1)S(1)} %iota_compare_fusion.5), kind=kOutput, calls=%fused_computation.62.clone.1 | convolution fusion | flops 33947136 | bytes 4853760 | tf_op jit(solution)/shard_map/while/body/eval_jaxpr/rgqd,rgtd->rgqt/dot_general | solution.py:55
  64.0 5.1 %collective-permute-done = bf16[8,8192]{1,0:T(8,128)(2,1)S(1)} collective-permute-done((bf16[8,8192]{1,0:T(8,128)(2,1)S(1)}, bf16[8,8192]{1,0:T(8,128)(2,1)S(1)}, u32[]{:S(2)}, u32[]{:S(2)}) %collective-permute-start) | collective-permute-done | bytes 131104 | tf_op jit(solution)/shard_map/while/body/eval_jaxpr/ppermute | solution.py:22
  82.5 5.2 %collective-permute-done = bf16[8,8192]{1,0:T(8,128)(2,1)S(1)} collective-permute-done((bf16[8,8192]{1,0:T(8,128)(2,1)S(1)}, bf16[8,8192]{1,0:T(8,128)(2,1)S(1)}, u32[]{:S(2)}, u32[]{:S(2)}) %collective-permute-start) | collective-permute-done | bytes 131104 | tf_op jit(solution)/shard_map/while/body/eval_jaxpr/ppermute | solution.py:22
  89.5 3.5 %fusion.59 = (f32[8,8,8]{2,1,0:T(8,128)S(1)}, f32[8,8,8,256]{3,2,1,0:T(8,128)S(1)}) fusion(bf16[8,2,8,256,128]{4,3,2,0,1:T(8,128)(2,1)} %get-tuple-element.490, bf16[8,8,8,128]{3,0,2,1:T(8,128)(2,1)S(1)} %convert_element_type.107, pred[8,256]{1,0:T(8,128)(4,1)S(1)} %iota_compare_fusion.5), kind=kOutput, calls=%fused_computation.62.clone.1 | convolution fusion | flops 33947136 | bytes 4853760 | tf_op jit(solution)/shard_map/while/body/eval_jaxpr/rgqd,rgtd->rgqt/dot_general | solution.py:55
  100.4 5.7 %collective-permute-done = bf16[8,8192]{1,0:T(8,128)(2,1)S(1)} collective-permute-done((bf16[8,8192]{1,0:T(8,128)(2,1)S(1)}, bf16[8,8192]{1,0:T(8,128)(2,1)S(1)}, u32[]{:S(2)}, u32[]{:S(2)}) %collective-permute-start) | collective-permute-done | bytes 131104 | tf_op jit(solution)/shard_map/while/body/eval_jaxpr/ppermute | solution.py:22
  108.0 3.5 %fusion.59 = (f32[8,8,8]{2,1,0:T(8,128)S(1)}, f32[8,8,8,256]{3,2,1,0:T(8,128)S(1)}) fusion(bf16[8,2,8,256,128]{4,3,2,0,1:T(8,128)(2,1)} %get-tuple-element.490, bf16[8,8,8,128]{3,0,2,1:T(8,128)(2,1)S(1)} %convert_element_type.107, pred[8,256]{1,0:T(8,128)(4,1)S(1)} %iota_compare_fusion.5), kind=kOutput, calls=%fused_computation.62.clone.1 | convolution fusion | flops 33947136 | bytes 4853760 | tf_op jit(solution)/shard_map/while/body/eval_jaxpr/rgqd,rgtd->rgqt/dot_general | solution.py:55
  118.8 5.7 %collective-permute-done = bf16[8,8192]{1,0:T(8,128)(2,1)S(1)} collective-permute-done((bf16[8,8192]{1,0:T(8,128)(2,1)S(1)}, bf16[8,8192]{1,0:T(8,128)(2,1)S(1)}, u32[]{:S(2)}, u32[]{:S(2)}) %collective-permute-start) | collective-permute-done | bytes 131104 | tf_op jit(solution)/shard_map/while/body/eval_jaxpr/ppermute | solution.py:22
  126.4 3.5 %fusion.59 = (f32[8,8,8]{2,1,0:T(8,128)S(1)}, f32[8,8,8,256]{3,2,1,0:T(8,128)S(1)}) fusion(bf16[8,2,8,256,128]{4,3,2,0,1:T(8,128)(2,1)} %get-tuple-element.490, bf16[8,8,8,128]{3,0,2,1:T(8,128)(2,1)S(1)} %convert_element_type.107, pred[8,256]{1,0:T(8,128)(4,1)S(1)} %iota_compare_fusion.5), kind=kOutput, calls=%fused_computation.62.clone.1 | convolution fusion | flops 33947136 | bytes 4853760 | tf_op jit(solution)/shard_map/while/body/eval_jaxpr/rgqd,rgtd->rgqt/dot_general | solution.py:55
  137.3 5.7 %collective-permute-done = bf16[8,8192]{1,0:T(8,128)(2,1)S(1)} collective-permute-done((bf16[8,8192]{1,0:T(8,128)(2,1)S(1)}, bf16[8,8192]{1,0:T(8,128)(2,1)S(1)}, u32[]{:S(2)}, u32[]{:S(2)}) %collective-permute-start) | collective-permute-done | bytes 131104 | tf_op jit(solution)/shard_map/while/body/eval_jaxpr/ppermute | solution.py:22
  155.7 5.7 %collective-permute-done = bf16[8,8192]{1,0:T(8,128)(2,1)S(1)} collective-permute-done((bf16[8,8192]{1,0:T(8,128)(2,1)S(1)}, bf16[8,8192]{1,0:T(8,128)(2,1)S(1)}, u32[]{:S(2)}, u32[]{:S(2)}) %collective-permute-start) | collective-permute-done | bytes 131104 | tf_op jit(solution)/shard_map/while/body/eval_jaxpr/ppermute | solution.py:22
  163.3 3.5 %fusion.59 = (f32[8,8,8]{2,1,0:T(8,128)S(1)}, f32[8,8,8,256]{3,2,1,0:T(8,128)S(1)}) fusion(bf16[8,2,8,256,128]{4,3,2,0,1:T(8,128)(2,1)} %get-tuple-element.490, bf16[8,8,8,128]{3,0,2,1:T(8,128)(2,1)S(1)} %convert_element_type.107, pred[8,256]{1,0:T(8,128)(4,1)S(1)} %iota_compare_fusion.5), kind=kOutput, calls=%fused_computation.62.clone.1 | convolution fusion | flops 33947136 | bytes 4853760 | tf_op jit(solution)/shard_map/while/body/eval_jaxpr/rgqd,rgtd->rgqt/dot_general | solution.py:55
  174.2 5.7 %collective-permute-done = bf16[8,8192]{1,0:T(8,128)(2,1)S(1)} collective-permute-done((bf16[8,8192]{1,0:T(8,128)(2,1)S(1)}, bf16[8,8192]{1,0:T(8,128)(2,1)S(1)}, u32[]{:S(2)}, u32[]{:S(2)}) %collective-permute-start) | collective-permute-done | bytes 131104 | tf_op jit(solution)/shard_map/while/body/eval_jaxpr/ppermute | solution.py:22
  181.7 3.5 %fusion.59 = (f32[8,8,8]{2,1,0:T(8,128)S(1)}, f32[8,8,8,256]{3,2,1,0:T(8,128)S(1)}) fusion(bf16[8,2,8,256,128]{4,3,2,0,1:T(8,128)(2,1)} %get-tuple-element.490, bf16[8,8,8,128]{3,0,2,1:T(8,128)(2,1)S(1)} %convert_element_type.107, pred[8,256]{1,0:T(8,128)(4,1)S(1)} %iota_compare_fusion.5), kind=kOutput, calls=%fused_computation.62.clone.1 | convolution fusion | flops 33947136 | bytes 4853760 | tf_op jit(solution)/shard_map/while/body/eval_jaxpr/rgqd,rgtd->rgqt/dot_general | solution.py:55
  192.6 5.7 %collective-permute-done = bf16[8,8192]{1,0:T(8,128)(2,1)S(1)} collective-permute-done((bf16[8,8192]{1,0:T(8,128)(2,1)S(1)}, bf16[8,8192]{1,0:T(8,128)(2,1)S(1)}, u32[]{:S(2)}, u32[]{:S(2)}) %collective-permute-start) | collective-permute-done | bytes 131104 | tf_op jit(solution)/shard_map/while/body/eval_jaxpr/ppermute | solution.py:22
  211.0 5.7 %collective-permute-done = bf16[8,8192]{1,0:T(8,128)(2,1)S(1)} collective-permute-done((bf16[8,8192]{1,0:T(8,128)(2,1)S(1)}, bf16[8,8192]{1,0:T(8,128)(2,1)S(1)}, u32[]{:S(2)}, u32[]{:S(2)}) %collective-permute-start) | collective-permute-done | bytes 131104 | tf_op jit(solution)/shard_map/while/body/eval_jaxpr/ppermute | solution.py:22
  229.5 5.7 %collective-permute-done = bf16[8,8192]{1,0:T(8,128)(2,1)S(1)} collective-permute-done((bf16[8,8192]{1,0:T(8,128)(2,1)S(1)}, bf16[8,8192]{1,0:T(8,128)(2,1)S(1)}, u32[]{:S(2)}, u32[]{:S(2)}) %collective-permute-start) | collective-permute-done | bytes 131104 | tf_op jit(solution)/shard_map/while/body/eval_jaxpr/ppermute | solution.py:22
  237.1 3.5 %fusion.59 = (f32[8,8,8]{2,1,0:T(8,128)S(1)}, f32[8,8,8,256]{3,2,1,0:T(8,128)S(1)}) fusion(bf16[8,2,8,256,128]{4,3,2,0,1:T(8,128)(2,1)} %get-tuple-element.490, bf16[8,8,8,128]{3,0,2,1:T(8,128)(2,1)S(1)} %convert_element_type.107, pred[8,256]{1,0:T(8,128)(4,1)S(1)} %iota_compare_fusion.5), kind=kOutput, calls=%fused_computation.62.clone.1 | convolution fusion | flops 33947136 | bytes 4853760 | tf_op jit(solution)/shard_map/while/body/eval_jaxpr/rgqd,rgtd->rgqt/dot_general | solution.py:55
  247.9 5.7 %collective-permute-done = bf16[8,8192]{1,0:T(8,128)(2,1)S(1)} collective-permute-done((bf16[8,8192]{1,0:T(8,128)(2,1)S(1)}, bf16[8,8192]{1,0:T(8,128)(2,1)S(1)}, u32[]{:S(2)}, u32[]{:S(2)}) %collective-permute-start) | collective-permute-done | bytes 131104 | tf_op jit(solution)/shard_map/while/body/eval_jaxpr/ppermute | solution.py:22
  (280 shorter events, 131.2 us)
Async XLA Ops:
  4.2 7.6 %copy-start.5 = (s32[1,8,2]{1,2,0:T(2,128)S(1)}, s32[1,8,2]{1,2,0:T(2,128)}, u32[]{:S(2)}) copy-start(s32[1,8,2]{1,2,0:T(2,128)} %param.11) | copy-start | bytes 196
  8.5 2.1 copy-start.4
  10.1 22.7 %collective-permute-start.3 = (bf16[2,2,2,8,128,128]{5,4,3,2,1,0:T(8,128)(2,1)}, bf16[2,2,2,8,128,128]{5,4,3,2,1,0:T(8,128)(2,1)S(1)}, u32[]{:S(2)}, u32[]{:S(2)}) collective-permute-start(bf16[2,2,2,8,128,128]{5,4,3,2,1,0:T(8,128)(2,1)} %broadcast_select_fusion.2), channel_id=1, source_target_pairs={{0,8},{8,0},{1,9},{9,1},{2,10},{10,2},{3,11},{11,3},{4,12},{12,4},... | collective-permute-start | bytes 6291464 | tf_op jit(solution)/shard_map/ppermute | solution.py:16
  10.1 20.4 %collective-permute-start.2 = (s32[2]{0:T(128)S(1)}, s32[2]{0:T(128)S(1)}, u32[]{:S(2)}, u32[]{:S(2)}) collective-permute-start(s32[2]{0:T(128)S(1)} %gather_fusion.1), channel_id=1, source_target_pairs={{0,8},{8,0},{1,9},{9,1},{2,10},{10,2},{3,11},{11,3},{4,12},{12,4},... | collective-permute-start | bytes 32 | tf_op jit(solution)/shard_map/ppermute | solution.py:16
  11.7 19.4 %collective-permute-start.1 = (bf16[4,2,8192]{2,0,1:T(4,128)(2,1)S(1)}, bf16[4,2,8192]{2,0,1:T(4,128)(2,1)S(1)}, u32[]{:S(2)}, u32[]{:S(2)}) collective-permute-start(bf16[4,2,8192]{2,0,1:T(4,128)(2,1)S(1)} %bitcast.105), channel_id=1, source_target_pairs={{0,8},{8,0},{1,9},{9,1},{2,10},{10,2},{3,11},{11,3},{4,12},{12,4},... | collective-permute-start | bytes 393224 | tf_op jit(solution)/shard_map/ppermute | solution.py:16
  32.8 1.3 copy-start
  41.1 8.6 %copy-start.2 = (f32[1,8192]{1,0:T(1,128)S(1)}, f32[1,8192]{1,0:T(1,128)}, u32[]{:S(2)}) copy-start(f32[1,8192]{1,0:T(1,128)} %param.15) | copy-start | bytes 98308
  41.1 8.6 %copy-start.3 = (f32[1,8192]{1,0:T(1,128)S(1)}, f32[1,8192]{1,0:T(1,128)}, u32[]{:S(2)}) copy-start(f32[1,8192]{1,0:T(1,128)} %param.14) | copy-start | bytes 98308
  49.6 204.0 %copy-start.1 = (bf16[2,2,2,8,128,128]{5,4,3,2,1,0:T(8,128)(2,1)S(1)}, bf16[2,2,2,8,128,128]{5,4,3,2,1,0:T(8,128)(2,1)}, u32[]{:S(2)}) copy-start(bf16[2,2,2,8,128,128]{5,4,3,2,1,0:T(8,128)(2,1)} %copy-done) | copy-start | bytes 6291460
  60.5 8.6 %collective-permute-start = (bf16[8,8192]{1,0:T(8,128)(2,1)S(1)}, bf16[8,8192]{1,0:T(8,128)(2,1)S(1)}, u32[]{:S(2)}, u32[]{:S(2)}) collective-permute-start(bf16[8,8192]{1,0:T(8,128)(2,1)S(1)} %get-tuple-element.446), channel_id=1, source_target_pairs={{0,1},{1,2},{2,3},{3,4},{4,5},{5,6},{6,7},{8,9},{9,10},{10,11},{11... | collective-permute-start | bytes 393224 | tf_op jit(solution)/shard_map/while/body/eval_jaxpr/ppermute | solution.py:22
  79.8 7.8 %collective-permute-start = (bf16[8,8192]{1,0:T(8,128)(2,1)S(1)}, bf16[8,8192]{1,0:T(8,128)(2,1)S(1)}, u32[]{:S(2)}, u32[]{:S(2)}) collective-permute-start(bf16[8,8192]{1,0:T(8,128)(2,1)S(1)} %get-tuple-element.446), channel_id=1, source_target_pairs={{0,1},{1,2},{2,3},{3,4},{4,5},{5,6},{6,7},{8,9},{9,10},{10,11},{11... | collective-permute-start | bytes 393224 | tf_op jit(solution)/shard_map/while/body/eval_jaxpr/ppermute | solution.py:22
  98.4 7.7 %collective-permute-start = (bf16[8,8192]{1,0:T(8,128)(2,1)S(1)}, bf16[8,8192]{1,0:T(8,128)(2,1)S(1)}, u32[]{:S(2)}, u32[]{:S(2)}) collective-permute-start(bf16[8,8192]{1,0:T(8,128)(2,1)S(1)} %get-tuple-element.446), channel_id=1, source_target_pairs={{0,1},{1,2},{2,3},{3,4},{4,5},{5,6},{6,7},{8,9},{9,10},{10,11},{11... | collective-permute-start | bytes 393224 | tf_op jit(solution)/shard_map/while/body/eval_jaxpr/ppermute | solution.py:22
  116.8 7.7 %collective-permute-start = (bf16[8,8192]{1,0:T(8,128)(2,1)S(1)}, bf16[8,8192]{1,0:T(8,128)(2,1)S(1)}, u32[]{:S(2)}, u32[]{:S(2)}) collective-permute-start(bf16[8,8192]{1,0:T(8,128)(2,1)S(1)} %get-tuple-element.446), channel_id=1, source_target_pairs={{0,1},{1,2},{2,3},{3,4},{4,5},{5,6},{6,7},{8,9},{9,10},{10,11},{11... | collective-permute-start | bytes 393224 | tf_op jit(solution)/shard_map/while/body/eval_jaxpr/ppermute | solution.py:22
  135.3 7.7 %collective-permute-start = (bf16[8,8192]{1,0:T(8,128)(2,1)S(1)}, bf16[8,8192]{1,0:T(8,128)(2,1)S(1)}, u32[]{:S(2)}, u32[]{:S(2)}) collective-permute-start(bf16[8,8192]{1,0:T(8,128)(2,1)S(1)} %get-tuple-element.446), channel_id=1, source_target_pairs={{0,1},{1,2},{2,3},{3,4},{4,5},{5,6},{6,7},{8,9},{9,10},{10,11},{11... | collective-permute-start | bytes 393224 | tf_op jit(solution)/shard_map/while/body/eval_jaxpr/ppermute | solution.py:22
  153.7 7.7 %collective-permute-start = (bf16[8,8192]{1,0:T(8,128)(2,1)S(1)}, bf16[8,8192]{1,0:T(8,128)(2,1)S(1)}, u32[]{:S(2)}, u32[]{:S(2)}) collective-permute-start(bf16[8,8192]{1,0:T(8,128)(2,1)S(1)} %get-tuple-element.446), channel_id=1, source_target_pairs={{0,1},{1,2},{2,3},{3,4},{4,5},{5,6},{6,7},{8,9},{9,10},{10,11},{11... | collective-permute-start | bytes 393224 | tf_op jit(solution)/shard_map/while/body/eval_jaxpr/ppermute | solution.py:22
  172.2 7.7 %collective-permute-start = (bf16[8,8192]{1,0:T(8,128)(2,1)S(1)}, bf16[8,8192]{1,0:T(8,128)(2,1)S(1)}, u32[]{:S(2)}, u32[]{:S(2)}) collective-permute-start(bf16[8,8192]{1,0:T(8,128)(2,1)S(1)} %get-tuple-element.446), channel_id=1, source_target_pairs={{0,1},{1,2},{2,3},{3,4},{4,5},{5,6},{6,7},{8,9},{9,10},{10,11},{11... | collective-permute-start | bytes 393224 | tf_op jit(solution)/shard_map/while/body/eval_jaxpr/ppermute | solution.py:22
  190.6 7.7 %collective-permute-start = (bf16[8,8192]{1,0:T(8,128)(2,1)S(1)}, bf16[8,8192]{1,0:T(8,128)(2,1)S(1)}, u32[]{:S(2)}, u32[]{:S(2)}) collective-permute-start(bf16[8,8192]{1,0:T(8,128)(2,1)S(1)} %get-tuple-element.446), channel_id=1, source_target_pairs={{0,1},{1,2},{2,3},{3,4},{4,5},{5,6},{6,7},{8,9},{9,10},{10,11},{11... | collective-permute-start | bytes 393224 | tf_op jit(solution)/shard_map/while/body/eval_jaxpr/ppermute | solution.py:22
  209.0 7.7 %collective-permute-start = (bf16[8,8192]{1,0:T(8,128)(2,1)S(1)}, bf16[8,8192]{1,0:T(8,128)(2,1)S(1)}, u32[]{:S(2)}, u32[]{:S(2)}) collective-permute-start(bf16[8,8192]{1,0:T(8,128)(2,1)S(1)} %get-tuple-element.446), channel_id=1, source_target_pairs={{0,1},{1,2},{2,3},{3,4},{4,5},{5,6},{6,7},{8,9},{9,10},{10,11},{11... | collective-permute-start | bytes 393224 | tf_op jit(solution)/shard_map/while/body/eval_jaxpr/ppermute | solution.py:22
  227.5 7.7 %collective-permute-start = (bf16[8,8192]{1,0:T(8,128)(2,1)S(1)}, bf16[8,8192]{1,0:T(8,128)(2,1)S(1)}, u32[]{:S(2)}, u32[]{:S(2)}) collective-permute-start(bf16[8,8192]{1,0:T(8,128)(2,1)S(1)} %get-tuple-element.446), channel_id=1, source_target_pairs={{0,1},{1,2},{2,3},{3,4},{4,5},{5,6},{6,7},{8,9},{9,10},{10,11},{11... | collective-permute-start | bytes 393224 | tf_op jit(solution)/shard_map/while/body/eval_jaxpr/ppermute | solution.py:22
  245.9 7.7 %collective-permute-start = (bf16[8,8192]{1,0:T(8,128)(2,1)S(1)}, bf16[8,8192]{1,0:T(8,128)(2,1)S(1)}, u32[]{:S(2)}, u32[]{:S(2)}) collective-permute-start(bf16[8,8192]{1,0:T(8,128)(2,1)S(1)} %get-tuple-element.446), channel_id=1, source_target_pairs={{0,1},{1,2},{2,3},{3,4},{4,5},{5,6},{6,7},{8,9},{9,10},{10,11},{11... | collective-permute-start | bytes 393224 | tf_op jit(solution)/shard_map/while/body/eval_jaxpr/ppermute | solution.py:22
where the time goes:
time: 257 us; the launch traced here: 255 us
  matrix products  76.1 us (30%)
  waiting for transfers between devices  62.1 us (24%)
  local copies, waits for them, and re-layouts  49.2 us (19%)
  other arithmetic  42.1 us (16%)
  starting transfers between devices  23.7 us (9%)
    ppermute x11, waiting for transfers between devices, passed_along(): return lax.ppermute(array, axis, pairs)  62.1 us
    dot_general x11, matrix products, layer(): jnp.einsum('rgqd,rgtd->rgqt', query, keys, preferred_element_type=jnp.flo...  38 us
    dot_general x11, matrix products, layer(): jnp.einsum('rgqt,rgtd->rgqd', cache_w, values, preferred_element_type=jnp...  32.3 us
    ppermute x11, starting transfers between devices, passed_along(): return lax.ppermute(array, axis, pairs)  23.1 us
    dynamic_update_slice x11, other arithmetic, tick(): lax.dynamic_update_slice(finished, jnp.where(live, result[None], previous...  19.2 us
    gather x2, local copies, waits for them, and re-layouts, gather_slots(): picked = pool[table]  18.5 us
    unnamed x17, local copies, waits for them, and re-layouts  12.5 us
    reduce_sum x11, other arithmetic, layer(): jnp.mean(wide * wide, axis=-1, keepdims=True) + 1e-05  12.1 us
  transfers between devices with their start and end apart: 14, of which 11 were waited for; matrix products, arithmetic and copies ran while one was open for 9% of the time, Pallas kernels for 0%

commit v1 on v0

v1 whole, which is shorter than its diff:
```python
import math

import jax
import jax.numpy as jnp
from jax import lax
from jax.sharding import PartitionSpec as P

CHUNKS = 2


def partner(block, axis, stride):
    count = lax.axis_size(axis)
    route = []
    for low in range(count):
        high = low | 1 << stride
        if high != low and high < count:
            route += [(low, high), (high, low)]
    return lax.ppermute(block, axis, route)


def passed_along(array, axis, by):
    peers = lax.axis_size(axis)
    pairs = [(i, i + by) for i in range(peers) if 0 <= i + by < peers]
    return lax.ppermute(array, axis, pairs)


def layer(rows, keys, values, lens, gain, scale):
    steps, reqs, width = rows.shape
    pages = keys.shape[1]
    kv_heads = keys.shape[2]
    page_len = keys.shape[3]
    head = keys.shape[4]
    group = width // (kv_heads * head)
    wide = rows.astype(jnp.float32)
    normed = wide * lax.rsqrt(jnp.mean(wide * wide, axis=-1, keepdims=True) + 1e-05) * gain
    heads = normed.reshape(steps, reqs, kv_heads, group, head)
    query = jnp.transpose(heads.astype(jnp.bfloat16), (1, 2, 0, 3, 4))
    query = query.reshape(reqs, kv_heads, steps * group, head)
    fresh = jnp.mean(heads, axis=3).astype(jnp.bfloat16)
    fresh = jnp.transpose(fresh, (1, 2, 0, 3))
    factor = 1.0 / math.sqrt(head)
    wide_query = jnp.broadcast_to(query[:, None], (reqs, pages) + query.shape[1:])
    cache_scores = (
        jnp.einsum("rjgxd,rjgpd->rjgxp", wide_query, keys, preferred_element_type=jnp.float32)
        * factor
    )
    positions = jnp.arange(pages)[:, None] * page_len + jnp.arange(page_len)[None, :]
    live = positions[None] < lens[:, None, None]
    cache_scores = jnp.where(live[:, :, None, None, :], cache_scores, -1e30)
    new_scores = (
        jnp.einsum("rgxd,rgsd->rgxs", query, fresh, preferred_element_type=jnp.float32) * factor
    )
    step_of = jnp.arange(steps * group) // group
    done = jnp.arange(steps)[None, :] <= step_of[:, None]
    new_scores = jnp.where(done[None, None], new_scores, -1e30)
    top = jnp.maximum(
        jnp.max(cache_scores, axis=(1, 4)), jnp.max(new_scores, axis=-1)
    )[..., None]
    cache_exp = jnp.exp(cache_scores - top[:, None])
    new_exp = jnp.exp(new_scores - top)
    total = jnp.sum(cache_exp, axis=(1, 4))[..., None] + jnp.sum(new_exp, axis=-1, keepdims=True)
    cache_w = (cache_exp / total[:, None]).astype(jnp.bfloat16)
    new_w = (new_exp / total).astype(jnp.bfloat16)
    attended = jnp.einsum(
        "rjgxp,rjgpd->rjgxd", cache_w, values, preferred_element_type=jnp.float32
    ).sum(axis=1)
    attended = attended + jnp.einsum(
        "rgxs,rgsd->rgxd", new_w, fresh, preferred_element_type=jnp.float32
    )
    attended = attended.reshape(reqs, kv_heads, steps, group, head)
    attended = jnp.transpose(attended, (2, 0, 1, 3, 4)).reshape(steps, reqs, width)
    return (wide + scale * attended).astype(jnp.bfloat16)


def per_device(tokens, kv_pool, page_table, lengths, migrate_ids, norm_gain, out_scale):
    inputs = tokens[0]
    pool = kv_pool[0, 0]
    table = page_table[0]
    lens = lengths[0]
    moving = migrate_ids[0]
    gain = norm_gain[0]
    scale = out_scale[0]
    steps, reqs, width = inputs.shape
    page_len = pool.shape[3]
    chosen = table[moving]
    outgoing = pool[chosen]
    spots = jnp.arange(chosen.shape[1])[:, None] * page_len + jnp.arange(page_len)[None, :]
    keep = spots[None, :, :] < lens[moving][:, None, None]
    outgoing = jnp.where(keep[:, :, None, None, :, None], outgoing, jnp.zeros((), jnp.bfloat16))
    received, arrived_rows = partner((outgoing, inputs[:, moving]), "inst", 0)
    arrived_lens = partner(lens[moving], "inst", 0)
    caches = pool[table].at[moving].set(received)
    lens_used = lens.at[moving].set(arrived_lens)
    inputs = inputs.at[:, moving].set(arrived_rows)
    keys = caches[:, :, 0]
    values = caches[:, :, 1]
    section = lax.axis_index("section")
    count = lax.axis_size("section")
    chunks = CHUNKS
    block = reqs // chunks

    def tick(k, carry):
        incoming, finished = carry
        item = k - section
        live = jnp.logical_and(item >= 0, item < chunks)
        start = jnp.clip(item, 0, chunks - 1) * block
        zero = jnp.zeros((), jnp.int32)
        first = lax.dynamic_slice_in_dim(inputs, start, block, 1)
        rows = jnp.where(section == 0, first, incoming)
        part_keys = lax.dynamic_slice_in_dim(keys, start, block, 0)
        part_values = lax.dynamic_slice_in_dim(values, start, block, 0)
        part_lens = lax.dynamic_slice_in_dim(lens_used, start, block, 0)
        result = layer(rows, part_keys, part_values, part_lens, gain, scale)
        previous = lax.dynamic_slice_in_dim(finished, start, block, 1)
        finished = lax.dynamic_update_slice(
            finished, jnp.where(live, result, previous), (zero, start, zero)
        )
        passed = passed_along(result, "section", 1)
        return (passed, finished)

    start_carry = (
        jnp.zeros((steps, block, width), jnp.bfloat16),
        jnp.zeros((steps, reqs, width), jnp.bfloat16),
    )
    _, finished = lax.fori_loop(0, chunks + count - 1, tick, start_carry)
    return (finished[None, None], received[None, None])


def solution(mesh):
    in_specs = (
        P(("groups", "inst"), None, None, None),
        P(("groups", "inst"), "section", None, None, None, None, None),
        P(("groups", "inst"), None, None),
        P(("groups", "inst"), None),
        P(("groups", "inst"), None),
        P("section", None),
        P("section", None),
    )
    out_specs = (
        P(("groups", "inst"), "section", None, None, None),
        P(("groups", "inst"), "section", None, None, None, None, None, None),
    )
    return jax.shard_map(
        per_device, mesh=mesh, in_specs=in_specs, out_specs=out_specs, check_vma=False
    )
```

time: 257 us -> 190 us (0.74)
  matrix products: 76.1 us -> 40.3 us
  other arithmetic: 42.1 us -> 19.4 us
  local copies, waits for them, and re-layouts: 49.2 us -> 40 us
  waiting for transfers between devices: 62.1 us -> 67.7 us
  starting transfers between devices: 23.7 us -> 20 us
    dot_general x44 -> x36, matrix products: 76.1 us -> 40.3 us  [the longest x9 29.2 us: layer(): jnp.einsum('rjgxd,rjgpd->rjgxp', wide_query, keys, preferred_element_type...]
    dynamic_update_slice x11 -> x9, other arithmetic: 19.2 us -> 3.58 us  [tick(): lax.dynamic_update_slice(finished, jnp.where(live, result, previous), (ze...]
    gather x2 -> x1, local copies, waits for them, and re-layouts: 18.5 us -> 8.15 us  [per_device(): caches = pool[table].at[moving].set(received)]
    unnamed x17 -> x15, local copies, waits for them, and re-layouts: 12.5 us -> 4.43 us
    reduce_sum x11 -> x9, other arithmetic: 12.1 us -> 4.46 us  [layer(): jnp.mean(wide * wide, axis=-1, keepdims=True) + 1e-05]
    squeeze x0 -> x1, local copies, waits for them, and re-layouts: none -> 6.05 us  [per_device(): values = caches[:, :, 1]]
    ppermute x11 -> x9, waiting for transfers between devices: 62.1 us -> 67.7 us  [passed_along(): return lax.ppermute(array, axis, pairs)]
    reshape x0 -> x18, local copies, waits for them, and re-layouts: none -> 5.09 us  [the longest x9 3.25 us: layer(): heads = normed.reshape(steps, reqs, kv_heads, group, head)]
  transfers between devices with their start and end apart: 14 -> 12, of which waited for: 11 -> 9; matrix products, arithmetic and copies ran while one was open for 9% -> 6% of each run, Pallas kernels for 0% -> 0%
where the time goes in v1:
time: 190 us
  waiting for transfers between devices  67.7 us (36%)
  matrix products  40.3 us (21%)
  local copies, waits for them, and re-layouts  40 us (21%)
  starting transfers between devices  20 us (11%)
  other arithmetic  19.4 us (10%)
    ppermute x9, waiting for transfers between devices, passed_along(): return lax.ppermute(array, axis, pairs)  67.7 us
    dot_general x9, matrix products, layer(): jnp.einsum('rjgxd,rjgpd->rjgxp', wide_query, keys, preferred_element_type...  29.2 us
    ppermute x9, starting transfers between devices, passed_along(): return lax.ppermute(array, axis, pairs)  19.4 us
    gather x1, local copies, waits for them, and re-layouts, per_device(): caches = pool[table].at[moving].set(received)  8.15 us
    dot_general x9, matrix products, layer(): jnp.einsum('rjgxp,rjgpd->rjgxd', cache_w, values, preferred_element_type=...  6.32 us
    squeeze x1, local copies, waits for them, and re-layouts, per_device(): values = caches[:, :, 1]  6.05 us
    scatter x1, local copies, waits for them, and re-layouts, per_device(): caches = pool[table].at[moving].set(received)  5.26 us
    reduce_sum x9, other arithmetic, layer(): jnp.mean(wide * wide, axis=-1, keepdims=True) + 1e-05  4.46 us
  transfers between devices with their start and end apart: 12, of which 9 were waited for; matrix products, arithmetic and copies ran while one was open for 6% of the time, Pallas kernels for 0%

profile of v1, /device:TPU:26, one launch (start us, length us, event | category | flops | bytes accessed | tf_op | source)
XLA Modules:
  0.0 189.5 jit_solution(18026638535731386598)
XLA Ops:
  4.2 4.4 %gather_fusion.4 = bf16[4,2,8,128,128]{4,3,2,1,0:T(8,128)(2,1)S(1)} fusion(bf16[16,2,8,128,128]{4,3,2,1,0:T(8,128)(2,1)} %bitcast.67, s32[1024]{0:T(1024)S(1)} %pad_clamp_fusion), kind=kCustom, calls=%fused_computation.4 | custom fusion | bytes 4194320 | tf_op jit(solution)/shard_map/gather | solution.py:86
  12.0 8.1 %gather_fusion.2 = bf16[16,2,8,128,128]{4,3,2,1,0:T(8,128)(2,1)} fusion(bf16[16,2,8,128,128]{4,3,2,1,0:T(8,128)(2,1)} %bitcast.68, s32[1024]{0:T(1024)S(1)} %pad_clamp_fusion.1), kind=kCustom, calls=%fused_computation.2 | custom fusion | bytes 16777280 | tf_op jit(solution)/shard_map/gather | solution.py:92
  21.4 5.3 %scatter_fusion.2 = bf16[8,2,2,8,128,128]{5,4,3,2,1,0:T(8,128)(2,1)} fusion(bf16[8,2,2,8,128,128]{5,4,3,2,1,0:T(8,128)(2,1)} %bitcast.65, s32[2]{0:T(128)S(1)} %fusion.28, bf16[2,2,2,8,128,128]{5,4,3,2,1,0:T(8,128)(2,1)S(1)} %collective-permute-done.3), kind=kCustom, calls=%fused_computation.7 | custom fusion | bytes 6291464 | tf_op jit(solution)/shard_map/scatter | solution.py:92
  26.7 6.0 %slice_bitcast_fusion = (bf16[8,2,8,128,128]{4,3,2,1,0:T(8,128)(2,1)}, bf16[8,2,8,128,128]{4,3,2,1,0:T(8,128)(2,1)}) fusion(bf16[8,2,2,8,128,128]{5,4,3,2,1,0:T(8,128)(2,1)} %scatter_fusion.2), kind=kLoop, calls=%fused_computation.55 | loop fusion | bytes 16777216 | tf_op jit(solution)/shard_map/squeeze | solution.py:96
  32.9 153.3 %while.17 = (s32[]{:T(128)}, bf16[4,4,8192]{2,1,0:T(4,128)(2,1)S(1)}, bf16[4,8,8192]{2,1,0:T(8,128)(2,1)S(1)}, pred[]{:T(512)}, s32[]{:T(128)}, /*index=5*/bf16[...) while((s32[]{:T(128)}, ...), condition=%wide.region_10.11_spmd, body=%wide.region_3.10_spmd.sunk | while | flops 140426912 | bytes 35828884 | solution.py:125
  34.9 3.2 %fusion.52 = (f32[4,8,32]{2,1,0:T(8,128)S(1)}, f32[4,2,8,32,128]{4,3,2,1,0:T(8,128)S(1)}) fusion(bf16[8,2,8,128,128]{4,3,2,1,0:T(8,128)(2,1)} %get-tuple-element.469, s32[]{:T(128)S(6)} %select_n.161, bf16[4,8,32,128]{3,2,1,0:T(8,128)(2,1)S(1)} %bitcast.66, pred[4,2,128]{2,1,0:T(4,128)(4,1)S(1)} %broadcast_compare_fusion.3), kind=kOutput, calls=%fused_computation.70.clone.1 | convolution fusion | flops 67894272 | bytes 3412996 | tf_op jit(solution)/shard_map/while/body/eval_jaxpr/rjgxd,rjgpd->rjgxp/dot_general | solution.py:44
  40.3 3.4 %collective-permute-start = (bf16[4,4,8192]{2,1,0:T(4,128)(2,1)S(1)}, bf16[4,4,8192]{2,1,0:T(4,128)(2,1)S(1)}, u32[]{:S(2)}, u32[]{:S(2)}) collective-permute-start(bf16[4,4,8192]{2,1,0:T(4,128)(2,1)S(1)} %get-tuple-element.426), channel_id=1, source_target_pairs={{0,1},{1,2},{2,3},{3,4},{4,5},{5,6},{6,7},{8,9},{9,10},{10,11},{11... | collective-permute-start | bytes 786440 | tf_op jit(solution)/shard_map/while/body/eval_jaxpr/ppermute | solution.py:24
  43.7 8.1 %collective-permute-done = bf16[4,4,8192]{2,1,0:T(4,128)(2,1)S(1)} collective-permute-done((bf16[4,4,8192]{2,1,0:T(4,128)(2,1)S(1)}, bf16[4,4,8192]{2,1,0:T(4,128)(2,1)S(1)}, u32[]{:S(2)}, u32[]{:S(2)}) %collective-permute-start) | collective-permute-done | bytes 262176 | tf_op jit(solution)/shard_map/while/body/eval_jaxpr/ppermute | solution.py:24
  53.7 3.2 %fusion.52 = (f32[4,8,32]{2,1,0:T(8,128)S(1)}, f32[4,2,8,32,128]{4,3,2,1,0:T(8,128)S(1)}) fusion(bf16[8,2,8,128,128]{4,3,2,1,0:T(8,128)(2,1)} %get-tuple-element.469, s32[]{:T(128)S(6)} %select_n.161, bf16[4,8,32,128]{3,2,1,0:T(8,128)(2,1)S(1)} %bitcast.66, pred[4,2,128]{2,1,0:T(4,128)(4,1)S(1)} %broadcast_compare_fusion.3), kind=kOutput, calls=%fused_computation.70.clone.1 | convolution fusion | flops 67894272 | bytes 3412996 | tf_op jit(solution)/shard_map/while/body/eval_jaxpr/rjgxd,rjgpd->rjgxp/dot_general | solution.py:44
  61.7 8.2 %collective-permute-done = bf16[4,4,8192]{2,1,0:T(4,128)(2,1)S(1)} collective-permute-done((bf16[4,4,8192]{2,1,0:T(4,128)(2,1)S(1)}, bf16[4,4,8192]{2,1,0:T(4,128)(2,1)S(1)}, u32[]{:S(2)}, u32[]{:S(2)}) %collective-permute-start) | collective-permute-done | bytes 262176 | tf_op jit(solution)/shard_map/while/body/eval_jaxpr/ppermute | solution.py:24
  71.9 3.2 %fusion.52 = (f32[4,8,32]{2,1,0:T(8,128)S(1)}, f32[4,2,8,32,128]{4,3,2,1,0:T(8,128)S(1)}) fusion(bf16[8,2,8,128,128]{4,3,2,1,0:T(8,128)(2,1)} %get-tuple-element.469, s32[]{:T(128)S(6)} %select_n.161, bf16[4,8,32,128]{3,2,1,0:T(8,128)(2,1)S(1)} %bitcast.66, pred[4,2,128]{2,1,0:T(4,128)(4,1)S(1)} %broadcast_compare_fusion.3), kind=kOutput, calls=%fused_computation.70.clone.1 | convolution fusion | flops 67894272 | bytes 3412996 | tf_op jit(solution)/shard_map/while/body/eval_jaxpr/rjgxd,rjgpd->rjgxp/dot_general | solution.py:44
  79.2 8.0 %collective-permute-done = bf16[4,4,8192]{2,1,0:T(4,128)(2,1)S(1)} collective-permute-done((bf16[4,4,8192]{2,1,0:T(4,128)(2,1)S(1)}, bf16[4,4,8192]{2,1,0:T(4,128)(2,1)S(1)}, u32[]{:S(2)}, u32[]{:S(2)}) %collective-permute-start) | collective-permute-done | bytes 262176 | tf_op jit(solution)/shard_map/while/body/eval_jaxpr/ppermute | solution.py:24
  89.1 3.2 %fusion.52 = (f32[4,8,32]{2,1,0:T(8,128)S(1)}, f32[4,2,8,32,128]{4,3,2,1,0:T(8,128)S(1)}) fusion(bf16[8,2,8,128,128]{4,3,2,1,0:T(8,128)(2,1)} %get-tuple-element.469, s32[]{:T(128)S(6)} %select_n.161, bf16[4,8,32,128]{3,2,1,0:T(8,128)(2,1)S(1)} %bitcast.66, pred[4,2,128]{2,1,0:T(4,128)(4,1)S(1)} %broadcast_compare_fusion.3), kind=kOutput, calls=%fused_computation.70.clone.1 | convolution fusion | flops 67894272 | bytes 3412996 | tf_op jit(solution)/shard_map/while/body/eval_jaxpr/rjgxd,rjgpd->rjgxp/dot_general | solution.py:44
  96.4 7.2 %collective-permute-done = bf16[4,4,8192]{2,1,0:T(4,128)(2,1)S(1)} collective-permute-done((bf16[4,4,8192]{2,1,0:T(4,128)(2,1)S(1)}, bf16[4,4,8192]{2,1,0:T(4,128)(2,1)S(1)}, u32[]{:S(2)}, u32[]{:S(2)}) %collective-permute-start) | collective-permute-done | bytes 262176 | tf_op jit(solution)/shard_map/while/body/eval_jaxpr/ppermute | solution.py:24
  105.6 3.2 %fusion.52 = (f32[4,8,32]{2,1,0:T(8,128)S(1)}, f32[4,2,8,32,128]{4,3,2,1,0:T(8,128)S(1)}) fusion(bf16[8,2,8,128,128]{4,3,2,1,0:T(8,128)(2,1)} %get-tuple-element.469, s32[]{:T(128)S(6)} %select_n.161, bf16[4,8,32,128]{3,2,1,0:T(8,128)(2,1)S(1)} %bitcast.66, pred[4,2,128]{2,1,0:T(4,128)(4,1)S(1)} %broadcast_compare_fusion.3), kind=kOutput, calls=%fused_computation.70.clone.1 | convolution fusion | flops 67894272 | bytes 3412996 | tf_op jit(solution)/shard_map/while/body/eval_jaxpr/rjgxd,rjgpd->rjgxp/dot_general | solution.py:44
  112.9 7.2 %collective-permute-done = bf16[4,4,8192]{2,1,0:T(4,128)(2,1)S(1)} collective-permute-done((bf16[4,4,8192]{2,1,0:T(4,128)(2,1)S(1)}, bf16[4,4,8192]{2,1,0:T(4,128)(2,1)S(1)}, u32[]{:S(2)}, u32[]{:S(2)}) %collective-permute-start) | collective-permute-done | bytes 262176 | tf_op jit(solution)/shard_map/while/body/eval_jaxpr/ppermute | solution.py:24
  122.1 3.2 %fusion.52 = (f32[4,8,32]{2,1,0:T(8,128)S(1)}, f32[4,2,8,32,128]{4,3,2,1,0:T(8,128)S(1)}) fusion(bf16[8,2,8,128,128]{4,3,2,1,0:T(8,128)(2,1)} %get-tuple-element.469, s32[]{:T(128)S(6)} %select_n.161, bf16[4,8,32,128]{3,2,1,0:T(8,128)(2,1)S(1)} %bitcast.66, pred[4,2,128]{2,1,0:T(4,128)(4,1)S(1)} %broadcast_compare_fusion.3), kind=kOutput, calls=%fused_computation.70.clone.1 | convolution fusion | flops 67894272 | bytes 3412996 | tf_op jit(solution)/shard_map/while/body/eval_jaxpr/rjgxd,rjgpd->rjgxp/dot_general | solution.py:44
  129.4 7.2 %collective-permute-done = bf16[4,4,8192]{2,1,0:T(4,128)(2,1)S(1)} collective-permute-done((bf16[4,4,8192]{2,1,0:T(4,128)(2,1)S(1)}, bf16[4,4,8192]{2,1,0:T(4,128)(2,1)S(1)}, u32[]{:S(2)}, u32[]{:S(2)}) %collective-permute-start) | collective-permute-done | bytes 262176 | tf_op jit(solution)/shard_map/while/body/eval_jaxpr/ppermute | solution.py:24
  138.6 3.2 %fusion.52 = (f32[4,8,32]{2,1,0:T(8,128)S(1)}, f32[4,2,8,32,128]{4,3,2,1,0:T(8,128)S(1)}) fusion(bf16[8,2,8,128,128]{4,3,2,1,0:T(8,128)(2,1)} %get-tuple-element.469, s32[]{:T(128)S(6)} %select_n.161, bf16[4,8,32,128]{3,2,1,0:T(8,128)(2,1)S(1)} %bitcast.66, pred[4,2,128]{2,1,0:T(4,128)(4,1)S(1)} %broadcast_compare_fusion.3), kind=kOutput, calls=%fused_computation.70.clone.1 | convolution fusion | flops 67894272 | bytes 3412996 | tf_op jit(solution)/shard_map/while/body/eval_jaxpr/rjgxd,rjgpd->rjgxp/dot_general | solution.py:44
  145.9 7.2 %collective-permute-done = bf16[4,4,8192]{2,1,0:T(4,128)(2,1)S(1)} collective-permute-done((bf16[4,4,8192]{2,1,0:T(4,128)(2,1)S(1)}, bf16[4,4,8192]{2,1,0:T(4,128)(2,1)S(1)}, u32[]{:S(2)}, u32[]{:S(2)}) %collective-permute-start) | collective-permute-done | bytes 262176 | tf_op jit(solution)/shard_map/while/body/eval_jaxpr/ppermute | solution.py:24
  155.1 3.2 %fusion.52 = (f32[4,8,32]{2,1,0:T(8,128)S(1)}, f32[4,2,8,32,128]{4,3,2,1,0:T(8,128)S(1)}) fusion(bf16[8,2,8,128,128]{4,3,2,1,0:T(8,128)(2,1)} %get-tuple-element.469, s32[]{:T(128)S(6)} %select_n.161, bf16[4,8,32,128]{3,2,1,0:T(8,128)(2,1)S(1)} %bitcast.66, pred[4,2,128]{2,1,0:T(4,128)(4,1)S(1)} %broadcast_compare_fusion.3), kind=kOutput, calls=%fused_computation.70.clone.1 | convolution fusion | flops 67894272 | bytes 3412996 | tf_op jit(solution)/shard_map/while/body/eval_jaxpr/rjgxd,rjgpd->rjgxp/dot_general | solution.py:44
  162.4 7.2 %collective-permute-done = bf16[4,4,8192]{2,1,0:T(4,128)(2,1)S(1)} collective-permute-done((bf16[4,4,8192]{2,1,0:T(4,128)(2,1)S(1)}, bf16[4,4,8192]{2,1,0:T(4,128)(2,1)S(1)}, u32[]{:S(2)}, u32[]{:S(2)}) %collective-permute-start) | collective-permute-done | bytes 262176 | tf_op jit(solution)/shard_map/while/body/eval_jaxpr/ppermute | solution.py:24
  178.9 7.2 %collective-permute-done = bf16[4,4,8192]{2,1,0:T(4,128)(2,1)S(1)} collective-permute-done((bf16[4,4,8192]{2,1,0:T(4,128)(2,1)S(1)}, bf16[4,4,8192]{2,1,0:T(4,128)(2,1)S(1)}, u32[]{:S(2)}, u32[]{:S(2)}) %collective-permute-start) | collective-permute-done | bytes 262176 | tf_op jit(solution)/shard_map/while/body/eval_jaxpr/ppermute | solution.py:24
  186.2 3.3 %copy.107 = bf16[1,1,2,2,2,8,128,128]{7,6,5,4,3,2,1,0:T(8,128)(2,1)} copy(bf16[1,1,2,2,2,8,128,128]{7,6,5,4,3,2,1,0:T(8,128)(2,1)} %bitcast.69) | data formatting | bytes 4194304
  (284 shorter events, 63.1 us)
Async XLA Ops:
  4.2 6.5 %copy-start.5 = (bf16[1,4,8,8192]{3,2,1,0:T(8,128)(2,1)S(1)}, bf16[1,4,8,8192]{3,2,1,0:T(8,128)(2,1)}, u32[]{:S(2)}) copy-start(bf16[1,4,8,8192]{3,2,1,0:T(8,128)(2,1)} %param.9) | copy-start | bytes 1572868
  4.2 7.7 %copy-start.6 = (s32[1,8,2]{1,2,0:T(2,128)S(1)}, s32[1,8,2]{1,2,0:T(2,128)}, u32[]{:S(2)}) copy-start(s32[1,8,2]{1,2,0:T(2,128)} %param.11) | copy-start | bytes 196
  10.1 11.3 %collective-permute-start.3 = (bf16[2,2,2,8,128,128]{5,4,3,2,1,0:T(8,128)(2,1)}, bf16[2,2,2,8,128,128]{5,4,3,2,1,0:T(8,128)(2,1)S(1)}, u32[]{:S(2)}, u32[]{:S(2)}) collective-permute-start(bf16[2,2,2,8,128,128]{5,4,3,2,1,0:T(8,128)(2,1)} %broadcast_select_fusion), channel_id=1, source_target_pairs={{0,8},{8,0},{1,9},{9,1},{2,10},{10,2},{3,11},{11,3},{4,12},{12,4},... | collective-permute-start | bytes 6291464 | tf_op jit(solution)/shard_map/ppermute | solution.py:18
  10.1 10.0 %collective-permute-start.2 = (s32[2]{0:T(128)S(1)}, s32[2]{0:T(128)S(1)}, u32[]{:S(2)}, u32[]{:S(2)}) collective-permute-start(s32[2]{0:T(128)S(1)} %gather_fusion.1), channel_id=1, source_target_pairs={{0,8},{8,0},{1,9},{9,1},{2,10},{10,2},{3,11},{11,3},{4,12},{12,4},... | collective-permute-start | bytes 32 | tf_op jit(solution)/shard_map/ppermute | solution.py:18
  11.7 9.0 %collective-permute-start.1 = (bf16[4,2,8192]{2,0,1:T(4,128)(2,1)S(1)}, bf16[4,2,8192]{2,0,1:T(4,128)(2,1)S(1)}, u32[]{:S(2)}, u32[]{:S(2)}) collective-permute-start(bf16[4,2,8192]{2,0,1:T(4,128)(2,1)S(1)} %bitcast.77), channel_id=1, source_target_pairs={{0,8},{8,0},{1,9},{9,1},{2,10},{10,2},{3,11},{11,3},{4,12},{12,4},... | collective-permute-start | bytes 393224 | tf_op jit(solution)/shard_map/ppermute | solution.py:18
  21.4 11.3 %copy-start = (bf16[2,2,2,8,128,128]{5,4,3,2,1,0:T(8,128)(2,1)}, bf16[2,2,2,8,128,128]{5,4,3,2,1,0:T(8,128)(2,1)S(1)}, u32[]{:S(2)}) copy-start(bf16[2,2,2,8,128,128]{5,4,3,2,1,0:T(8,128)(2,1)S(1)} %collective-permute-done.3) | copy-start | bytes 6291460
  26.7 6.2 %copy-start.3 = (f32[1,8192]{1,0:T(1,128)S(1)}, f32[1,8192]{1,0:T(1,128)}, u32[]{:S(2)}) copy-start(f32[1,8192]{1,0:T(1,128)} %param.15) | copy-start | bytes 98308
  26.7 6.2 %copy-start.4 = (f32[1,8192]{1,0:T(1,128)S(1)}, f32[1,8192]{1,0:T(1,128)}, u32[]{:S(2)}) copy-start(f32[1,8192]{1,0:T(1,128)} %param.14) | copy-start | bytes 98308
  40.3 11.5 %collective-permute-start = (bf16[4,4,8192]{2,1,0:T(4,128)(2,1)S(1)}, bf16[4,4,8192]{2,1,0:T(4,128)(2,1)S(1)}, u32[]{:S(2)}, u32[]{:S(2)}) collective-permute-start(bf16[4,4,8192]{2,1,0:T(4,128)(2,1)S(1)} %get-tuple-element.426), channel_id=1, source_target_pairs={{0,1},{1,2},{2,3},{3,4},{4,5},{5,6},{6,7},{8,9},{9,10},{10,11},{11... | collective-permute-start | bytes 786440 | tf_op jit(solution)/shard_map/while/body/eval_jaxpr/ppermute | solution.py:24
  53.0 4.5 %copy-start.2 = (bf16[8,2,8,128,128]{4,3,2,1,0:T(8,128)(2,1)S(1)}, bf16[8,2,8,128,128]{4,3,2,1,0:T(8,128)(2,1)}, u32[]{:S(2)}) copy-start(bf16[8,2,8,128,128]{4,3,2,1,0:T(8,128)(2,1)} %get-tuple-element.470) | copy-start | bytes 12582916 | tf_op jit(solution)/shard_map/while
  59.2 10.8 %collective-permute-start = (bf16[4,4,8192]{2,1,0:T(4,128)(2,1)S(1)}, bf16[4,4,8192]{2,1,0:T(4,128)(2,1)S(1)}, u32[]{:S(2)}, u32[]{:S(2)}) collective-permute-start(bf16[4,4,8192]{2,1,0:T(4,128)(2,1)S(1)} %get-tuple-element.426), channel_id=1, source_target_pairs={{0,1},{1,2},{2,3},{3,4},{4,5},{5,6},{6,7},{8,9},{9,10},{10,11},{11... | collective-permute-start | bytes 786440 | tf_op jit(solution)/shard_map/while/body/eval_jaxpr/ppermute | solution.py:24
  71.1 4.5 %copy-start.2 = (bf16[8,2,8,128,128]{4,3,2,1,0:T(8,128)(2,1)S(1)}, bf16[8,2,8,128,128]{4,3,2,1,0:T(8,128)(2,1)}, u32[]{:S(2)}) copy-start(bf16[8,2,8,128,128]{4,3,2,1,0:T(8,128)(2,1)} %get-tuple-element.470) | copy-start | bytes 12582916 | tf_op jit(solution)/shard_map/while
  77.3 9.9 %collective-permute-start = (bf16[4,4,8192]{2,1,0:T(4,128)(2,1)S(1)}, bf16[4,4,8192]{2,1,0:T(4,128)(2,1)S(1)}, u32[]{:S(2)}, u32[]{:S(2)}) collective-permute-start(bf16[4,4,8192]{2,1,0:T(4,128)(2,1)S(1)} %get-tuple-element.426), channel_id=1, source_target_pairs={{0,1},{1,2},{2,3},{3,4},{4,5},{5,6},{6,7},{8,9},{9,10},{10,11},{11... | collective-permute-start | bytes 786440 | tf_op jit(solution)/shard_map/while/body/eval_jaxpr/ppermute | solution.py:24
  94.5 9.2 %collective-permute-start = (bf16[4,4,8192]{2,1,0:T(4,128)(2,1)S(1)}, bf16[4,4,8192]{2,1,0:T(4,128)(2,1)S(1)}, u32[]{:S(2)}, u32[]{:S(2)}) collective-permute-start(bf16[4,4,8192]{2,1,0:T(4,128)(2,1)S(1)} %get-tuple-element.426), channel_id=1, source_target_pairs={{0,1},{1,2},{2,3},{3,4},{4,5},{5,6},{6,7},{8,9},{9,10},{10,11},{11... | collective-permute-start | bytes 786440 | tf_op jit(solution)/shard_map/while/body/eval_jaxpr/ppermute | solution.py:24
  104.8 4.5 %copy-start.2 = (bf16[8,2,8,128,128]{4,3,2,1,0:T(8,128)(2,1)S(1)}, bf16[8,2,8,128,128]{4,3,2,1,0:T(8,128)(2,1)}, u32[]{:S(2)}) copy-start(bf16[8,2,8,128,128]{4,3,2,1,0:T(8,128)(2,1)} %get-tuple-element.470) | copy-start | bytes 12582916 | tf_op jit(solution)/shard_map/while
  111.0 9.2 %collective-permute-start = (bf16[4,4,8192]{2,1,0:T(4,128)(2,1)S(1)}, bf16[4,4,8192]{2,1,0:T(4,128)(2,1)S(1)}, u32[]{:S(2)}, u32[]{:S(2)}) collective-permute-start(bf16[4,4,8192]{2,1,0:T(4,128)(2,1)S(1)} %get-tuple-element.426), channel_id=1, source_target_pairs={{0,1},{1,2},{2,3},{3,4},{4,5},{5,6},{6,7},{8,9},{9,10},{10,11},{11... | collective-permute-start | bytes 786440 | tf_op jit(solution)/shard_map/while/body/eval_jaxpr/ppermute | solution.py:24
  121.3 4.5 %copy-start.2 = (bf16[8,2,8,128,128]{4,3,2,1,0:T(8,128)(2,1)S(1)}, bf16[8,2,8,128,128]{4,3,2,1,0:T(8,128)(2,1)}, u32[]{:S(2)}) copy-start(bf16[8,2,8,128,128]{4,3,2,1,0:T(8,128)(2,1)} %get-tuple-element.470) | copy-start | bytes 12582916 | tf_op jit(solution)/shard_map/while
  127.5 9.2 %collective-permute-start = (bf16[4,4,8192]{2,1,0:T(4,128)(2,1)S(1)}, bf16[4,4,8192]{2,1,0:T(4,128)(2,1)S(1)}, u32[]{:S(2)}, u32[]{:S(2)}) collective-permute-start(bf16[4,4,8192]{2,1,0:T(4,128)(2,1)S(1)} %get-tuple-element.426), channel_id=1, source_target_pairs={{0,1},{1,2},{2,3},{3,4},{4,5},{5,6},{6,7},{8,9},{9,10},{10,11},{11... | collective-permute-start | bytes 786440 | tf_op jit(solution)/shard_map/while/body/eval_jaxpr/ppermute | solution.py:24
  137.8 4.5 %copy-start.2 = (bf16[8,2,8,128,128]{4,3,2,1,0:T(8,128)(2,1)S(1)}, bf16[8,2,8,128,128]{4,3,2,1,0:T(8,128)(2,1)}, u32[]{:S(2)}) copy-start(bf16[8,2,8,128,128]{4,3,2,1,0:T(8,128)(2,1)} %get-tuple-element.470) | copy-start | bytes 12582916 | tf_op jit(solution)/shard_map/while
  144.0 9.2 %collective-permute-start = (bf16[4,4,8192]{2,1,0:T(4,128)(2,1)S(1)}, bf16[4,4,8192]{2,1,0:T(4,128)(2,1)S(1)}, u32[]{:S(2)}, u32[]{:S(2)}) collective-permute-start(bf16[4,4,8192]{2,1,0:T(4,128)(2,1)S(1)} %get-tuple-element.426), channel_id=1, source_target_pairs={{0,1},{1,2},{2,3},{3,4},{4,5},{5,6},{6,7},{8,9},{9,10},{10,11},{11... | collective-permute-start | bytes 786440 | tf_op jit(solution)/shard_map/while/body/eval_jaxpr/ppermute | solution.py:24
  154.3 4.5 %copy-start.2 = (bf16[8,2,8,128,128]{4,3,2,1,0:T(8,128)(2,1)S(1)}, bf16[8,2,8,128,128]{4,3,2,1,0:T(8,128)(2,1)}, u32[]{:S(2)}) copy-start(bf16[8,2,8,128,128]{4,3,2,1,0:T(8,128)(2,1)} %get-tuple-element.470) | copy-start | bytes 12582916 | tf_op jit(solution)/shard_map/while
  160.5 9.2 %collective-permute-start = (bf16[4,4,8192]{2,1,0:T(4,128)(2,1)S(1)}, bf16[4,4,8192]{2,1,0:T(4,128)(2,1)S(1)}, u32[]{:S(2)}, u32[]{:S(2)}) collective-permute-start(bf16[4,4,8192]{2,1,0:T(4,128)(2,1)S(1)} %get-tuple-element.426), channel_id=1, source_target_pairs={{0,1},{1,2},{2,3},{3,4},{4,5},{5,6},{6,7},{8,9},{9,10},{10,11},{11... | collective-permute-start | bytes 786440 | tf_op jit(solution)/shard_map/while/body/eval_jaxpr/ppermute | solution.py:24
  170.8 4.5 %copy-start.2 = (bf16[8,2,8,128,128]{4,3,2,1,0:T(8,128)(2,1)S(1)}, bf16[8,2,8,128,128]{4,3,2,1,0:T(8,128)(2,1)}, u32[]{:S(2)}) copy-start(bf16[8,2,8,128,128]{4,3,2,1,0:T(8,128)(2,1)} %get-tuple-element.470) | copy-start | bytes 12582916 | tf_op jit(solution)/shard_map/while
  177.0 9.2 %collective-permute-start = (bf16[4,4,8192]{2,1,0:T(4,128)(2,1)S(1)}, bf16[4,4,8192]{2,1,0:T(4,128)(2,1)S(1)}, u32[]{:S(2)}, u32[]{:S(2)}) collective-permute-start(bf16[4,4,8192]{2,1,0:T(4,128)(2,1)S(1)} %get-tuple-element.426), channel_id=1, source_target_pairs={{0,1},{1,2},{2,3},{3,4},{4,5},{5,6},{6,7},{8,9},{9,10},{10,11},{11... | collective-permute-start | bytes 786440 | tf_op jit(solution)/shard_map/while/body/eval_jaxpr/ppermute | solution.py:24
  (3 other events, 12.3 us)

commit v2 on v1

--- a/solution.py
+++ b/solution.py
@@ -5,7 +5,7 @@
 from jax import lax
 from jax.sharding import PartitionSpec as P
 
-CHUNKS = 2
+CHUNKS = 4
 
 
 def partner(block, axis, stride):

time: 190 us -> 208 us (1.095)
  other arithmetic: 19.4 us -> 36.7 us
  waiting for transfers between devices: 67.7 us -> 63.1 us
  starting transfers between devices: 20 us -> 23.7 us
  matrix products: 40.3 us -> 43.7 us
  local copies, waits for them, and re-layouts: 40 us -> 37 us
    dynamic_update_slice x9 -> x11, other arithmetic: 3.58 us -> 22.3 us  [tick(): lax.dynamic_update_slice(finished, jnp.where(live, result, previous), (ze...]
    dot_general x9 -> x11, matrix products: 6.32 us -> 17.3 us  [layer(): jnp.einsum('rjgxp,rjgpd->rjgxd', cache_w, values, preferred_element_type=...]
    dot_general x9 -> x11, matrix products: 29.2 us -> 21.6 us  [layer(): jnp.einsum('rjgxd,rjgpd->rjgxp', wide_query, keys, preferred_element_type...]
    ppermute x9 -> x11, waiting for transfers between devices: 67.7 us -> 63.1 us  [passed_along(): return lax.ppermute(array, axis, pairs)]
    ppermute x9 -> x11, starting transfers between devices: 19.4 us -> 23.1 us  [passed_along(): return lax.ppermute(array, axis, pairs)]
    unnamed x15 -> x11, local copies, waits for them, and re-layouts: 4.43 us -> 2.4 us
    reduce_sum x9 -> x11, other arithmetic: 4.46 us -> 3.76 us  [layer(): jnp.mean(wide * wide, axis=-1, keepdims=True) + 1e-05]
  transfers between devices with their start and end apart: 12 -> 14, of which waited for: 9 -> 11; matrix products, arithmetic and copies ran while one was open for 6% -> 5% of each run, Pallas kernels for 0% -> 0%
where the time goes in v2:
time: 208 us; the launch traced here: 207 us
  waiting for transfers between devices  63.1 us (30%)
  matrix products  43.7 us (21%)
  local copies, waits for them, and re-layouts  37 us (18%)
  other arithmetic  36.7 us (18%)
  starting transfers between devices  23.7 us (11%)
    ppermute x11, waiting for transfers between devices, passed_along(): return lax.ppermute(array, axis, pairs)  63.1 us
    ppermute x11, starting transfers between devices, passed_along(): return lax.ppermute(array, axis, pairs)  23.1 us
    dynamic_update_slice x11, other arithmetic, tick(): lax.dynamic_update_slice(finished, jnp.where(live, result, previous), (ze...  22.3 us
    dot_general x11, matrix products, layer(): jnp.einsum('rjgxd,rjgpd->rjgxp', wide_query, keys, preferred_element_type...  21.6 us
    dot_general x11, matrix products, layer(): jnp.einsum('rjgxp,rjgpd->rjgxd', cache_w, values, preferred_element_type=...  17.3 us
    gather x1, local copies, waits for them, and re-layouts, per_device(): caches = pool[table].at[moving].set(received)  8.15 us
    squeeze x1, local copies, waits for them, and re-layouts, per_device(): values = caches[:, :, 1]  6.05 us
    scatter x1, local copies, waits for them, and re-layouts, per_device(): caches = pool[table].at[moving].set(received)  5.1 us
  transfers between devices with their start and end apart: 14, of which 11 were waited for; matrix products, arithmetic and copies ran while one was open for 5% of the time, Pallas kernels for 0%

profile of v2, /device:TPU:26, one launch (start us, length us, event | category | flops | bytes accessed | tf_op | source)
XLA Modules:
  0.0 206.6 jit_solution(4995173433618579502)
XLA Ops:
  4.2 4.4 %gather_fusion.4 = bf16[4,2,8,128,128]{4,3,2,1,0:T(8,128)(2,1)S(1)} fusion(bf16[16,2,8,128,128]{4,3,2,1,0:T(8,128)(2,1)} %bitcast.66, s32[1024]{0:T(1024)S(1)} %pad_clamp_fusion), kind=kCustom, calls=%fused_computation.4 | custom fusion | bytes 4194320 | tf_op jit(solution)/shard_map/gather | solution.py:86
  12.0 8.1 %gather_fusion.2 = bf16[16,2,8,128,128]{4,3,2,1,0:T(8,128)(2,1)} fusion(bf16[16,2,8,128,128]{4,3,2,1,0:T(8,128)(2,1)} %bitcast.67, s32[1024]{0:T(1024)S(1)} %pad_clamp_fusion.1), kind=kCustom, calls=%fused_computation.2 | custom fusion | bytes 16777280 | tf_op jit(solution)/shard_map/gather | solution.py:92
  21.4 5.1 %scatter_fusion.2 = bf16[8,2,2,8,128,128]{5,4,3,2,1,0:T(8,128)(2,1)} fusion(bf16[8,2,2,8,128,128]{5,4,3,2,1,0:T(8,128)(2,1)} %bitcast.65, s32[2]{0:T(128)S(1)} %fusion.19, bf16[2,2,2,8,128,128]{5,4,3,2,1,0:T(8,128)(2,1)S(1)} %collective-permute-done.3), kind=kCustom, calls=%fused_computation.7 | custom fusion | bytes 6291464 | tf_op jit(solution)/shard_map/scatter | solution.py:92
  26.5 6.0 %slice_bitcast_fusion = (bf16[8,2,8,128,128]{4,3,2,1,0:T(8,128)(2,1)}, bf16[8,2,8,128,128]{4,3,2,1,0:T(8,128)(2,1)}) fusion(bf16[8,2,2,8,128,128]{5,4,3,2,1,0:T(8,128)(2,1)} %scatter_fusion.2), kind=kLoop, calls=%fused_computation.54 | loop fusion | bytes 16777216 | tf_op jit(solution)/shard_map/squeeze | solution.py:96
  33.5 171.7 %while.17 = (s32[]{:T(128)}, bf16[4,2,8192]{2,1,0:T(2,128)(2,1)S(1)}, bf16[4,8,8192]{2,1,0:T(8,128)(2,1)}, pred[]{:T(512)}, s32[]{:T(128)}, /*index=5*/bf16[4,8,...) while((s32[]{:T(128)}, ...), condition=%wide.region_10.11_spmd, body=%wide.region_3.10_spmd.sunk | while | flops 70213776 | bytes 9547754 | solution.py:125
  39.3 2.0 fusion.49
  41.3 3.4 %collective-permute-start = (bf16[4,2,8192]{2,1,0:T(2,128)(2,1)S(1)}, bf16[4,2,8192]{2,1,0:T(2,128)(2,1)S(1)}, u32[]{:S(2)}, u32[]{:S(2)}) collective-permute-start(bf16[4,2,8192]{2,1,0:T(2,128)(2,1)S(1)} %get-tuple-element.426), channel_id=1, source_target_pairs={{0,1},{1,2},{2,3},{3,4},{4,5},{5,6},{6,7},{8,9},{9,10},{10,11},{11... | collective-permute-start | bytes 393224 | tf_op jit(solution)/shard_map/while/body/eval_jaxpr/ppermute | solution.py:24
  44.8 5.3 %collective-permute-done = bf16[4,2,8192]{2,1,0:T(2,128)(2,1)S(1)} collective-permute-done((bf16[4,2,8192]{2,1,0:T(2,128)(2,1)S(1)}, bf16[4,2,8192]{2,1,0:T(2,128)(2,1)S(1)}, u32[]{:S(2)}, u32[]{:S(2)}) %collective-permute-start) | collective-permute-done | bytes 131104 | tf_op jit(solution)/shard_map/while/body/eval_jaxpr/ppermute | solution.py:24
  55.8 2.0 fusion.49
  57.8 2.5 %collective-permute-start = (bf16[4,2,8192]{2,1,0:T(2,128)(2,1)S(1)}, bf16[4,2,8192]{2,1,0:T(2,128)(2,1)S(1)}, u32[]{:S(2)}, u32[]{:S(2)}) collective-permute-start(bf16[4,2,8192]{2,1,0:T(2,128)(2,1)S(1)} %get-tuple-element.426), channel_id=1, source_target_pairs={{0,1},{1,2},{2,3},{3,4},{4,5},{5,6},{6,7},{8,9},{9,10},{10,11},{11... | collective-permute-start | bytes 393224 | tf_op jit(solution)/shard_map/while/body/eval_jaxpr/ppermute | solution.py:24
  60.3 5.4 %collective-permute-done = bf16[4,2,8192]{2,1,0:T(2,128)(2,1)S(1)} collective-permute-done((bf16[4,2,8192]{2,1,0:T(2,128)(2,1)S(1)}, bf16[4,2,8192]{2,1,0:T(2,128)(2,1)S(1)}, u32[]{:S(2)}, u32[]{:S(2)}) %collective-permute-start) | collective-permute-done | bytes 131104 | tf_op jit(solution)/shard_map/while/body/eval_jaxpr/ppermute | solution.py:24
  71.4 2.0 fusion.49
  75.4 5.8 %collective-permute-done = bf16[4,2,8192]{2,1,0:T(2,128)(2,1)S(1)} collective-permute-done((bf16[4,2,8192]{2,1,0:T(2,128)(2,1)S(1)}, bf16[4,2,8192]{2,1,0:T(2,128)(2,1)S(1)}, u32[]{:S(2)}, u32[]{:S(2)}) %collective-permute-start) | collective-permute-done | bytes 131104 | tf_op jit(solution)/shard_map/while/body/eval_jaxpr/ppermute | solution.py:24
  86.9 2.0 fusion.49
  90.9 5.8 %collective-permute-done = bf16[4,2,8192]{2,1,0:T(2,128)(2,1)S(1)} collective-permute-done((bf16[4,2,8192]{2,1,0:T(2,128)(2,1)S(1)}, bf16[4,2,8192]{2,1,0:T(2,128)(2,1)S(1)}, u32[]{:S(2)}, u32[]{:S(2)}) %collective-permute-start) | collective-permute-done | bytes 131104 | tf_op jit(solution)/shard_map/while/body/eval_jaxpr/ppermute | solution.py:24
  102.4 2.0 fusion.49
  106.4 5.8 %collective-permute-done = bf16[4,2,8192]{2,1,0:T(2,128)(2,1)S(1)} collective-permute-done((bf16[4,2,8192]{2,1,0:T(2,128)(2,1)S(1)}, bf16[4,2,8192]{2,1,0:T(2,128)(2,1)S(1)}, u32[]{:S(2)}, u32[]{:S(2)}) %collective-permute-start) | collective-permute-done | bytes 131104 | tf_op jit(solution)/shard_map/while/body/eval_jaxpr/ppermute | solution.py:24
  121.9 5.8 %collective-permute-done = bf16[4,2,8192]{2,1,0:T(2,128)(2,1)S(1)} collective-permute-done((bf16[4,2,8192]{2,1,0:T(2,128)(2,1)S(1)}, bf16[4,2,8192]{2,1,0:T(2,128)(2,1)S(1)}, u32[]{:S(2)}, u32[]{:S(2)}) %collective-permute-start) | collective-permute-done | bytes 131104 | tf_op jit(solution)/shard_map/while/body/eval_jaxpr/ppermute | solution.py:24
  137.4 5.8 %collective-permute-done = bf16[4,2,8192]{2,1,0:T(2,128)(2,1)S(1)} collective-permute-done((bf16[4,2,8192]{2,1,0:T(2,128)(2,1)S(1)}, bf16[4,2,8192]{2,1,0:T(2,128)(2,1)S(1)}, u32[]{:S(2)}, u32[]{:S(2)}) %collective-permute-start) | collective-permute-done | bytes 131104 | tf_op jit(solution)/shard_map/while/body/eval_jaxpr/ppermute | solution.py:24
  148.9 2.0 fusion.49
  152.9 5.8 %collective-permute-done = bf16[4,2,8192]{2,1,0:T(2,128)(2,1)S(1)} collective-permute-done((bf16[4,2,8192]{2,1,0:T(2,128)(2,1)S(1)}, bf16[4,2,8192]{2,1,0:T(2,128)(2,1)S(1)}, u32[]{:S(2)}, u32[]{:S(2)}) %collective-permute-start) | collective-permute-done | bytes 131104 | tf_op jit(solution)/shard_map/while/body/eval_jaxpr/ppermute | solution.py:24
  168.4 5.8 %collective-permute-done = bf16[4,2,8192]{2,1,0:T(2,128)(2,1)S(1)} collective-permute-done((bf16[4,2,8192]{2,1,0:T(2,128)(2,1)S(1)}, bf16[4,2,8192]{2,1,0:T(2,128)(2,1)S(1)}, u32[]{:S(2)}, u32[]{:S(2)}) %collective-permute-start) | collective-permute-done | bytes 131104 | tf_op jit(solution)/shard_map/while/body/eval_jaxpr/ppermute | solution.py:24
  183.9 5.8 %collective-permute-done = bf16[4,2,8192]{2,1,0:T(2,128)(2,1)S(1)} collective-permute-done((bf16[4,2,8192]{2,1,0:T(2,128)(2,1)S(1)}, bf16[4,2,8192]{2,1,0:T(2,128)(2,1)S(1)}, u32[]{:S(2)}, u32[]{:S(2)}) %collective-permute-start) | collective-permute-done | bytes 131104 | tf_op jit(solution)/shard_map/while/body/eval_jaxpr/ppermute | solution.py:24
  199.4 5.8 %collective-permute-done = bf16[4,2,8192]{2,1,0:T(2,128)(2,1)S(1)} collective-permute-done((bf16[4,2,8192]{2,1,0:T(2,128)(2,1)S(1)}, bf16[4,2,8192]{2,1,0:T(2,128)(2,1)S(1)}, u32[]{:S(2)}, u32[]{:S(2)}) %collective-permute-start) | collective-permute-done | bytes 131104 | tf_op jit(solution)/shard_map/while/body/eval_jaxpr/ppermute | solution.py:24
  (316 shorter events, 99.3 us)
Async XLA Ops:
  4.2 6.5 %copy-start.2 = (bf16[1,4,8,8192]{3,2,1,0:T(8,128)(2,1)S(1)}, bf16[1,4,8,8192]{3,2,1,0:T(8,128)(2,1)}, u32[]{:S(2)}) copy-start(bf16[1,4,8,8192]{3,2,1,0:T(8,128)(2,1)} %param.9) | copy-start | bytes 1572868
  4.2 7.7 %copy-start.3 = (s32[1,8,2]{1,2,0:T(2,128)S(1)}, s32[1,8,2]{1,2,0:T(2,128)}, u32[]{:S(2)}) copy-start(s32[1,8,2]{1,2,0:T(2,128)} %param.11) | copy-start | bytes 196
  10.2 11.3 %collective-permute-start.3 = (bf16[2,2,2,8,128,128]{5,4,3,2,1,0:T(8,128)(2,1)}, bf16[2,2,2,8,128,128]{5,4,3,2,1,0:T(8,128)(2,1)S(1)}, u32[]{:S(2)}, u32[]{:S(2)}) collective-permute-start(bf16[2,2,2,8,128,128]{5,4,3,2,1,0:T(8,128)(2,1)} %broadcast_select_fusion.2), channel_id=1, source_target_pairs={{0,8},{8,0},{1,9},{9,1},{2,10},{10,2},{3,11},{11,3},{4,12},{12,4},... | collective-permute-start | bytes 6291464 | tf_op jit(solution)/shard_map/ppermute | solution.py:18
  10.2 10.0 %collective-permute-start.2 = (s32[2]{0:T(128)S(1)}, s32[2]{0:T(128)S(1)}, u32[]{:S(2)}, u32[]{:S(2)}) collective-permute-start(s32[2]{0:T(128)S(1)} %gather_fusion.1), channel_id=1, source_target_pairs={{0,8},{8,0},{1,9},{9,1},{2,10},{10,2},{3,11},{11,3},{4,12},{12,4},... | collective-permute-start | bytes 32 | tf_op jit(solution)/shard_map/ppermute | solution.py:18
  11.8 9.0 %collective-permute-start.1 = (bf16[4,2,8192]{2,0,1:T(4,128)(2,1)S(1)}, bf16[4,2,8192]{2,0,1:T(4,128)(2,1)S(1)}, u32[]{:S(2)}, u32[]{:S(2)}) collective-permute-start(bf16[4,2,8192]{2,0,1:T(4,128)(2,1)S(1)} %bitcast.77), channel_id=1, source_target_pairs={{0,8},{8,0},{1,9},{9,1},{2,10},{10,2},{3,11},{11,3},{4,12},{12,4},... | collective-permute-start | bytes 393224 | tf_op jit(solution)/shard_map/ppermute | solution.py:18
  26.5 7.0 %copy-start = (f32[1,8192]{1,0:T(1,128)S(1)}, f32[1,8192]{1,0:T(1,128)}, u32[]{:S(2)}) copy-start(f32[1,8192]{1,0:T(1,128)} %param.15) | copy-start | bytes 98308
  26.5 7.0 %copy-start.1 = (f32[1,8192]{1,0:T(1,128)S(1)}, f32[1,8192]{1,0:T(1,128)}, u32[]{:S(2)}) copy-start(f32[1,8192]{1,0:T(1,128)} %param.14) | copy-start | bytes 98308
  41.3 8.7 %collective-permute-start = (bf16[4,2,8192]{2,1,0:T(2,128)(2,1)S(1)}, bf16[4,2,8192]{2,1,0:T(2,128)(2,1)S(1)}, u32[]{:S(2)}, u32[]{:S(2)}) collective-permute-start(bf16[4,2,8192]{2,1,0:T(2,128)(2,1)S(1)} %get-tuple-element.426), channel_id=1, source_target_pairs={{0,1},{1,2},{2,3},{3,4},{4,5},{5,6},{6,7},{8,9},{9,10},{10,11},{11... | collective-permute-start | bytes 393224 | tf_op jit(solution)/shard_map/while/body/eval_jaxpr/ppermute | solution.py:24
  57.8 7.9 %collective-permute-start = (bf16[4,2,8192]{2,1,0:T(2,128)(2,1)S(1)}, bf16[4,2,8192]{2,1,0:T(2,128)(2,1)S(1)}, u32[]{:S(2)}, u32[]{:S(2)}) collective-permute-start(bf16[4,2,8192]{2,1,0:T(2,128)(2,1)S(1)} %get-tuple-element.426), channel_id=1, source_target_pairs={{0,1},{1,2},{2,3},{3,4},{4,5},{5,6},{6,7},{8,9},{9,10},{10,11},{11... | collective-permute-start | bytes 393224 | tf_op jit(solution)/shard_map/while/body/eval_jaxpr/ppermute | solution.py:24
  73.4 7.7 %collective-permute-start = (bf16[4,2,8192]{2,1,0:T(2,128)(2,1)S(1)}, bf16[4,2,8192]{2,1,0:T(2,128)(2,1)S(1)}, u32[]{:S(2)}, u32[]{:S(2)}) collective-permute-start(bf16[4,2,8192]{2,1,0:T(2,128)(2,1)S(1)} %get-tuple-element.426), channel_id=1, source_target_pairs={{0,1},{1,2},{2,3},{3,4},{4,5},{5,6},{6,7},{8,9},{9,10},{10,11},{11... | collective-permute-start | bytes 393224 | tf_op jit(solution)/shard_map/while/body/eval_jaxpr/ppermute | solution.py:24
  89.0 7.7 %collective-permute-start = (bf16[4,2,8192]{2,1,0:T(2,128)(2,1)S(1)}, bf16[4,2,8192]{2,1,0:T(2,128)(2,1)S(1)}, u32[]{:S(2)}, u32[]{:S(2)}) collective-permute-start(bf16[4,2,8192]{2,1,0:T(2,128)(2,1)S(1)} %get-tuple-element.426), channel_id=1, source_target_pairs={{0,1},{1,2},{2,3},{3,4},{4,5},{5,6},{6,7},{8,9},{9,10},{10,11},{11... | collective-permute-start | bytes 393224 | tf_op jit(solution)/shard_map/while/body/eval_jaxpr/ppermute | solution.py:24
  104.5 7.7 %collective-permute-start = (bf16[4,2,8192]{2,1,0:T(2,128)(2,1)S(1)}, bf16[4,2,8192]{2,1,0:T(2,128)(2,1)S(1)}, u32[]{:S(2)}, u32[]{:S(2)}) collective-permute-start(bf16[4,2,8192]{2,1,0:T(2,128)(2,1)S(1)} %get-tuple-element.426), channel_id=1, source_target_pairs={{0,1},{1,2},{2,3},{3,4},{4,5},{5,6},{6,7},{8,9},{9,10},{10,11},{11... | collective-permute-start | bytes 393224 | tf_op jit(solution)/shard_map/while/body/eval_jaxpr/ppermute | solution.py:24
  120.0 7.7 %collective-permute-start = (bf16[4,2,8192]{2,1,0:T(2,128)(2,1)S(1)}, bf16[4,2,8192]{2,1,0:T(2,128)(2,1)S(1)}, u32[]{:S(2)}, u32[]{:S(2)}) collective-permute-start(bf16[4,2,8192]{2,1,0:T(2,128)(2,1)S(1)} %get-tuple-element.426), channel_id=1, source_target_pairs={{0,1},{1,2},{2,3},{3,4},{4,5},{5,6},{6,7},{8,9},{9,10},{10,11},{11... | collective-permute-start | bytes 393224 | tf_op jit(solution)/shard_map/while/body/eval_jaxpr/ppermute | solution.py:24
  135.5 7.7 %collective-permute-start = (bf16[4,2,8192]{2,1,0:T(2,128)(2,1)S(1)}, bf16[4,2,8192]{2,1,0:T(2,128)(2,1)S(1)}, u32[]{:S(2)}, u32[]{:S(2)}) collective-permute-start(bf16[4,2,8192]{2,1,0:T(2,128)(2,1)S(1)} %get-tuple-element.426), channel_id=1, source_target_pairs={{0,1},{1,2},{2,3},{3,4},{4,5},{5,6},{6,7},{8,9},{9,10},{10,11},{11... | collective-permute-start | bytes 393224 | tf_op jit(solution)/shard_map/while/body/eval_jaxpr/ppermute | solution.py:24
  151.0 7.7 %collective-permute-start = (bf16[4,2,8192]{2,1,0:T(2,128)(2,1)S(1)}, bf16[4,2,8192]{2,1,0:T(2,128)(2,1)S(1)}, u32[]{:S(2)}, u32[]{:S(2)}) collective-permute-start(bf16[4,2,8192]{2,1,0:T(2,128)(2,1)S(1)} %get-tuple-element.426), channel_id=1, source_target_pairs={{0,1},{1,2},{2,3},{3,4},{4,5},{5,6},{6,7},{8,9},{9,10},{10,11},{11... | collective-permute-start | bytes 393224 | tf_op jit(solution)/shard_map/while/body/eval_jaxpr/ppermute | solution.py:24
  166.5 7.7 %collective-permute-start = (bf16[4,2,8192]{2,1,0:T(2,128)(2,1)S(1)}, bf16[4,2,8192]{2,1,0:T(2,128)(2,1)S(1)}, u32[]{:S(2)}, u32[]{:S(2)}) collective-permute-start(bf16[4,2,8192]{2,1,0:T(2,128)(2,1)S(1)} %get-tuple-element.426), channel_id=1, source_target_pairs={{0,1},{1,2},{2,3},{3,4},{4,5},{5,6},{6,7},{8,9},{9,10},{10,11},{11... | collective-permute-start | bytes 393224 | tf_op jit(solution)/shard_map/while/body/eval_jaxpr/ppermute | solution.py:24
  182.0 7.7 %collective-permute-start = (bf16[4,2,8192]{2,1,0:T(2,128)(2,1)S(1)}, bf16[4,2,8192]{2,1,0:T(2,128)(2,1)S(1)}, u32[]{:S(2)}, u32[]{:S(2)}) collective-permute-start(bf16[4,2,8192]{2,1,0:T(2,128)(2,1)S(1)} %get-tuple-element.426), channel_id=1, source_target_pairs={{0,1},{1,2},{2,3},{3,4},{4,5},{5,6},{6,7},{8,9},{9,10},{10,11},{11... | collective-permute-start | bytes 393224 | tf_op jit(solution)/shard_map/while/body/eval_jaxpr/ppermute | solution.py:24
  197.5 7.7 %collective-permute-start = (bf16[4,2,8192]{2,1,0:T(2,128)(2,1)S(1)}, bf16[4,2,8192]{2,1,0:T(2,128)(2,1)S(1)}, u32[]{:S(2)}, u32[]{:S(2)}) collective-permute-start(bf16[4,2,8192]{2,1,0:T(2,128)(2,1)S(1)} %get-tuple-element.426), channel_id=1, source_target_pairs={{0,1},{1,2},{2,3},{3,4},{4,5},{5,6},{6,7},{8,9},{9,10},{10,11},{11... | collective-permute-start | bytes 393224 | tf_op jit(solution)/shard_map/while/body/eval_jaxpr/ppermute | solution.py:24

commit v3 on v1

--- a/solution.py
+++ b/solution.py
@@ -87,13 +87,10 @@
     spots = jnp.arange(chosen.shape[1])[:, None] * page_len + jnp.arange(page_len)[None, :]
     keep = spots[None, :, :] < lens[moving][:, None, None]
     outgoing = jnp.where(keep[:, :, None, None, :, None], outgoing, jnp.zeros((), jnp.bfloat16))
-    received, arrived_rows = partner((outgoing, inputs[:, moving]), "inst", 0)
-    arrived_lens = partner(lens[moving], "inst", 0)
-    caches = pool[table].at[moving].set(received)
-    lens_used = lens.at[moving].set(arrived_lens)
-    inputs = inputs.at[:, moving].set(arrived_rows)
-    keys = caches[:, :, 0]
-    values = caches[:, :, 1]
+    received = partner(outgoing, "inst", 0)
+    keys = pool[:, 0][table]
+    values = pool[:, 1][table]
+    lens_used = lens
     section = lax.axis_index("section")
     count = lax.axis_size("section")
     chunks = CHUNKS
@@ -123,6 +120,8 @@
         jnp.zeros((steps, reqs, width), jnp.bfloat16),
     )
     _, finished = lax.fori_loop(0, chunks + count - 1, tick, start_carry)
+    handed = partner(finished[:, moving], "inst", 0)
+    finished = finished.at[:, moving].set(handed)
     return (finished[None, None], received[None, None])
 
 

time: 190 us -> 187 us (0.984)
    scatter x3 -> x1, local copies, waits for them, and re-layouts: 6.48 us -> 0.64 us  [per_device(): finished = finished.at[:, moving].set(handed)]
    dynamic_update_slice x9 -> x0, other arithmetic: 3.58 us -> none  [tick(): lax.dynamic_update_slice(finished, jnp.where(live, result, previous), (ze...]
    select_n x2 -> x11, other arithmetic: 0.66 us -> 3.94 us  [the longest x9 3.28 us: tick(): jnp.where(live, result, previous)]
    gather x2 -> x3, local copies, waits for them, and re-layouts: 8.81 us -> 11.2 us  [the longest x1 5.3 us: per_device(): values = pool[:, 1][table]]
    ppermute x9, waiting for transfers between devices: 67.7 us -> 65.5 us  [passed_along(): return lax.ppermute(array, axis, pairs)]
    dynamic_update_slice x0 -> x9, local copies, waits for them, and re-layouts: none -> 2.03 us  [tick(): lax.dynamic_update_slice(finished, jnp.where(live, result, previous), (ze...]
    unnamed x15 -> x12, local copies, waits for them, and re-layouts: 4.43 us -> 4.26 us
  transfers between devices with their start and end apart: 12 -> 11, of which waited for: 9 -> 10; matrix products, arithmetic and copies ran while one was open for 6% -> 46% of each run, Pallas kernels for 0% -> 0%
where the time goes in v3:
time: 187 us; the launch traced here: 186 us
  waiting for transfers between devices  66.8 us (36%)
  matrix products  40.3 us (22%)
  local copies, waits for them, and re-layouts  39.2 us (21%)
  starting transfers between devices  19.5 us (10%)
  other arithmetic  17.8 us (10%)
    ppermute x9, waiting for transfers between devices, passed_along(): return lax.ppermute(array, axis, pairs)  65.5 us
    dot_general x9, matrix products, layer(): jnp.einsum('rjgxd,rjgpd->rjgxp', wide_query, keys, preferred_element_type...  29.2 us
    ppermute x9, starting transfers between devices, passed_along(): return lax.ppermute(array, axis, pairs)  19.4 us
    dot_general x9, matrix products, layer(): jnp.einsum('rjgxp,rjgpd->rjgxd', cache_w, values, preferred_element_type=...  6.32 us
    squeeze x1, local copies, waits for them, and re-layouts, per_device(): values = pool[:, 1][table]  6.1 us
    gather x1, local copies, waits for them, and re-layouts, per_device(): values = pool[:, 1][table]  5.3 us
    gather x1, local copies, waits for them, and re-layouts, per_device(): keys = pool[:, 0][table]  5.2 us
    gather x1, local copies, waits for them, and re-layouts, per_device(): outgoing = pool[chosen]  4.33 us
  transfers between devices with their start and end apart: 11, of which 10 were waited for; matrix products, arithmetic and copies ran while one was open for 46% of the time, Pallas kernels for 0%

profile of v3, /device:TPU:26, one launch (start us, length us, event | category | flops | bytes accessed | tf_op | source)
XLA Modules:
  0.0 185.9 jit_solution(314182845871319416)
XLA Ops:
  4.1 4.3 %gather_fusion.5 = bf16[4,2,8,128,128]{4,3,2,1,0:T(8,128)(2,1)S(1)} fusion(bf16[16,2,8,128,128]{4,3,2,1,0:T(8,128)(2,1)} %bitcast.66, s32[1024]{0:T(1024)S(1)} %pad_clamp_fusion), kind=kCustom, calls=%fused_computation.5 | custom fusion | bytes 4194320 | tf_op jit(solution)/shard_map/gather | solution.py:86
  10.1 6.1 %slice_bitcast_fusion = (bf16[16,8,128,128]{3,2,1,0:T(8,128)(2,1)}, bf16[16,8,128,128]{3,2,1,0:T(8,128)(2,1)}) fusion(bf16[16,2,8,128,128]{4,3,2,1,0:T(8,128)(2,1)} %bitcast.67), kind=kLoop, calls=%fused_computation.55 | loop fusion | bytes 16777216 | tf_op jit(solution)/shard_map/squeeze | solution.py:92
  16.4 5.2 %gather_fusion = bf16[16,8,128,128]{3,2,1,0:T(8,128)(2,1)} fusion(bf16[16,8,128,128]{3,2,1,0:T(8,128)(2,1)} %get-tuple-element.339, s32[1024]{0:T(1024)S(1)} %pad_clamp_fusion.2), kind=kCustom, calls=%fused_computation | custom fusion | bytes 8388672 | tf_op jit(solution)/shard_map/gather | solution.py:91
  21.6 5.3 %gather_fusion.1 = bf16[16,8,128,128]{3,2,1,0:T(8,128)(2,1)} fusion(bf16[16,8,128,128]{3,2,1,0:T(8,128)(2,1)} %get-tuple-element.338, s32[1024]{0:T(1024)S(1)} %pad_clamp_fusion.2), kind=kCustom, calls=%fused_computation.1 | custom fusion | bytes 8388672 | tf_op jit(solution)/shard_map/gather | solution.py:92
  27.2 151.8 %while.17 = (s32[]{:T(128)}, bf16[4,4,8192]{2,1,0:T(4,128)(2,1)S(1)}, bf16[4,8,8192]{2,0,1:T(4,128)(2,1)S(1)}, pred[]{:T(512)}, s32[]{:T(128)}, /*index=5*/bf16[...) while((s32[]{:T(128)}, ...), condition=%wide.region_7.8_spmd, body=%wide.region_0.7_spmd.sunk | while | flops 140426912 | bytes 36353176 | solution.py:122
  28.9 3.2 %fusion.52 = (f32[4,8,32]{2,1,0:T(8,128)S(1)}, f32[4,2,8,32,128]{4,3,2,1,0:T(8,128)S(1)}) fusion(bf16[8,2,8,128,128]{4,3,2,1,0:T(8,128)(2,1)} %get-tuple-element.468, s32[]{:T(128)S(6)} %select_n.159, bf16[4,8,32,128]{3,2,1,0:T(8,128)(2,1)S(1)} %bitcast.65, pred[4,2,128]{2,1,0:T(4,128)(4,1)S(1)} %broadcast_compare_fusion.3), kind=kOutput, calls=%fused_computation.69.clone.1 | convolution fusion | flops 67894272 | bytes 3412996 | tf_op jit(solution)/shard_map/while/body/eval_jaxpr/rjgxd,rjgpd->rjgxp/dot_general | solution.py:44
  34.4 3.4 %collective-permute-start = (bf16[4,4,8192]{2,1,0:T(4,128)(2,1)S(1)}, bf16[4,4,8192]{2,1,0:T(4,128)(2,1)S(1)}, u32[]{:S(2)}, u32[]{:S(2)}) collective-permute-start(bf16[4,4,8192]{2,1,0:T(4,128)(2,1)S(1)} %get-tuple-element.425), channel_id=1, source_target_pairs={{0,1},{1,2},{2,3},{3,4},{4,5},{5,6},{6,7},{8,9},{9,10},{10,11},{11... | collective-permute-start | bytes 786440 | tf_op jit(solution)/shard_map/while/body/eval_jaxpr/ppermute | solution.py:24
  38.1 7.8 %collective-permute-done = bf16[4,4,8192]{2,1,0:T(4,128)(2,1)S(1)} collective-permute-done((bf16[4,4,8192]{2,1,0:T(4,128)(2,1)S(1)}, bf16[4,4,8192]{2,1,0:T(4,128)(2,1)S(1)}, u32[]{:S(2)}, u32[]{:S(2)}) %collective-permute-start) | collective-permute-done | bytes 262176 | tf_op jit(solution)/shard_map/while/body/eval_jaxpr/ppermute | solution.py:24
  47.6 3.2 %fusion.52 = (f32[4,8,32]{2,1,0:T(8,128)S(1)}, f32[4,2,8,32,128]{4,3,2,1,0:T(8,128)S(1)}) fusion(bf16[8,2,8,128,128]{4,3,2,1,0:T(8,128)(2,1)} %get-tuple-element.468, s32[]{:T(128)S(6)} %select_n.159, bf16[4,8,32,128]{3,2,1,0:T(8,128)(2,1)S(1)} %bitcast.65, pred[4,2,128]{2,1,0:T(4,128)(4,1)S(1)} %broadcast_compare_fusion.3), kind=kOutput, calls=%fused_computation.69.clone.1 | convolution fusion | flops 67894272 | bytes 3412996 | tf_op jit(solution)/shard_map/while/body/eval_jaxpr/rjgxd,rjgpd->rjgxp/dot_general | solution.py:44
  55.8 8.0 %collective-permute-done = bf16[4,4,8192]{2,1,0:T(4,128)(2,1)S(1)} collective-permute-done((bf16[4,4,8192]{2,1,0:T(4,128)(2,1)S(1)}, bf16[4,4,8192]{2,1,0:T(4,128)(2,1)S(1)}, u32[]{:S(2)}, u32[]{:S(2)}) %collective-permute-start) | collective-permute-done | bytes 262176 | tf_op jit(solution)/shard_map/while/body/eval_jaxpr/ppermute | solution.py:24
  65.5 3.2 %fusion.52 = (f32[4,8,32]{2,1,0:T(8,128)S(1)}, f32[4,2,8,32,128]{4,3,2,1,0:T(8,128)S(1)}) fusion(bf16[8,2,8,128,128]{4,3,2,1,0:T(8,128)(2,1)} %get-tuple-element.468, s32[]{:T(128)S(6)} %select_n.159, bf16[4,8,32,128]{3,2,1,0:T(8,128)(2,1)S(1)} %bitcast.65, pred[4,2,128]{2,1,0:T(4,128)(4,1)S(1)} %broadcast_compare_fusion.3), kind=kOutput, calls=%fused_computation.69.clone.1 | convolution fusion | flops 67894272 | bytes 3412996 | tf_op jit(solution)/shard_map/while/body/eval_jaxpr/rjgxd,rjgpd->rjgxp/dot_general | solution.py:44
  73.2 7.7 %collective-permute-done = bf16[4,4,8192]{2,1,0:T(4,128)(2,1)S(1)} collective-permute-done((bf16[4,4,8192]{2,1,0:T(4,128)(2,1)S(1)}, bf16[4,4,8192]{2,1,0:T(4,128)(2,1)S(1)}, u32[]{:S(2)}, u32[]{:S(2)}) %collective-permute-start) | collective-permute-done | bytes 262176 | tf_op jit(solution)/shard_map/while/body/eval_jaxpr/ppermute | solution.py:24
  82.5 3.2 %fusion.52 = (f32[4,8,32]{2,1,0:T(8,128)S(1)}, f32[4,2,8,32,128]{4,3,2,1,0:T(8,128)S(1)}) fusion(bf16[8,2,8,128,128]{4,3,2,1,0:T(8,128)(2,1)} %get-tuple-element.468, s32[]{:T(128)S(6)} %select_n.159, bf16[4,8,32,128]{3,2,1,0:T(8,128)(2,1)S(1)} %bitcast.65, pred[4,2,128]{2,1,0:T(4,128)(4,1)S(1)} %broadcast_compare_fusion.3), kind=kOutput, calls=%fused_computation.69.clone.1 | convolution fusion | flops 67894272 | bytes 3412996 | tf_op jit(solution)/shard_map/while/body/eval_jaxpr/rjgxd,rjgpd->rjgxp/dot_general | solution.py:44
  90.2 7.0 %collective-permute-done = bf16[4,4,8192]{2,1,0:T(4,128)(2,1)S(1)} collective-permute-done((bf16[4,4,8192]{2,1,0:T(4,128)(2,1)S(1)}, bf16[4,4,8192]{2,1,0:T(4,128)(2,1)S(1)}, u32[]{:S(2)}, u32[]{:S(2)}) %collective-permute-start) | collective-permute-done | bytes 262176 | tf_op jit(solution)/shard_map/while/body/eval_jaxpr/ppermute | solution.py:24
  98.9 3.2 %fusion.52 = (f32[4,8,32]{2,1,0:T(8,128)S(1)}, f32[4,2,8,32,128]{4,3,2,1,0:T(8,128)S(1)}) fusion(bf16[8,2,8,128,128]{4,3,2,1,0:T(8,128)(2,1)} %get-tuple-element.468, s32[]{:T(128)S(6)} %select_n.159, bf16[4,8,32,128]{3,2,1,0:T(8,128)(2,1)S(1)} %bitcast.65, pred[4,2,128]{2,1,0:T(4,128)(4,1)S(1)} %broadcast_compare_fusion.3), kind=kOutput, calls=%fused_computation.69.clone.1 | convolution fusion | flops 67894272 | bytes 3412996 | tf_op jit(solution)/shard_map/while/body/eval_jaxpr/rjgxd,rjgpd->rjgxp/dot_general | solution.py:44
  106.5 7.0 %collective-permute-done = bf16[4,4,8192]{2,1,0:T(4,128)(2,1)S(1)} collective-permute-done((bf16[4,4,8192]{2,1,0:T(4,128)(2,1)S(1)}, bf16[4,4,8192]{2,1,0:T(4,128)(2,1)S(1)}, u32[]{:S(2)}, u32[]{:S(2)}) %collective-permute-start) | collective-permute-done | bytes 262176 | tf_op jit(solution)/shard_map/while/body/eval_jaxpr/ppermute | solution.py:24
  115.2 3.2 %fusion.52 = (f32[4,8,32]{2,1,0:T(8,128)S(1)}, f32[4,2,8,32,128]{4,3,2,1,0:T(8,128)S(1)}) fusion(bf16[8,2,8,128,128]{4,3,2,1,0:T(8,128)(2,1)} %get-tuple-element.468, s32[]{:T(128)S(6)} %select_n.159, bf16[4,8,32,128]{3,2,1,0:T(8,128)(2,1)S(1)} %bitcast.65, pred[4,2,128]{2,1,0:T(4,128)(4,1)S(1)} %broadcast_compare_fusion.3), kind=kOutput, calls=%fused_computation.69.clone.1 | convolution fusion | flops 67894272 | bytes 3412996 | tf_op jit(solution)/shard_map/while/body/eval_jaxpr/rjgxd,rjgpd->rjgxp/dot_general | solution.py:44
  122.9 7.0 %collective-permute-done = bf16[4,4,8192]{2,1,0:T(4,128)(2,1)S(1)} collective-permute-done((bf16[4,4,8192]{2,1,0:T(4,128)(2,1)S(1)}, bf16[4,4,8192]{2,1,0:T(4,128)(2,1)S(1)}, u32[]{:S(2)}, u32[]{:S(2)}) %collective-permute-start) | collective-permute-done | bytes 262176 | tf_op jit(solution)/shard_map/while/body/eval_jaxpr/ppermute | solution.py:24
  131.6 3.2 %fusion.52 = (f32[4,8,32]{2,1,0:T(8,128)S(1)}, f32[4,2,8,32,128]{4,3,2,1,0:T(8,128)S(1)}) fusion(bf16[8,2,8,128,128]{4,3,2,1,0:T(8,128)(2,1)} %get-tuple-element.468, s32[]{:T(128)S(6)} %select_n.159, bf16[4,8,32,128]{3,2,1,0:T(8,128)(2,1)S(1)} %bitcast.65, pred[4,2,128]{2,1,0:T(4,128)(4,1)S(1)} %broadcast_compare_fusion.3), kind=kOutput, calls=%fused_computation.69.clone.1 | convolution fusion | flops 67894272 | bytes 3412996 | tf_op jit(solution)/shard_map/while/body/eval_jaxpr/rjgxd,rjgpd->rjgxp/dot_general | solution.py:44
  139.2 7.0 %collective-permute-done = bf16[4,4,8192]{2,1,0:T(4,128)(2,1)S(1)} collective-permute-done((bf16[4,4,8192]{2,1,0:T(4,128)(2,1)S(1)}, bf16[4,4,8192]{2,1,0:T(4,128)(2,1)S(1)}, u32[]{:S(2)}, u32[]{:S(2)}) %collective-permute-start) | collective-permute-done | bytes 262176 | tf_op jit(solution)/shard_map/while/body/eval_jaxpr/ppermute | solution.py:24
  147.9 3.2 %fusion.52 = (f32[4,8,32]{2,1,0:T(8,128)S(1)}, f32[4,2,8,32,128]{4,3,2,1,0:T(8,128)S(1)}) fusion(bf16[8,2,8,128,128]{4,3,2,1,0:T(8,128)(2,1)} %get-tuple-element.468, s32[]{:T(128)S(6)} %select_n.159, bf16[4,8,32,128]{3,2,1,0:T(8,128)(2,1)S(1)} %bitcast.65, pred[4,2,128]{2,1,0:T(4,128)(4,1)S(1)} %broadcast_compare_fusion.3), kind=kOutput, calls=%fused_computation.69.clone.1 | convolution fusion | flops 67894272 | bytes 3412996 | tf_op jit(solution)/shard_map/while/body/eval_jaxpr/rjgxd,rjgpd->rjgxp/dot_general | solution.py:44
  155.6 7.0 %collective-permute-done = bf16[4,4,8192]{2,1,0:T(4,128)(2,1)S(1)} collective-permute-done((bf16[4,4,8192]{2,1,0:T(4,128)(2,1)S(1)}, bf16[4,4,8192]{2,1,0:T(4,128)(2,1)S(1)}, u32[]{:S(2)}, u32[]{:S(2)}) %collective-permute-start) | collective-permute-done | bytes 262176 | tf_op jit(solution)/shard_map/while/body/eval_jaxpr/ppermute | solution.py:24
  164.3 3.2 %fusion.52 = (f32[4,8,32]{2,1,0:T(8,128)S(1)}, f32[4,2,8,32,128]{4,3,2,1,0:T(8,128)S(1)}) fusion(bf16[8,2,8,128,128]{4,3,2,1,0:T(8,128)(2,1)} %get-tuple-element.468, s32[]{:T(128)S(6)} %select_n.159, bf16[4,8,32,128]{3,2,1,0:T(8,128)(2,1)S(1)} %bitcast.65, pred[4,2,128]{2,1,0:T(4,128)(4,1)S(1)} %broadcast_compare_fusion.3), kind=kOutput, calls=%fused_computation.69.clone.1 | convolution fusion | flops 67894272 | bytes 3412996 | tf_op jit(solution)/shard_map/while/body/eval_jaxpr/rjgxd,rjgpd->rjgxp/dot_general | solution.py:44
  171.9 7.0 %collective-permute-done = bf16[4,4,8192]{2,1,0:T(4,128)(2,1)S(1)} collective-permute-done((bf16[4,4,8192]{2,1,0:T(4,128)(2,1)S(1)}, bf16[4,4,8192]{2,1,0:T(4,128)(2,1)S(1)}, u32[]{:S(2)}, u32[]{:S(2)}) %collective-permute-start) | collective-permute-done | bytes 262176 | tf_op jit(solution)/shard_map/while/body/eval_jaxpr/ppermute | solution.py:24
  (287 shorter events, 64.6 us)
Async XLA Ops:
  10.1 6.1 %copy-start.5 = (s32[1,8,2]{1,2,0:T(2,128)S(1)}, s32[1,8,2]{1,2,0:T(2,128)}, u32[]{:S(2)}) copy-start(s32[1,8,2]{1,2,0:T(2,128)} %param.11) | copy-start | bytes 196
  10.1 172.7 %collective-permute-start.2 = (bf16[2,2,2,8,128,128]{5,4,3,2,1,0:T(8,128)(2,1)}, bf16[2,2,2,8,128,128]{5,4,3,2,1,0:T(8,128)(2,1)}, u32[]{:S(2)}, u32[]{:S(2)}) collective-permute-start(bf16[2,2,2,8,128,128]{5,4,3,2,1,0:T(8,128)(2,1)} %broadcast_select_fusion), channel_id=1, source_target_pairs={{0,8},{8,0},{1,9},{9,1},{2,10},{10,2},{3,11},{11,3},{4,12},{12,4},... | collective-permute-start | bytes 6291464 | tf_op jit(solution)/shard_map/ppermute | solution.py:18
  21.6 5.5 %copy-start = (s32[1,8]{1,0:T(1,128)S(1)}, s32[1,8]{1,0:T(1,128)}, u32[]{:S(2)}) copy-start(s32[1,8]{1,0:T(1,128)} %param.12) | copy-start | bytes 100
  21.6 5.5 %copy-start.2 = (bf16[1,4,8,8192]{3,2,1,0:T(8,128)(2,1)S(1)}, bf16[1,4,8,8192]{3,2,1,0:T(8,128)(2,1)}, u32[]{:S(2)}) copy-start(bf16[1,4,8,8192]{3,2,1,0:T(8,128)(2,1)} %param.9) | copy-start | bytes 1572868
  21.6 5.5 %copy-start.3 = (f32[1,8192]{1,0:T(1,128)S(1)}, f32[1,8192]{1,0:T(1,128)}, u32[]{:S(2)}) copy-start(f32[1,8192]{1,0:T(1,128)} %param.15) | copy-start | bytes 98308
  21.6 5.6 %copy-start.4 = (f32[1,8192]{1,0:T(1,128)S(1)}, f32[1,8192]{1,0:T(1,128)}, u32[]{:S(2)}) copy-start(f32[1,8192]{1,0:T(1,128)} %param.14) | copy-start | bytes 98308
  28.1 4.5 %copy-start.1 = (bf16[8,2,8,128,128]{4,3,2,1,0:T(8,128)(2,1)S(1)}, bf16[8,2,8,128,128]{4,3,2,1,0:T(8,128)(2,1)}, u32[]{:S(2)}) copy-start(bf16[8,2,8,128,128]{4,3,2,1,0:T(8,128)(2,1)} %get-tuple-element.469) | copy-start | bytes 12582916 | tf_op jit(solution)/shard_map/while
  34.4 11.5 %collective-permute-start = (bf16[4,4,8192]{2,1,0:T(4,128)(2,1)S(1)}, bf16[4,4,8192]{2,1,0:T(4,128)(2,1)S(1)}, u32[]{:S(2)}, u32[]{:S(2)}) collective-permute-start(bf16[4,4,8192]{2,1,0:T(4,128)(2,1)S(1)} %get-tuple-element.425), channel_id=1, source_target_pairs={{0,1},{1,2},{2,3},{3,4},{4,5},{5,6},{6,7},{8,9},{9,10},{10,11},{11... | collective-permute-start | bytes 786440 | tf_op jit(solution)/shard_map/while/body/eval_jaxpr/ppermute | solution.py:24
  46.8 4.5 %copy-start.1 = (bf16[8,2,8,128,128]{4,3,2,1,0:T(8,128)(2,1)S(1)}, bf16[8,2,8,128,128]{4,3,2,1,0:T(8,128)(2,1)}, u32[]{:S(2)}) copy-start(bf16[8,2,8,128,128]{4,3,2,1,0:T(8,128)(2,1)} %get-tuple-element.469) | copy-start | bytes 12582916 | tf_op jit(solution)/shard_map/while
  53.1 10.7 %collective-permute-start = (bf16[4,4,8192]{2,1,0:T(4,128)(2,1)S(1)}, bf16[4,4,8192]{2,1,0:T(4,128)(2,1)S(1)}, u32[]{:S(2)}, u32[]{:S(2)}) collective-permute-start(bf16[4,4,8192]{2,1,0:T(4,128)(2,1)S(1)} %get-tuple-element.425), channel_id=1, source_target_pairs={{0,1},{1,2},{2,3},{3,4},{4,5},{5,6},{6,7},{8,9},{9,10},{10,11},{11... | collective-permute-start | bytes 786440 | tf_op jit(solution)/shard_map/while/body/eval_jaxpr/ppermute | solution.py:24
  64.7 4.5 %copy-start.1 = (bf16[8,2,8,128,128]{4,3,2,1,0:T(8,128)(2,1)S(1)}, bf16[8,2,8,128,128]{4,3,2,1,0:T(8,128)(2,1)}, u32[]{:S(2)}) copy-start(bf16[8,2,8,128,128]{4,3,2,1,0:T(8,128)(2,1)} %get-tuple-element.469) | copy-start | bytes 12582916 | tf_op jit(solution)/shard_map/while
  71.0 9.8 %collective-permute-start = (bf16[4,4,8192]{2,1,0:T(4,128)(2,1)S(1)}, bf16[4,4,8192]{2,1,0:T(4,128)(2,1)S(1)}, u32[]{:S(2)}, u32[]{:S(2)}) collective-permute-start(bf16[4,4,8192]{2,1,0:T(4,128)(2,1)S(1)} %get-tuple-element.425), channel_id=1, source_target_pairs={{0,1},{1,2},{2,3},{3,4},{4,5},{5,6},{6,7},{8,9},{9,10},{10,11},{11... | collective-permute-start | bytes 786440 | tf_op jit(solution)/shard_map/while/body/eval_jaxpr/ppermute | solution.py:24
  81.8 4.5 %copy-start.1 = (bf16[8,2,8,128,128]{4,3,2,1,0:T(8,128)(2,1)S(1)}, bf16[8,2,8,128,128]{4,3,2,1,0:T(8,128)(2,1)}, u32[]{:S(2)}) copy-start(bf16[8,2,8,128,128]{4,3,2,1,0:T(8,128)(2,1)} %get-tuple-element.469) | copy-start | bytes 12582916 | tf_op jit(solution)/shard_map/while
  88.0 9.2 %collective-permute-start = (bf16[4,4,8192]{2,1,0:T(4,128)(2,1)S(1)}, bf16[4,4,8192]{2,1,0:T(4,128)(2,1)S(1)}, u32[]{:S(2)}, u32[]{:S(2)}) collective-permute-start(bf16[4,4,8192]{2,1,0:T(4,128)(2,1)S(1)} %get-tuple-element.425), channel_id=1, source_target_pairs={{0,1},{1,2},{2,3},{3,4},{4,5},{5,6},{6,7},{8,9},{9,10},{10,11},{11... | collective-permute-start | bytes 786440 | tf_op jit(solution)/shard_map/while/body/eval_jaxpr/ppermute | solution.py:24
  98.1 4.5 %copy-start.1 = (bf16[8,2,8,128,128]{4,3,2,1,0:T(8,128)(2,1)S(1)}, bf16[8,2,8,128,128]{4,3,2,1,0:T(8,128)(2,1)}, u32[]{:S(2)}) copy-start(bf16[8,2,8,128,128]{4,3,2,1,0:T(8,128)(2,1)} %get-tuple-element.469) | copy-start | bytes 12582916 | tf_op jit(solution)/shard_map/while
  104.4 9.2 %collective-permute-start = (bf16[4,4,8192]{2,1,0:T(4,128)(2,1)S(1)}, bf16[4,4,8192]{2,1,0:T(4,128)(2,1)S(1)}, u32[]{:S(2)}, u32[]{:S(2)}) collective-permute-start(bf16[4,4,8192]{2,1,0:T(4,128)(2,1)S(1)} %get-tuple-element.425), channel_id=1, source_target_pairs={{0,1},{1,2},{2,3},{3,4},{4,5},{5,6},{6,7},{8,9},{9,10},{10,11},{11... | collective-permute-start | bytes 786440 | tf_op jit(solution)/shard_map/while/body/eval_jaxpr/ppermute | solution.py:24
  114.5 4.5 %copy-start.1 = (bf16[8,2,8,128,128]{4,3,2,1,0:T(8,128)(2,1)S(1)}, bf16[8,2,8,128,128]{4,3,2,1,0:T(8,128)(2,1)}, u32[]{:S(2)}) copy-start(bf16[8,2,8,128,128]{4,3,2,1,0:T(8,128)(2,1)} %get-tuple-element.469) | copy-start | bytes 12582916 | tf_op jit(solution)/shard_map/while
  120.7 9.2 %collective-permute-start = (bf16[4,4,8192]{2,1,0:T(4,128)(2,1)S(1)}, bf16[4,4,8192]{2,1,0:T(4,128)(2,1)S(1)}, u32[]{:S(2)}, u32[]{:S(2)}) collective-permute-start(bf16[4,4,8192]{2,1,0:T(4,128)(2,1)S(1)} %get-tuple-element.425), channel_id=1, source_target_pairs={{0,1},{1,2},{2,3},{3,4},{4,5},{5,6},{6,7},{8,9},{9,10},{10,11},{11... | collective-permute-start | bytes 786440 | tf_op jit(solution)/shard_map/while/body/eval_jaxpr/ppermute | solution.py:24
  137.1 9.2 %collective-permute-start = (bf16[4,4,8192]{2,1,0:T(4,128)(2,1)S(1)}, bf16[4,4,8192]{2,1,0:T(4,128)(2,1)S(1)}, u32[]{:S(2)}, u32[]{:S(2)}) collective-permute-start(bf16[4,4,8192]{2,1,0:T(4,128)(2,1)S(1)} %get-tuple-element.425), channel_id=1, source_target_pairs={{0,1},{1,2},{2,3},{3,4},{4,5},{5,6},{6,7},{8,9},{9,10},{10,11},{11... | collective-permute-start | bytes 786440 | tf_op jit(solution)/shard_map/while/body/eval_jaxpr/ppermute | solution.py:24
  147.2 4.5 %copy-start.1 = (bf16[8,2,8,128,128]{4,3,2,1,0:T(8,128)(2,1)S(1)}, bf16[8,2,8,128,128]{4,3,2,1,0:T(8,128)(2,1)}, u32[]{:S(2)}) copy-start(bf16[8,2,8,128,128]{4,3,2,1,0:T(8,128)(2,1)} %get-tuple-element.469) | copy-start | bytes 12582916 | tf_op jit(solution)/shard_map/while
  153.4 9.2 %collective-permute-start = (bf16[4,4,8192]{2,1,0:T(4,128)(2,1)S(1)}, bf16[4,4,8192]{2,1,0:T(4,128)(2,1)S(1)}, u32[]{:S(2)}, u32[]{:S(2)}) collective-permute-start(bf16[4,4,8192]{2,1,0:T(4,128)(2,1)S(1)} %get-tuple-element.425), channel_id=1, source_target_pairs={{0,1},{1,2},{2,3},{3,4},{4,5},{5,6},{6,7},{8,9},{9,10},{10,11},{11... | collective-permute-start | bytes 786440 | tf_op jit(solution)/shard_map/while/body/eval_jaxpr/ppermute | solution.py:24
  163.5 4.5 %copy-start.1 = (bf16[8,2,8,128,128]{4,3,2,1,0:T(8,128)(2,1)S(1)}, bf16[8,2,8,128,128]{4,3,2,1,0:T(8,128)(2,1)}, u32[]{:S(2)}) copy-start(bf16[8,2,8,128,128]{4,3,2,1,0:T(8,128)(2,1)} %get-tuple-element.469) | copy-start | bytes 12582916 | tf_op jit(solution)/shard_map/while
  169.8 9.2 %collective-permute-start = (bf16[4,4,8192]{2,1,0:T(4,128)(2,1)S(1)}, bf16[4,4,8192]{2,1,0:T(4,128)(2,1)S(1)}, u32[]{:S(2)}, u32[]{:S(2)}) collective-permute-start(bf16[4,4,8192]{2,1,0:T(4,128)(2,1)S(1)} %get-tuple-element.425), channel_id=1, source_target_pairs={{0,1},{1,2},{2,3},{3,4},{4,5},{5,6},{6,7},{8,9},{9,10},{10,11},{11... | collective-permute-start | bytes 786440 | tf_op jit(solution)/shard_map/while/body/eval_jaxpr/ppermute | solution.py:24
  179.6 1.4 collective-permute-start.1
  (1 other events, 4.5 us)

commit v4 on v3

--- a/solution.py
+++ b/solution.py
@@ -4,6 +4,8 @@
 import jax.numpy as jnp
 from jax import lax
 from jax.sharding import PartitionSpec as P
+from jax.experimental import pallas as pl
+from jax.experimental.pallas import tpu as pltpu
 
 CHUNKS = 2
 
@@ -72,6 +74,105 @@
     return (wide + scale * attended).astype(jnp.bfloat16)
 
 
+def attend_kernel(table_ref, lens_ref, start_ref, q_ref, f_ref, *refs):
+    pages = (len(refs) - 1) // 2
+    key_refs = refs[:pages]
+    value_refs = refs[pages:2 * pages]
+    o_ref = refs[-1]
+    req = start_ref[0] + pl.program_id(0)
+    length = lens_ref[req]
+    query = q_ref[0]
+    kv_heads, rows, head = query.shape
+    fresh = f_ref[0].astype(jnp.float32)
+    steps = fresh.shape[1]
+    group = rows // steps
+    page_len = key_refs[0].shape[3]
+    factor = 1.0 / math.sqrt(head)
+    spots = lax.broadcasted_iota(jnp.int32, (kv_heads, rows, page_len), 2)
+    scores = []
+    for j in range(pages):
+        got = lax.dot_general(
+            query, key_refs[j][0, 0], (((2,), (2,)), ((0,), (0,))),
+            preferred_element_type=jnp.float32,
+        ) * factor
+        scores.append(jnp.where(spots + j * page_len < length, got, -1e30))
+    wide_query = query.astype(jnp.float32)
+    step_of = lax.broadcasted_iota(jnp.int32, (kv_heads, rows), 1) // group
+    news = []
+    for s in range(steps):
+        got = jnp.sum(wide_query * fresh[:, s][:, None, :], axis=-1) * factor
+        news.append(jnp.where(step_of >= s, got, -1e30))
+    top = jnp.max(scores[0], axis=-1)
+    for j in range(1, pages):
+        top = jnp.maximum(top, jnp.max(scores[j], axis=-1))
+    for s in range(steps):
+        top = jnp.maximum(top, news[s])
+    exps = [jnp.exp(x - top[..., None]) for x in scores]
+    new_exps = [jnp.exp(x - top) for x in news]
+    total = sum(jnp.sum(x, axis=-1) for x in exps) + sum(new_exps)
+    out = None
+    for j in range(pages):
+        weight = (exps[j] / total[..., None]).astype(jnp.bfloat16)
+        part = lax.dot_general(
+            weight, value_refs[j][0, 0], (((2,), (1,)), ((0,), (0,))),
+            preferred_element_type=jnp.float32,
+        )
+        out = part if out is None else out + part
+    for s in range(steps):
+        weight = (new_exps[s] / total).astype(jnp.bfloat16).astype(jnp.float32)
+        out = out + weight[..., None] * fresh[:, s][:, None, :]
+    o_ref[0] = out
+
+
+def attend(query, fresh, pool, table, lens, start):
+    reqs, kv_heads, rows, head = query.shape
+    steps = fresh.shape[2]
+    pages = table.shape[1]
+    page_len = pool.shape[3]
+    flat = table.reshape(-1)
+
+    def page_spec(j, half):
+        def index(r, table_ref, lens_ref, start_ref):
+            return (table_ref[(start_ref[0] + r) * pages + j], half, 0, 0, 0)
+
+        return pl.BlockSpec((1, 1, kv_heads, page_len, head), index)
+
+    def row_spec(width):
+        return pl.BlockSpec((1, kv_heads, width, head), lambda r, *_: (r, 0, 0, 0))
+
+    grid_spec = pltpu.PrefetchScalarGridSpec(
+        num_scalar_prefetch=3,
+        grid=(reqs,),
+        in_specs=[row_spec(rows), row_spec(steps)]
+        + [page_spec(j, 0) for j in range(pages)]
+        + [page_spec(j, 1) for j in range(pages)],
+        out_specs=row_spec(rows),
+    )
+    return pl.pallas_call(
+        attend_kernel,
+        grid_spec=grid_spec,
+        out_shape=jax.ShapeDtypeStruct(query.shape, jnp.float32),
+    )(flat, lens, start.reshape(1), query, fresh, *([pool] * (2 * pages)))
+
+
+def layer_paged(rows, pool, table, lens, start, gain, scale):
+    steps, reqs, width = rows.shape
+    kv_heads = pool.shape[2]
+    head = pool.shape[4]
+    group = width // (kv_heads * head)
+    wide = rows.astype(jnp.float32)
+    normed = wide * lax.rsqrt(jnp.mean(wide * wide, axis=-1, keepdims=True) + 1e-05) * gain
+    heads = normed.reshape(steps, reqs, kv_heads, group, head)
+    query = jnp.transpose(heads.astype(jnp.bfloat16), (1, 2, 0, 3, 4))
+    query = query.reshape(reqs, kv_heads, steps * group, head)
+    fresh = jnp.mean(heads, axis=3).astype(jnp.bfloat16)
+    fresh = jnp.transpose(fresh, (1, 2, 0, 3))
+    attended = attend(query, fresh, pool, table, lens, start)
+    attended = attended.reshape(reqs, kv_heads, steps, group, head)
+    attended = jnp.transpose(attended, (2, 0, 1, 3, 4)).reshape(steps, reqs, width)
+    return (wide + scale * attended).astype(jnp.bfloat16)
+
+
 def per_device(tokens, kv_pool, page_table, lengths, migrate_ids, norm_gain, out_scale):
     inputs = tokens[0]
     pool = kv_pool[0, 0]
@@ -88,8 +189,6 @@
     keep = spots[None, :, :] < lens[moving][:, None, None]
     outgoing = jnp.where(keep[:, :, None, None, :, None], outgoing, jnp.zeros((), jnp.bfloat16))
     received = partner(outgoing, "inst", 0)
-    keys = pool[:, 0][table]
-    values = pool[:, 1][table]
     lens_used = lens
     section = lax.axis_index("section")
     count = lax.axis_size("section")
@@ -104,10 +203,7 @@
         zero = jnp.zeros((), jnp.int32)
         first = lax.dynamic_slice_in_dim(inputs, start, block, 1)
         rows = jnp.where(section == 0, first, incoming)
-        part_keys = lax.dynamic_slice_in_dim(keys, start, block, 0)
-        part_values = lax.dynamic_slice_in_dim(values, start, block, 0)
-        part_lens = lax.dynamic_slice_in_dim(lens_used, start, block, 0)
-        result = layer(rows, part_keys, part_values, part_lens, gain, scale)
+        result = layer_paged(rows, pool, table, lens_used, start, gain, scale)
         previous = lax.dynamic_slice_in_dim(finished, start, block, 1)
         finished = lax.dynamic_update_slice(
             finished, jnp.where(live, result, previous), (zero, start, zero)

time: 187 us -> 208 us (1.11)
  Pallas kernels: 0 us -> 62.4 us
  matrix products: 40.3 us -> 0 us
  other arithmetic: 17.8 us -> 12.2 us
  local copies, waits for them, and re-layouts: 39.2 us -> 43.3 us
    pallas_call x0 -> x9, Pallas kernels: none -> 62.4 us  [attend(): pl.pallas_call(attend_kernel, grid_spec=grid_spec, out_shape=jax.ShapeDty...]
    dot_general x36 -> x0, matrix products: 40.3 us -> none  [the longest x9 29.2 us: layer(): jnp.einsum('rjgxd,rjgpd->rjgxp', wide_query, keys, preferred_element_type...]
    transpose x18, local copies, waits for them, and re-layouts: 0.84 us -> 16.6 us  [the longest x9 9.77 us: layer_paged(): jnp.transpose(attended, (2, 0, 1, 3, 4)).reshape(steps, reqs, width)]
    gather x2 -> x0, local copies, waits for them, and re-layouts: 10.5 us -> none  [the longest x1 5.3 us: per_device(): values = pool[:, 1][table]]
    squeeze x1 -> x0, local copies, waits for them, and re-layouts: 6.1 us -> none  [per_device(): values = pool[:, 1][table]]
    while x18 -> x10, local copies, waits for them, and re-layouts: 0.04 us -> 5.65 us
    reduce_sum x36 -> x18, other arithmetic: 8.8 us -> 4.79 us  [the longest x9 3.27 us: layer_paged(): jnp.mean(wide * wide, axis=-1, keepdims=True) + 1e-05]
    unnamed x12 -> x14, local copies, waits for them, and re-layouts: 4.26 us -> 4.57 us
  transfers between devices with their start and end apart: 11 -> 11, of which waited for: 10 -> 10; matrix products, arithmetic and copies ran while one was open for 46% -> 21% of each run, Pallas kernels for 0% -> 30%
where the time goes in v4:
time: 208 us; the launch traced here: 206 us
  waiting for transfers between devices  66.8 us (32%)
  Pallas kernels  62.4 us (30%)
  local copies, waits for them, and re-layouts  43.3 us (21%)
  starting transfers between devices  19.5 us (9%)
  other arithmetic  12.2 us (6%)
    ppermute x9, waiting for transfers between devices, passed_along(): return lax.ppermute(array, axis, pairs)  65.5 us
    pallas_call x9, Pallas kernels, attend(): pl.pallas_call(attend_kernel, grid_spec=grid_spec, out_shape=jax.ShapeDty...  62.4 us
    ppermute x9, starting transfers between devices, passed_along(): return lax.ppermute(array, axis, pairs)  19.4 us
    transpose x9, local copies, waits for them, and re-layouts, layer_paged(): jnp.transpose(attended, (2, 0, 1, 3, 4)).reshape(steps, reqs, width)  9.77 us
    transpose x9, local copies, waits for them, and re-layouts, layer_paged(): query = jnp.transpose(heads.astype(jnp.bfloat16), (1, 2, 0, 3, 4))  6.79 us
    while x9, local copies, waits for them, and re-layouts  5.57 us
    unnamed x14, local copies, waits for them, and re-layouts  4.57 us
    gather x1, local copies, waits for them, and re-layouts, per_device(): outgoing = pool[chosen]  4.33 us
  transfers between devices with their start and end apart: 11, of which 10 were waited for; matrix products, arithmetic and copies ran while one was open for 21% of the time, Pallas kernels for 30%

profile of v4, /device:TPU:26, one launch (start us, length us, event | category | flops | bytes accessed | tf_op | source)
XLA Modules:
  0.0 205.8 jit_solution(13014639043984119489)
XLA Ops:
  4.2 4.3 %gather_fusion.3 = bf16[4,2,8,128,128]{4,3,2,1,0:T(8,128)(2,1)S(1)} fusion(bf16[16,2,8,128,128]{4,3,2,1,0:T(8,128)(2,1)} %bitcast.52, s32[1024]{0:T(1024)S(1)} %pad_clamp_fusion), kind=kCustom, calls=%fused_computation.3 | custom fusion | bytes 4194320 | tf_op jit(solution)/shard_map/gather | solution.py:187
  10.9 187.9 %while.17 = (s32[]{:T(128)}, bf16[4,4,8192]{2,1,0:T(4,128)(2,1)S(1)}, bf16[4,8,8192]{2,0,1:T(4,128)(2,1)S(1)}, pred[]{:T(512)}, s32[]{:T(128)}, /*index=5*/bf16[...) while((s32[]{:T(128)}, ...), condition=%wide.wide.region_3.4_spmd, body=%wide.wide.region_0.3_spmd.sunk | while | flops 1851420 | bytes 9994810 | solution.py:218
  13.5 6.9 %eval_jaxpr.6 = f32[4,8,32,128]{3,2,1,0:T(8,128)} custom-call(s32[16]{0:T(128)S(1)} %get-tuple-element.473.table_ref, s32[8]{0:T(128)S(1)} %get-tuple-element.471.lens_ref, s32[1]{0:T(128)} %bitcast.45.start_ref, bf16[4,8,32,128]{3,2,1,0:T(8,128)(2,1)} %bitcast.57, bf16[4,8,4,128]{3,2,1,0:T(4,128)(2,1)} %bitcast.60, ...), custom_call_target="tpu_custom_call" | custom-call | tf_op jit(solution)/shard_map/while/body/eval_jaxpr/pallas_call | solution.py:151
  22.1 3.4 %collective-permute-start = (bf16[4,4,8192]{2,1,0:T(4,128)(2,1)S(1)}, bf16[4,4,8192]{2,1,0:T(4,128)(2,1)S(1)}, u32[]{:S(2)}, u32[]{:S(2)}) collective-permute-start(bf16[4,4,8192]{2,1,0:T(4,128)(2,1)S(1)} %get-tuple-element.426), channel_id=1, source_target_pairs={{0,1},{1,2},{2,3},{3,4},{4,5},{5,6},{6,7},{8,9},{9,10},{10,11},{11... | collective-permute-start | bytes 786440 | tf_op jit(solution)/shard_map/while/body/eval_jaxpr/ppermute | solution.py:26
  25.8 7.8 %collective-permute-done = bf16[4,4,8192]{2,1,0:T(4,128)(2,1)S(1)} collective-permute-done((bf16[4,4,8192]{2,1,0:T(4,128)(2,1)S(1)}, bf16[4,4,8192]{2,1,0:T(4,128)(2,1)S(1)}, u32[]{:S(2)}, u32[]{:S(2)}) %collective-permute-start) | collective-permute-done | bytes 262176 | tf_op jit(solution)/shard_map/while/body/eval_jaxpr/ppermute | solution.py:26
  36.2 6.9 %eval_jaxpr.6 = f32[4,8,32,128]{3,2,1,0:T(8,128)} custom-call(s32[16]{0:T(128)S(1)} %get-tuple-element.473.table_ref, s32[8]{0:T(128)S(1)} %get-tuple-element.471.lens_ref, s32[1]{0:T(128)} %bitcast.45.start_ref, bf16[4,8,32,128]{3,2,1,0:T(8,128)(2,1)} %bitcast.57, bf16[4,8,4,128]{3,2,1,0:T(4,128)(2,1)} %bitcast.60, ...), custom_call_target="tpu_custom_call" | custom-call | tf_op jit(solution)/shard_map/while/body/eval_jaxpr/pallas_call | solution.py:151
  44.8 2.5 %collective-permute-start = (bf16[4,4,8192]{2,1,0:T(4,128)(2,1)S(1)}, bf16[4,4,8192]{2,1,0:T(4,128)(2,1)S(1)}, u32[]{:S(2)}, u32[]{:S(2)}) collective-permute-start(bf16[4,4,8192]{2,1,0:T(4,128)(2,1)S(1)} %get-tuple-element.426), channel_id=1, source_target_pairs={{0,1},{1,2},{2,3},{3,4},{4,5},{5,6},{6,7},{8,9},{9,10},{10,11},{11... | collective-permute-start | bytes 786440 | tf_op jit(solution)/shard_map/while/body/eval_jaxpr/ppermute | solution.py:26
  47.6 8.0 %collective-permute-done = bf16[4,4,8192]{2,1,0:T(4,128)(2,1)S(1)} collective-permute-done((bf16[4,4,8192]{2,1,0:T(4,128)(2,1)S(1)}, bf16[4,4,8192]{2,1,0:T(4,128)(2,1)S(1)}, u32[]{:S(2)}, u32[]{:S(2)}) %collective-permute-start) | collective-permute-done | bytes 262176 | tf_op jit(solution)/shard_map/while/body/eval_jaxpr/ppermute | solution.py:26
  58.1 6.9 %eval_jaxpr.6 = f32[4,8,32,128]{3,2,1,0:T(8,128)} custom-call(s32[16]{0:T(128)S(1)} %get-tuple-element.473.table_ref, s32[8]{0:T(128)S(1)} %get-tuple-element.471.lens_ref, s32[1]{0:T(128)} %bitcast.45.start_ref, bf16[4,8,32,128]{3,2,1,0:T(8,128)(2,1)} %bitcast.57, bf16[4,8,4,128]{3,2,1,0:T(4,128)(2,1)} %bitcast.60, ...), custom_call_target="tpu_custom_call" | custom-call | tf_op jit(solution)/shard_map/while/body/eval_jaxpr/pallas_call | solution.py:151
  68.9 7.7 %collective-permute-done = bf16[4,4,8192]{2,1,0:T(4,128)(2,1)S(1)} collective-permute-done((bf16[4,4,8192]{2,1,0:T(4,128)(2,1)S(1)}, bf16[4,4,8192]{2,1,0:T(4,128)(2,1)S(1)}, u32[]{:S(2)}, u32[]{:S(2)}) %collective-permute-start) | collective-permute-done | bytes 262176 | tf_op jit(solution)/shard_map/while/body/eval_jaxpr/ppermute | solution.py:26
  79.2 6.9 %eval_jaxpr.6 = f32[4,8,32,128]{3,2,1,0:T(8,128)} custom-call(s32[16]{0:T(128)S(1)} %get-tuple-element.473.table_ref, s32[8]{0:T(128)S(1)} %get-tuple-element.471.lens_ref, s32[1]{0:T(128)} %bitcast.45.start_ref, bf16[4,8,32,128]{3,2,1,0:T(8,128)(2,1)} %bitcast.57, bf16[4,8,4,128]{3,2,1,0:T(4,128)(2,1)} %bitcast.60, ...), custom_call_target="tpu_custom_call" | custom-call | tf_op jit(solution)/shard_map/while/body/eval_jaxpr/pallas_call | solution.py:151
  89.9 7.0 %collective-permute-done = bf16[4,4,8192]{2,1,0:T(4,128)(2,1)S(1)} collective-permute-done((bf16[4,4,8192]{2,1,0:T(4,128)(2,1)S(1)}, bf16[4,4,8192]{2,1,0:T(4,128)(2,1)S(1)}, u32[]{:S(2)}, u32[]{:S(2)}) %collective-permute-start) | collective-permute-done | bytes 262176 | tf_op jit(solution)/shard_map/while/body/eval_jaxpr/ppermute | solution.py:26
  99.5 6.9 %eval_jaxpr.6 = f32[4,8,32,128]{3,2,1,0:T(8,128)} custom-call(s32[16]{0:T(128)S(1)} %get-tuple-element.473.table_ref, s32[8]{0:T(128)S(1)} %get-tuple-element.471.lens_ref, s32[1]{0:T(128)} %bitcast.45.start_ref, bf16[4,8,32,128]{3,2,1,0:T(8,128)(2,1)} %bitcast.57, bf16[4,8,4,128]{3,2,1,0:T(4,128)(2,1)} %bitcast.60, ...), custom_call_target="tpu_custom_call" | custom-call | tf_op jit(solution)/shard_map/while/body/eval_jaxpr/pallas_call | solution.py:151
  110.3 7.0 %collective-permute-done = bf16[4,4,8192]{2,1,0:T(4,128)(2,1)S(1)} collective-permute-done((bf16[4,4,8192]{2,1,0:T(4,128)(2,1)S(1)}, bf16[4,4,8192]{2,1,0:T(4,128)(2,1)S(1)}, u32[]{:S(2)}, u32[]{:S(2)}) %collective-permute-start) | collective-permute-done | bytes 262176 | tf_op jit(solution)/shard_map/while/body/eval_jaxpr/ppermute | solution.py:26
  119.9 6.9 %eval_jaxpr.6 = f32[4,8,32,128]{3,2,1,0:T(8,128)} custom-call(s32[16]{0:T(128)S(1)} %get-tuple-element.473.table_ref, s32[8]{0:T(128)S(1)} %get-tuple-element.471.lens_ref, s32[1]{0:T(128)} %bitcast.45.start_ref, bf16[4,8,32,128]{3,2,1,0:T(8,128)(2,1)} %bitcast.57, bf16[4,8,4,128]{3,2,1,0:T(4,128)(2,1)} %bitcast.60, ...), custom_call_target="tpu_custom_call" | custom-call | tf_op jit(solution)/shard_map/while/body/eval_jaxpr/pallas_call | solution.py:151
  128.5 1.9 collective-permute-start
  130.7 7.0 %collective-permute-done = bf16[4,4,8192]{2,1,0:T(4,128)(2,1)S(1)} collective-permute-done((bf16[4,4,8192]{2,1,0:T(4,128)(2,1)S(1)}, bf16[4,4,8192]{2,1,0:T(4,128)(2,1)S(1)}, u32[]{:S(2)}, u32[]{:S(2)}) %collective-permute-start) | collective-permute-done | bytes 262176 | tf_op jit(solution)/shard_map/while/body/eval_jaxpr/ppermute | solution.py:26
  140.3 6.9 %eval_jaxpr.6 = f32[4,8,32,128]{3,2,1,0:T(8,128)} custom-call(s32[16]{0:T(128)S(1)} %get-tuple-element.473.table_ref, s32[8]{0:T(128)S(1)} %get-tuple-element.471.lens_ref, s32[1]{0:T(128)} %bitcast.45.start_ref, bf16[4,8,32,128]{3,2,1,0:T(8,128)(2,1)} %bitcast.57, bf16[4,8,4,128]{3,2,1,0:T(4,128)(2,1)} %bitcast.60, ...), custom_call_target="tpu_custom_call" | custom-call | tf_op jit(solution)/shard_map/while/body/eval_jaxpr/pallas_call | solution.py:151
  151.0 7.0 %collective-permute-done = bf16[4,4,8192]{2,1,0:T(4,128)(2,1)S(1)} collective-permute-done((bf16[4,4,8192]{2,1,0:T(4,128)(2,1)S(1)}, bf16[4,4,8192]{2,1,0:T(4,128)(2,1)S(1)}, u32[]{:S(2)}, u32[]{:S(2)}) %collective-permute-start) | collective-permute-done | bytes 262176 | tf_op jit(solution)/shard_map/while/body/eval_jaxpr/ppermute | solution.py:26
  160.6 6.9 %eval_jaxpr.6 = f32[4,8,32,128]{3,2,1,0:T(8,128)} custom-call(s32[16]{0:T(128)S(1)} %get-tuple-element.473.table_ref, s32[8]{0:T(128)S(1)} %get-tuple-element.471.lens_ref, s32[1]{0:T(128)} %bitcast.45.start_ref, bf16[4,8,32,128]{3,2,1,0:T(8,128)(2,1)} %bitcast.57, bf16[4,8,4,128]{3,2,1,0:T(4,128)(2,1)} %bitcast.60, ...), custom_call_target="tpu_custom_call" | custom-call | tf_op jit(solution)/shard_map/while/body/eval_jaxpr/pallas_call | solution.py:151
  171.4 7.0 %collective-permute-done = bf16[4,4,8192]{2,1,0:T(4,128)(2,1)S(1)} collective-permute-done((bf16[4,4,8192]{2,1,0:T(4,128)(2,1)S(1)}, bf16[4,4,8192]{2,1,0:T(4,128)(2,1)S(1)}, u32[]{:S(2)}, u32[]{:S(2)}) %collective-permute-start) | collective-permute-done | bytes 262176 | tf_op jit(solution)/shard_map/while/body/eval_jaxpr/ppermute | solution.py:26
  181.0 6.9 %eval_jaxpr.6 = f32[4,8,32,128]{3,2,1,0:T(8,128)} custom-call(s32[16]{0:T(128)S(1)} %get-tuple-element.473.table_ref, s32[8]{0:T(128)S(1)} %get-tuple-element.471.lens_ref, s32[1]{0:T(128)} %bitcast.45.start_ref, bf16[4,8,32,128]{3,2,1,0:T(8,128)(2,1)} %bitcast.57, bf16[4,8,4,128]{3,2,1,0:T(4,128)(2,1)} %bitcast.60, ...), custom_call_target="tpu_custom_call" | custom-call | tf_op jit(solution)/shard_map/while/body/eval_jaxpr/pallas_call | solution.py:151
  191.8 7.0 %collective-permute-done = bf16[4,4,8192]{2,1,0:T(4,128)(2,1)S(1)} collective-permute-done((bf16[4,4,8192]{2,1,0:T(4,128)(2,1)S(1)}, bf16[4,4,8192]{2,1,0:T(4,128)(2,1)S(1)}, u32[]{:S(2)}, u32[]{:S(2)}) %collective-permute-start) | collective-permute-done | bytes 262176 | tf_op jit(solution)/shard_map/while/body/eval_jaxpr/ppermute | solution.py:26
  202.6 3.2 %copy.77 = bf16[1,1,2,2,2,8,128,128]{7,6,5,4,3,2,1,0:T(8,128)(2,1)} copy(bf16[1,1,2,2,2,8,128,128]{7,6,5,4,3,2,1,0:T(8,128)(2,1)} %bitcast.20) | data formatting | bytes 4194304
  (158 shorter events, 61.0 us)
Async XLA Ops:
  8.5 1.7 copy-start.5
  8.5 2.3 %copy-start = (s32[1,8]{1,0:T(1,128)S(1)}, s32[1,8]{1,0:T(1,128)}, u32[]{:S(2)}) copy-start(s32[1,8]{1,0:T(1,128)} %param.12) | copy-start | bytes 100
  8.5 2.3 %copy-start.1 = (bf16[1,4,8,8192]{3,2,1,0:T(8,128)(2,1)S(1)}, bf16[1,4,8,8192]{3,2,1,0:T(8,128)(2,1)}, u32[]{:S(2)}) copy-start(bf16[1,4,8,8192]{3,2,1,0:T(8,128)(2,1)} %param.9) | copy-start | bytes 1572868
  8.5 2.3 %copy-start.2 = (f32[1,8192]{1,0:T(1,128)S(1)}, f32[1,8192]{1,0:T(1,128)}, u32[]{:S(2)}) copy-start(f32[1,8192]{1,0:T(1,128)} %param.15) | copy-start | bytes 98308
  8.5 2.3 %copy-start.3 = (f32[1,8192]{1,0:T(1,128)S(1)}, f32[1,8192]{1,0:T(1,128)}, u32[]{:S(2)}) copy-start(f32[1,8192]{1,0:T(1,128)} %param.14) | copy-start | bytes 98308
  10.2 192.4 %collective-permute-start.2 = (bf16[2,2,2,8,128,128]{5,4,3,2,1,0:T(8,128)(2,1)}, bf16[2,2,2,8,128,128]{5,4,3,2,1,0:T(8,128)(2,1)}, u32[]{:S(2)}, u32[]{:S(2)}) collective-permute-start(bf16[2,2,2,8,128,128]{5,4,3,2,1,0:T(8,128)(2,1)} %broadcast_select_fusion), channel_id=1, source_target_pairs={{0,8},{8,0},{1,9},{9,1},{2,10},{10,2},{3,11},{11,3},{4,12},{12,4},... | collective-permute-start | bytes 6291464 | tf_op jit(solution)/shard_map/ppermute | solution.py:20
  10.2 0.6 copy-start.4
  22.1 11.5 %collective-permute-start = (bf16[4,4,8192]{2,1,0:T(4,128)(2,1)S(1)}, bf16[4,4,8192]{2,1,0:T(4,128)(2,1)S(1)}, u32[]{:S(2)}, u32[]{:S(2)}) collective-permute-start(bf16[4,4,8192]{2,1,0:T(4,128)(2,1)S(1)} %get-tuple-element.426), channel_id=1, source_target_pairs={{0,1},{1,2},{2,3},{3,4},{4,5},{5,6},{6,7},{8,9},{9,10},{10,11},{11... | collective-permute-start | bytes 786440 | tf_op jit(solution)/shard_map/while/body/eval_jaxpr/ppermute | solution.py:26
  44.8 10.7 %collective-permute-start = (bf16[4,4,8192]{2,1,0:T(4,128)(2,1)S(1)}, bf16[4,4,8192]{2,1,0:T(4,128)(2,1)S(1)}, u32[]{:S(2)}, u32[]{:S(2)}) collective-permute-start(bf16[4,4,8192]{2,1,0:T(4,128)(2,1)S(1)} %get-tuple-element.426), channel_id=1, source_target_pairs={{0,1},{1,2},{2,3},{3,4},{4,5},{5,6},{6,7},{8,9},{9,10},{10,11},{11... | collective-permute-start | bytes 786440 | tf_op jit(solution)/shard_map/while/body/eval_jaxpr/ppermute | solution.py:26
  66.7 9.8 %collective-permute-start = (bf16[4,4,8192]{2,1,0:T(4,128)(2,1)S(1)}, bf16[4,4,8192]{2,1,0:T(4,128)(2,1)S(1)}, u32[]{:S(2)}, u32[]{:S(2)}) collective-permute-start(bf16[4,4,8192]{2,1,0:T(4,128)(2,1)S(1)} %get-tuple-element.426), channel_id=1, source_target_pairs={{0,1},{1,2},{2,3},{3,4},{4,5},{5,6},{6,7},{8,9},{9,10},{10,11},{11... | collective-permute-start | bytes 786440 | tf_op jit(solution)/shard_map/while/body/eval_jaxpr/ppermute | solution.py:26
  87.8 9.2 %collective-permute-start = (bf16[4,4,8192]{2,1,0:T(4,128)(2,1)S(1)}, bf16[4,4,8192]{2,1,0:T(4,128)(2,1)S(1)}, u32[]{:S(2)}, u32[]{:S(2)}) collective-permute-start(bf16[4,4,8192]{2,1,0:T(4,128)(2,1)S(1)} %get-tuple-element.426), channel_id=1, source_target_pairs={{0,1},{1,2},{2,3},{3,4},{4,5},{5,6},{6,7},{8,9},{9,10},{10,11},{11... | collective-permute-start | bytes 786440 | tf_op jit(solution)/shard_map/while/body/eval_jaxpr/ppermute | solution.py:26
  108.2 9.2 %collective-permute-start = (bf16[4,4,8192]{2,1,0:T(4,128)(2,1)S(1)}, bf16[4,4,8192]{2,1,0:T(4,128)(2,1)S(1)}, u32[]{:S(2)}, u32[]{:S(2)}) collective-permute-start(bf16[4,4,8192]{2,1,0:T(4,128)(2,1)S(1)} %get-tuple-element.426), channel_id=1, source_target_pairs={{0,1},{1,2},{2,3},{3,4},{4,5},{5,6},{6,7},{8,9},{9,10},{10,11},{11... | collective-permute-start | bytes 786440 | tf_op jit(solution)/shard_map/while/body/eval_jaxpr/ppermute | solution.py:26
  128.5 9.2 %collective-permute-start = (bf16[4,4,8192]{2,1,0:T(4,128)(2,1)S(1)}, bf16[4,4,8192]{2,1,0:T(4,128)(2,1)S(1)}, u32[]{:S(2)}, u32[]{:S(2)}) collective-permute-start(bf16[4,4,8192]{2,1,0:T(4,128)(2,1)S(1)} %get-tuple-element.426), channel_id=1, source_target_pairs={{0,1},{1,2},{2,3},{3,4},{4,5},{5,6},{6,7},{8,9},{9,10},{10,11},{11... | collective-permute-start | bytes 786440 | tf_op jit(solution)/shard_map/while/body/eval_jaxpr/ppermute | solution.py:26
  148.9 9.2 %collective-permute-start = (bf16[4,4,8192]{2,1,0:T(4,128)(2,1)S(1)}, bf16[4,4,8192]{2,1,0:T(4,128)(2,1)S(1)}, u32[]{:S(2)}, u32[]{:S(2)}) collective-permute-start(bf16[4,4,8192]{2,1,0:T(4,128)(2,1)S(1)} %get-tuple-element.426), channel_id=1, source_target_pairs={{0,1},{1,2},{2,3},{3,4},{4,5},{5,6},{6,7},{8,9},{9,10},{10,11},{11... | collective-permute-start | bytes 786440 | tf_op jit(solution)/shard_map/while/body/eval_jaxpr/ppermute | solution.py:26
  169.3 9.2 %collective-permute-start = (bf16[4,4,8192]{2,1,0:T(4,128)(2,1)S(1)}, bf16[4,4,8192]{2,1,0:T(4,128)(2,1)S(1)}, u32[]{:S(2)}, u32[]{:S(2)}) collective-permute-start(bf16[4,4,8192]{2,1,0:T(4,128)(2,1)S(1)} %get-tuple-element.426), channel_id=1, source_target_pairs={{0,1},{1,2},{2,3},{3,4},{4,5},{5,6},{6,7},{8,9},{9,10},{10,11},{11... | collective-permute-start | bytes 786440 | tf_op jit(solution)/shard_map/while/body/eval_jaxpr/ppermute | solution.py:26
  189.6 9.2 %collective-permute-start = (bf16[4,4,8192]{2,1,0:T(4,128)(2,1)S(1)}, bf16[4,4,8192]{2,1,0:T(4,128)(2,1)S(1)}, u32[]{:S(2)}, u32[]{:S(2)}) collective-permute-start(bf16[4,4,8192]{2,1,0:T(4,128)(2,1)S(1)} %get-tuple-element.426), channel_id=1, source_target_pairs={{0,1},{1,2},{2,3},{3,4},{4,5},{5,6},{6,7},{8,9},{9,10},{10,11},{11... | collective-permute-start | bytes 786440 | tf_op jit(solution)/shard_map/while/body/eval_jaxpr/ppermute | solution.py:26
  199.5 1.4 collective-permute-start.1

commit v5 on v3

--- a/solution.py
+++ b/solution.py
@@ -26,10 +26,10 @@
 
 def layer(rows, keys, values, lens, gain, scale):
     steps, reqs, width = rows.shape
-    pages = keys.shape[1]
-    kv_heads = keys.shape[2]
-    page_len = keys.shape[3]
-    head = keys.shape[4]
+    pages = values.shape[1]
+    kv_heads = values.shape[2]
+    page_len = values.shape[3]
+    head = values.shape[4]
     group = width // (kv_heads * head)
     wide = rows.astype(jnp.float32)
     normed = wide * lax.rsqrt(jnp.mean(wide * wide, axis=-1, keepdims=True) + 1e-05) * gain
@@ -41,7 +41,7 @@
     factor = 1.0 / math.sqrt(head)
     wide_query = jnp.broadcast_to(query[:, None], (reqs, pages) + query.shape[1:])
     cache_scores = (
-        jnp.einsum("rjgxd,rjgpd->rjgxp", wide_query, keys, preferred_element_type=jnp.float32)
+        jnp.einsum("rjgxd,rjgdp->rjgxp", wide_query, keys, preferred_element_type=jnp.float32)
         * factor
     )
     positions = jnp.arange(pages)[:, None] * page_len + jnp.arange(page_len)[None, :]
@@ -88,7 +88,7 @@
     keep = spots[None, :, :] < lens[moving][:, None, None]
     outgoing = jnp.where(keep[:, :, None, None, :, None], outgoing, jnp.zeros((), jnp.bfloat16))
     received = partner(outgoing, "inst", 0)
-    keys = pool[:, 0][table]
+    keys = jnp.swapaxes(pool[:, 0][table], -1, -2)
     values = pool[:, 1][table]
     lens_used = lens
     section = lax.axis_index("section")

time: 187 us -> 188 us (level)
  local copies, waits for them, and re-layouts: 39.2 us -> 45.5 us
  matrix products: 40.3 us -> 35.5 us
    gather x1 -> x2, local copies, waits for them, and re-layouts: 5.2 us -> 11.6 us  [per_device(): keys = jnp.swapaxes(pool[:, 0][table], -1, -2)]
    dot_general x9, matrix products: 29.2 us -> 24.3 us  [layer(): jnp.einsum('rjgxd,rjgdp->rjgxp', wide_query, keys, preferred_element_type...]
where the time goes in v5:
time: 188 us; the launch traced here: 187 us
  waiting for transfers between devices  66.8 us (36%)
  local copies, waits for them, and re-layouts  45.5 us (24%)
  matrix products  35.5 us (19%)
  starting transfers between devices  19.5 us (10%)
  other arithmetic  17.8 us (9%)
    ppermute x9, waiting for transfers between devices, passed_along(): return lax.ppermute(array, axis, pairs)  65.5 us
    dot_general x9, matrix products, layer(): jnp.einsum('rjgxd,rjgdp->rjgxp', wide_query, keys, preferred_element_type...  24.3 us
    ppermute x9, starting transfers between devices, passed_along(): return lax.ppermute(array, axis, pairs)  19.4 us
    gather x2, local copies, waits for them, and re-layouts, per_device(): keys = jnp.swapaxes(pool[:, 0][table], -1, -2)  11.6 us
    dot_general x9, matrix products, layer(): jnp.einsum('rjgxp,rjgpd->rjgxd', cache_w, values, preferred_element_type=...  6.32 us
    squeeze x1, local copies, waits for them, and re-layouts, per_device(): values = pool[:, 1][table]  6.03 us
    gather x1, local copies, waits for them, and re-layouts, per_device(): values = pool[:, 1][table]  5.3 us
    gather x1, local copies, waits for them, and re-layouts, per_device(): outgoing = pool[chosen]  4.33 us
  transfers between devices with their start and end apart: 11, of which 10 were waited for; matrix products, arithmetic and copies ran while one was open for 46% of the time, Pallas kernels for 0%

profile of v5, /device:TPU:26, one launch (start us, length us, event | category | flops | bytes accessed | tf_op | source)
XLA Modules:
  0.0 187.4 jit_solution(6539871113230754078)
XLA Ops:
  4.1 4.3 %gather_fusion.5 = bf16[4,2,8,128,128]{4,3,2,1,0:T(8,128)(2,1)S(1)} fusion(bf16[16,2,8,128,128]{4,3,2,1,0:T(8,128)(2,1)} %bitcast.68, s32[1024]{0:T(1024)S(1)} %pad_clamp_fusion), kind=kCustom, calls=%fused_computation.5 | custom fusion | bytes 4194320 | tf_op jit(solution)/shard_map/gather | solution.py:86
  10.1 6.0 %slice_bitcast_fusion = (bf16[16,8,128,128]{3,2,1,0:T(8,128)(2,1)}, bf16[16,8,128,128]{3,2,1,0:T(8,128)(2,1)}) fusion(bf16[16,2,8,128,128]{4,3,2,1,0:T(8,128)(2,1)} %bitcast.69), kind=kLoop, calls=%fused_computation.55 | loop fusion | bytes 16777216 | tf_op jit(solution)/shard_map/squeeze | solution.py:92
  16.3 5.2 %gather_fusion = bf16[16,8,128,128]{3,2,1,0:T(8,128)(2,1)} fusion(bf16[16,8,128,128]{3,2,1,0:T(8,128)(2,1)} %get-tuple-element.339, s32[1024]{0:T(1024)S(1)} %pad_clamp_fusion.2), kind=kCustom, calls=%fused_computation | custom fusion | bytes 8388672 | tf_op jit(solution)/shard_map/gather | solution.py:91
  21.6 6.4 %copy.57 = bf16[16,8,128,128]{2,3,1,0:T(8,128)(2,1)} copy(bf16[16,8,128,128]{3,2,1,0:T(8,128)(2,1)} %gather_fusion) | data formatting | bytes 8388608 | tf_op jit(solution)/shard_map/gather | solution.py:91
  28.0 5.3 %gather_fusion.1 = bf16[16,8,128,128]{3,2,1,0:T(8,128)(2,1)} fusion(bf16[16,8,128,128]{3,2,1,0:T(8,128)(2,1)} %get-tuple-element.338, s32[1024]{0:T(1024)S(1)} %pad_clamp_fusion.2), kind=kCustom, calls=%fused_computation.1 | custom fusion | bytes 8388672 | tf_op jit(solution)/shard_map/gather | solution.py:92
  33.5 146.9 %while.17 = (s32[]{:T(128)}, bf16[4,4,8192]{2,1,0:T(4,128)(2,1)S(1)}, bf16[4,8,8192]{2,0,1:T(4,128)(2,1)S(1)}, pred[]{:T(512)}, s32[]{:T(128)}, /*index=5*/bf16[...) while((s32[]{:T(128)}, ...), condition=%wide.region_7.8_spmd, body=%wide.region_0.7_spmd.sunk | while | flops 140426912 | bytes 36353176 | solution.py:122
  35.3 2.7 %fusion.52 = (f32[4,8,32]{2,1,0:T(8,128)S(1)}, f32[4,2,8,32,128]{4,3,2,1,0:T(8,128)S(1)}) fusion(bf16[8,2,8,128,128]{4,3,2,1,0:T(8,128)(2,1)} %get-tuple-element.468, s32[]{:T(128)S(6)} %select_n.159, bf16[4,8,32,128]{3,2,1,0:T(8,128)(2,1)S(1)} %bitcast.67, pred[4,2,128]{2,1,0:T(4,128)(4,1)S(1)} %broadcast_compare_fusion.3), kind=kOutput, calls=%fused_computation.69.clone.1 | convolution fusion | flops 67894272 | bytes 3412996 | tf_op jit(solution)/shard_map/while/body/eval_jaxpr/rjgxd,rjgdp->rjgxp/dot_general | solution.py:44
  40.2 3.4 %collective-permute-start = (bf16[4,4,8192]{2,1,0:T(4,128)(2,1)S(1)}, bf16[4,4,8192]{2,1,0:T(4,128)(2,1)S(1)}, u32[]{:S(2)}, u32[]{:S(2)}) collective-permute-start(bf16[4,4,8192]{2,1,0:T(4,128)(2,1)S(1)} %get-tuple-element.425), channel_id=1, source_target_pairs={{0,1},{1,2},{2,3},{3,4},{4,5},{5,6},{6,7},{8,9},{9,10},{10,11},{11... | collective-permute-start | bytes 786440 | tf_op jit(solution)/shard_map/while/body/eval_jaxpr/ppermute | solution.py:24
  43.9 7.8 %collective-permute-done = bf16[4,4,8192]{2,1,0:T(4,128)(2,1)S(1)} collective-permute-done((bf16[4,4,8192]{2,1,0:T(4,128)(2,1)S(1)}, bf16[4,4,8192]{2,1,0:T(4,128)(2,1)S(1)}, u32[]{:S(2)}, u32[]{:S(2)}) %collective-permute-start) | collective-permute-done | bytes 262176 | tf_op jit(solution)/shard_map/while/body/eval_jaxpr/ppermute | solution.py:24
  53.4 2.7 %fusion.52 = (f32[4,8,32]{2,1,0:T(8,128)S(1)}, f32[4,2,8,32,128]{4,3,2,1,0:T(8,128)S(1)}) fusion(bf16[8,2,8,128,128]{4,3,2,1,0:T(8,128)(2,1)} %get-tuple-element.468, s32[]{:T(128)S(6)} %select_n.159, bf16[4,8,32,128]{3,2,1,0:T(8,128)(2,1)S(1)} %bitcast.67, pred[4,2,128]{2,1,0:T(4,128)(4,1)S(1)} %broadcast_compare_fusion.3), kind=kOutput, calls=%fused_computation.69.clone.1 | convolution fusion | flops 67894272 | bytes 3412996 | tf_op jit(solution)/shard_map/while/body/eval_jaxpr/rjgxd,rjgdp->rjgxp/dot_general | solution.py:44
  61.1 8.0 %collective-permute-done = bf16[4,4,8192]{2,1,0:T(4,128)(2,1)S(1)} collective-permute-done((bf16[4,4,8192]{2,1,0:T(4,128)(2,1)S(1)}, bf16[4,4,8192]{2,1,0:T(4,128)(2,1)S(1)}, u32[]{:S(2)}, u32[]{:S(2)}) %collective-permute-start) | collective-permute-done | bytes 262176 | tf_op jit(solution)/shard_map/while/body/eval_jaxpr/ppermute | solution.py:24
  70.8 2.7 %fusion.52 = (f32[4,8,32]{2,1,0:T(8,128)S(1)}, f32[4,2,8,32,128]{4,3,2,1,0:T(8,128)S(1)}) fusion(bf16[8,2,8,128,128]{4,3,2,1,0:T(8,128)(2,1)} %get-tuple-element.468, s32[]{:T(128)S(6)} %select_n.159, bf16[4,8,32,128]{3,2,1,0:T(8,128)(2,1)S(1)} %bitcast.67, pred[4,2,128]{2,1,0:T(4,128)(4,1)S(1)} %broadcast_compare_fusion.3), kind=kOutput, calls=%fused_computation.69.clone.1 | convolution fusion | flops 67894272 | bytes 3412996 | tf_op jit(solution)/shard_map/while/body/eval_jaxpr/rjgxd,rjgdp->rjgxp/dot_general | solution.py:44
  77.9 7.7 %collective-permute-done = bf16[4,4,8192]{2,1,0:T(4,128)(2,1)S(1)} collective-permute-done((bf16[4,4,8192]{2,1,0:T(4,128)(2,1)S(1)}, bf16[4,4,8192]{2,1,0:T(4,128)(2,1)S(1)}, u32[]{:S(2)}, u32[]{:S(2)}) %collective-permute-start) | collective-permute-done | bytes 262176 | tf_op jit(solution)/shard_map/while/body/eval_jaxpr/ppermute | solution.py:24
  87.3 2.7 %fusion.52 = (f32[4,8,32]{2,1,0:T(8,128)S(1)}, f32[4,2,8,32,128]{4,3,2,1,0:T(8,128)S(1)}) fusion(bf16[8,2,8,128,128]{4,3,2,1,0:T(8,128)(2,1)} %get-tuple-element.468, s32[]{:T(128)S(6)} %select_n.159, bf16[4,8,32,128]{3,2,1,0:T(8,128)(2,1)S(1)} %bitcast.67, pred[4,2,128]{2,1,0:T(4,128)(4,1)S(1)} %broadcast_compare_fusion.3), kind=kOutput, calls=%fused_computation.69.clone.1 | convolution fusion | flops 67894272 | bytes 3412996 | tf_op jit(solution)/shard_map/while/body/eval_jaxpr/rjgxd,rjgdp->rjgxp/dot_general | solution.py:44
  94.4 7.0 %collective-permute-done = bf16[4,4,8192]{2,1,0:T(4,128)(2,1)S(1)} collective-permute-done((bf16[4,4,8192]{2,1,0:T(4,128)(2,1)S(1)}, bf16[4,4,8192]{2,1,0:T(4,128)(2,1)S(1)}, u32[]{:S(2)}, u32[]{:S(2)}) %collective-permute-start) | collective-permute-done | bytes 262176 | tf_op jit(solution)/shard_map/while/body/eval_jaxpr/ppermute | solution.py:24
  103.1 2.7 %fusion.52 = (f32[4,8,32]{2,1,0:T(8,128)S(1)}, f32[4,2,8,32,128]{4,3,2,1,0:T(8,128)S(1)}) fusion(bf16[8,2,8,128,128]{4,3,2,1,0:T(8,128)(2,1)} %get-tuple-element.468, s32[]{:T(128)S(6)} %select_n.159, bf16[4,8,32,128]{3,2,1,0:T(8,128)(2,1)S(1)} %bitcast.67, pred[4,2,128]{2,1,0:T(4,128)(4,1)S(1)} %broadcast_compare_fusion.3), kind=kOutput, calls=%fused_computation.69.clone.1 | convolution fusion | flops 67894272 | bytes 3412996 | tf_op jit(solution)/shard_map/while/body/eval_jaxpr/rjgxd,rjgdp->rjgxp/dot_general | solution.py:44
  110.2 7.0 %collective-permute-done = bf16[4,4,8192]{2,1,0:T(4,128)(2,1)S(1)} collective-permute-done((bf16[4,4,8192]{2,1,0:T(4,128)(2,1)S(1)}, bf16[4,4,8192]{2,1,0:T(4,128)(2,1)S(1)}, u32[]{:S(2)}, u32[]{:S(2)}) %collective-permute-start) | collective-permute-done | bytes 262176 | tf_op jit(solution)/shard_map/while/body/eval_jaxpr/ppermute | solution.py:24
  118.9 2.7 %fusion.52 = (f32[4,8,32]{2,1,0:T(8,128)S(1)}, f32[4,2,8,32,128]{4,3,2,1,0:T(8,128)S(1)}) fusion(bf16[8,2,8,128,128]{4,3,2,1,0:T(8,128)(2,1)} %get-tuple-element.468, s32[]{:T(128)S(6)} %select_n.159, bf16[4,8,32,128]{3,2,1,0:T(8,128)(2,1)S(1)} %bitcast.67, pred[4,2,128]{2,1,0:T(4,128)(4,1)S(1)} %broadcast_compare_fusion.3), kind=kOutput, calls=%fused_computation.69.clone.1 | convolution fusion | flops 67894272 | bytes 3412996 | tf_op jit(solution)/shard_map/while/body/eval_jaxpr/rjgxd,rjgdp->rjgxp/dot_general | solution.py:44
  126.0 7.0 %collective-permute-done = bf16[4,4,8192]{2,1,0:T(4,128)(2,1)S(1)} collective-permute-done((bf16[4,4,8192]{2,1,0:T(4,128)(2,1)S(1)}, bf16[4,4,8192]{2,1,0:T(4,128)(2,1)S(1)}, u32[]{:S(2)}, u32[]{:S(2)}) %collective-permute-start) | collective-permute-done | bytes 262176 | tf_op jit(solution)/shard_map/while/body/eval_jaxpr/ppermute | solution.py:24
  141.8 7.0 %collective-permute-done = bf16[4,4,8192]{2,1,0:T(4,128)(2,1)S(1)} collective-permute-done((bf16[4,4,8192]{2,1,0:T(4,128)(2,1)S(1)}, bf16[4,4,8192]{2,1,0:T(4,128)(2,1)S(1)}, u32[]{:S(2)}, u32[]{:S(2)}) %collective-permute-start) | collective-permute-done | bytes 262176 | tf_op jit(solution)/shard_map/while/body/eval_jaxpr/ppermute | solution.py:24
  150.5 2.7 %fusion.52 = (f32[4,8,32]{2,1,0:T(8,128)S(1)}, f32[4,2,8,32,128]{4,3,2,1,0:T(8,128)S(1)}) fusion(bf16[8,2,8,128,128]{4,3,2,1,0:T(8,128)(2,1)} %get-tuple-element.468, s32[]{:T(128)S(6)} %select_n.159, bf16[4,8,32,128]{3,2,1,0:T(8,128)(2,1)S(1)} %bitcast.67, pred[4,2,128]{2,1,0:T(4,128)(4,1)S(1)} %broadcast_compare_fusion.3), kind=kOutput, calls=%fused_computation.69.clone.1 | convolution fusion | flops 67894272 | bytes 3412996 | tf_op jit(solution)/shard_map/while/body/eval_jaxpr/rjgxd,rjgdp->rjgxp/dot_general | solution.py:44
  157.6 7.0 %collective-permute-done = bf16[4,4,8192]{2,1,0:T(4,128)(2,1)S(1)} collective-permute-done((bf16[4,4,8192]{2,1,0:T(4,128)(2,1)S(1)}, bf16[4,4,8192]{2,1,0:T(4,128)(2,1)S(1)}, u32[]{:S(2)}, u32[]{:S(2)}) %collective-permute-start) | collective-permute-done | bytes 262176 | tf_op jit(solution)/shard_map/while/body/eval_jaxpr/ppermute | solution.py:24
  173.4 7.0 %collective-permute-done = bf16[4,4,8192]{2,1,0:T(4,128)(2,1)S(1)} collective-permute-done((bf16[4,4,8192]{2,1,0:T(4,128)(2,1)S(1)}, bf16[4,4,8192]{2,1,0:T(4,128)(2,1)S(1)}, u32[]{:S(2)}, u32[]{:S(2)}) %collective-permute-start) | collective-permute-done | bytes 262176 | tf_op jit(solution)/shard_map/while/body/eval_jaxpr/ppermute | solution.py:24
  184.3 3.2 %copy.117 = bf16[1,1,2,2,2,8,128,128]{7,6,5,4,3,2,1,0:T(8,128)(2,1)} copy(bf16[1,1,2,2,2,8,128,128]{7,6,5,4,3,2,1,0:T(8,128)(2,1)} %bitcast.26) | data formatting | bytes 4194304
  (288 shorter events, 66.8 us)
Async XLA Ops:
  10.1 6.0 %copy-start.5 = (s32[1,8,2]{1,2,0:T(2,128)S(1)}, s32[1,8,2]{1,2,0:T(2,128)}, u32[]{:S(2)}) copy-start(s32[1,8,2]{1,2,0:T(2,128)} %param.11) | copy-start | bytes 196
  10.1 174.2 %collective-permute-start.2 = (bf16[2,2,2,8,128,128]{5,4,3,2,1,0:T(8,128)(2,1)}, bf16[2,2,2,8,128,128]{5,4,3,2,1,0:T(8,128)(2,1)}, u32[]{:S(2)}, u32[]{:S(2)}) collective-permute-start(bf16[2,2,2,8,128,128]{5,4,3,2,1,0:T(8,128)(2,1)} %broadcast_select_fusion), channel_id=1, source_target_pairs={{0,8},{8,0},{1,9},{9,1},{2,10},{10,2},{3,11},{11,3},{4,12},{12,4},... | collective-permute-start | bytes 6291464 | tf_op jit(solution)/shard_map/ppermute | solution.py:18
  28.0 5.5 %copy-start = (s32[1,8]{1,0:T(1,128)S(1)}, s32[1,8]{1,0:T(1,128)}, u32[]{:S(2)}) copy-start(s32[1,8]{1,0:T(1,128)} %param.12) | copy-start | bytes 100
  28.0 5.5 %copy-start.2 = (bf16[1,4,8,8192]{3,2,1,0:T(8,128)(2,1)S(1)}, bf16[1,4,8,8192]{3,2,1,0:T(8,128)(2,1)}, u32[]{:S(2)}) copy-start(bf16[1,4,8,8192]{3,2,1,0:T(8,128)(2,1)} %param.9) | copy-start | bytes 1572868
  28.0 5.6 %copy-start.3 = (f32[1,8192]{1,0:T(1,128)S(1)}, f32[1,8192]{1,0:T(1,128)}, u32[]{:S(2)}) copy-start(f32[1,8192]{1,0:T(1,128)} %param.15) | copy-start | bytes 98308
  28.0 5.6 %copy-start.4 = (f32[1,8192]{1,0:T(1,128)S(1)}, f32[1,8192]{1,0:T(1,128)}, u32[]{:S(2)}) copy-start(f32[1,8192]{1,0:T(1,128)} %param.14) | copy-start | bytes 98308
  34.5 4.0 %copy-start.1 = (bf16[8,2,8,128,128]{4,3,2,1,0:T(8,128)(2,1)S(1)}, bf16[8,2,8,128,128]{4,3,2,1,0:T(8,128)(2,1)}, u32[]{:S(2)}) copy-start(bf16[8,2,8,128,128]{4,3,2,1,0:T(8,128)(2,1)} %get-tuple-element.469) | copy-start | bytes 12582916 | tf_op jit(solution)/shard_map/while
  40.2 11.5 %collective-permute-start = (bf16[4,4,8192]{2,1,0:T(4,128)(2,1)S(1)}, bf16[4,4,8192]{2,1,0:T(4,128)(2,1)S(1)}, u32[]{:S(2)}, u32[]{:S(2)}) collective-permute-start(bf16[4,4,8192]{2,1,0:T(4,128)(2,1)S(1)} %get-tuple-element.425), channel_id=1, source_target_pairs={{0,1},{1,2},{2,3},{3,4},{4,5},{5,6},{6,7},{8,9},{9,10},{10,11},{11... | collective-permute-start | bytes 786440 | tf_op jit(solution)/shard_map/while/body/eval_jaxpr/ppermute | solution.py:24
  52.7 4.0 %copy-start.1 = (bf16[8,2,8,128,128]{4,3,2,1,0:T(8,128)(2,1)S(1)}, bf16[8,2,8,128,128]{4,3,2,1,0:T(8,128)(2,1)}, u32[]{:S(2)}) copy-start(bf16[8,2,8,128,128]{4,3,2,1,0:T(8,128)(2,1)} %get-tuple-element.469) | copy-start | bytes 12582916 | tf_op jit(solution)/shard_map/while
  58.4 10.7 %collective-permute-start = (bf16[4,4,8192]{2,1,0:T(4,128)(2,1)S(1)}, bf16[4,4,8192]{2,1,0:T(4,128)(2,1)S(1)}, u32[]{:S(2)}, u32[]{:S(2)}) collective-permute-start(bf16[4,4,8192]{2,1,0:T(4,128)(2,1)S(1)} %get-tuple-element.425), channel_id=1, source_target_pairs={{0,1},{1,2},{2,3},{3,4},{4,5},{5,6},{6,7},{8,9},{9,10},{10,11},{11... | collective-permute-start | bytes 786440 | tf_op jit(solution)/shard_map/while/body/eval_jaxpr/ppermute | solution.py:24
  70.0 4.0 %copy-start.1 = (bf16[8,2,8,128,128]{4,3,2,1,0:T(8,128)(2,1)S(1)}, bf16[8,2,8,128,128]{4,3,2,1,0:T(8,128)(2,1)}, u32[]{:S(2)}) copy-start(bf16[8,2,8,128,128]{4,3,2,1,0:T(8,128)(2,1)} %get-tuple-element.469) | copy-start | bytes 12582916 | tf_op jit(solution)/shard_map/while
  75.7 9.8 %collective-permute-start = (bf16[4,4,8192]{2,1,0:T(4,128)(2,1)S(1)}, bf16[4,4,8192]{2,1,0:T(4,128)(2,1)S(1)}, u32[]{:S(2)}, u32[]{:S(2)}) collective-permute-start(bf16[4,4,8192]{2,1,0:T(4,128)(2,1)S(1)} %get-tuple-element.425), channel_id=1, source_target_pairs={{0,1},{1,2},{2,3},{3,4},{4,5},{5,6},{6,7},{8,9},{9,10},{10,11},{11... | collective-permute-start | bytes 786440 | tf_op jit(solution)/shard_map/while/body/eval_jaxpr/ppermute | solution.py:24
  86.5 4.0 %copy-start.1 = (bf16[8,2,8,128,128]{4,3,2,1,0:T(8,128)(2,1)S(1)}, bf16[8,2,8,128,128]{4,3,2,1,0:T(8,128)(2,1)}, u32[]{:S(2)}) copy-start(bf16[8,2,8,128,128]{4,3,2,1,0:T(8,128)(2,1)} %get-tuple-element.469) | copy-start | bytes 12582916 | tf_op jit(solution)/shard_map/while
  92.2 9.2 %collective-permute-start = (bf16[4,4,8192]{2,1,0:T(4,128)(2,1)S(1)}, bf16[4,4,8192]{2,1,0:T(4,128)(2,1)S(1)}, u32[]{:S(2)}, u32[]{:S(2)}) collective-permute-start(bf16[4,4,8192]{2,1,0:T(4,128)(2,1)S(1)} %get-tuple-element.425), channel_id=1, source_target_pairs={{0,1},{1,2},{2,3},{3,4},{4,5},{5,6},{6,7},{8,9},{9,10},{10,11},{11... | collective-permute-start | bytes 786440 | tf_op jit(solution)/shard_map/while/body/eval_jaxpr/ppermute | solution.py:24
  102.3 4.0 %copy-start.1 = (bf16[8,2,8,128,128]{4,3,2,1,0:T(8,128)(2,1)S(1)}, bf16[8,2,8,128,128]{4,3,2,1,0:T(8,128)(2,1)}, u32[]{:S(2)}) copy-start(bf16[8,2,8,128,128]{4,3,2,1,0:T(8,128)(2,1)} %get-tuple-element.469) | copy-start | bytes 12582916 | tf_op jit(solution)/shard_map/while
  108.0 9.2 %collective-permute-start = (bf16[4,4,8192]{2,1,0:T(4,128)(2,1)S(1)}, bf16[4,4,8192]{2,1,0:T(4,128)(2,1)S(1)}, u32[]{:S(2)}, u32[]{:S(2)}) collective-permute-start(bf16[4,4,8192]{2,1,0:T(4,128)(2,1)S(1)} %get-tuple-element.425), channel_id=1, source_target_pairs={{0,1},{1,2},{2,3},{3,4},{4,5},{5,6},{6,7},{8,9},{9,10},{10,11},{11... | collective-permute-start | bytes 786440 | tf_op jit(solution)/shard_map/while/body/eval_jaxpr/ppermute | solution.py:24
  118.1 4.0 %copy-start.1 = (bf16[8,2,8,128,128]{4,3,2,1,0:T(8,128)(2,1)S(1)}, bf16[8,2,8,128,128]{4,3,2,1,0:T(8,128)(2,1)}, u32[]{:S(2)}) copy-start(bf16[8,2,8,128,128]{4,3,2,1,0:T(8,128)(2,1)} %get-tuple-element.469) | copy-start | bytes 12582916 | tf_op jit(solution)/shard_map/while
  123.8 9.2 %collective-permute-start = (bf16[4,4,8192]{2,1,0:T(4,128)(2,1)S(1)}, bf16[4,4,8192]{2,1,0:T(4,128)(2,1)S(1)}, u32[]{:S(2)}, u32[]{:S(2)}) collective-permute-start(bf16[4,4,8192]{2,1,0:T(4,128)(2,1)S(1)} %get-tuple-element.425), channel_id=1, source_target_pairs={{0,1},{1,2},{2,3},{3,4},{4,5},{5,6},{6,7},{8,9},{9,10},{10,11},{11... | collective-permute-start | bytes 786440 | tf_op jit(solution)/shard_map/while/body/eval_jaxpr/ppermute | solution.py:24
  133.9 4.0 %copy-start.1 = (bf16[8,2,8,128,128]{4,3,2,1,0:T(8,128)(2,1)S(1)}, bf16[8,2,8,128,128]{4,3,2,1,0:T(8,128)(2,1)}, u32[]{:S(2)}) copy-start(bf16[8,2,8,128,128]{4,3,2,1,0:T(8,128)(2,1)} %get-tuple-element.469) | copy-start | bytes 12582916 | tf_op jit(solution)/shard_map/while
  139.6 9.2 %collective-permute-start = (bf16[4,4,8192]{2,1,0:T(4,128)(2,1)S(1)}, bf16[4,4,8192]{2,1,0:T(4,128)(2,1)S(1)}, u32[]{:S(2)}, u32[]{:S(2)}) collective-permute-start(bf16[4,4,8192]{2,1,0:T(4,128)(2,1)S(1)} %get-tuple-element.425), channel_id=1, source_target_pairs={{0,1},{1,2},{2,3},{3,4},{4,5},{5,6},{6,7},{8,9},{9,10},{10,11},{11... | collective-permute-start | bytes 786440 | tf_op jit(solution)/shard_map/while/body/eval_jaxpr/ppermute | solution.py:24
  149.7 4.0 %copy-start.1 = (bf16[8,2,8,128,128]{4,3,2,1,0:T(8,128)(2,1)S(1)}, bf16[8,2,8,128,128]{4,3,2,1,0:T(8,128)(2,1)}, u32[]{:S(2)}) copy-start(bf16[8,2,8,128,128]{4,3,2,1,0:T(8,128)(2,1)} %get-tuple-element.469) | copy-start | bytes 12582916 | tf_op jit(solution)/shard_map/while
  155.5 9.2 %collective-permute-start = (bf16[4,4,8192]{2,1,0:T(4,128)(2,1)S(1)}, bf16[4,4,8192]{2,1,0:T(4,128)(2,1)S(1)}, u32[]{:S(2)}, u32[]{:S(2)}) collective-permute-start(bf16[4,4,8192]{2,1,0:T(4,128)(2,1)S(1)} %get-tuple-element.425), channel_id=1, source_target_pairs={{0,1},{1,2},{2,3},{3,4},{4,5},{5,6},{6,7},{8,9},{9,10},{10,11},{11... | collective-permute-start | bytes 786440 | tf_op jit(solution)/shard_map/while/body/eval_jaxpr/ppermute | solution.py:24
  171.3 9.2 %collective-permute-start = (bf16[4,4,8192]{2,1,0:T(4,128)(2,1)S(1)}, bf16[4,4,8192]{2,1,0:T(4,128)(2,1)S(1)}, u32[]{:S(2)}, u32[]{:S(2)}) collective-permute-start(bf16[4,4,8192]{2,1,0:T(4,128)(2,1)S(1)} %get-tuple-element.425), channel_id=1, source_target_pairs={{0,1},{1,2},{2,3},{3,4},{4,5},{5,6},{6,7},{8,9},{9,10},{10,11},{11... | collective-permute-start | bytes 786440 | tf_op jit(solution)/shard_map/while/body/eval_jaxpr/ppermute | solution.py:24
  181.1 1.4 collective-permute-start.1
  (1 other events, 4.0 us)

commit v6 on v4

--- a/solution.py
+++ b/solution.py
@@ -7,7 +7,7 @@
 from jax.experimental import pallas as pl
 from jax.experimental.pallas import tpu as pltpu
 
-CHUNKS = 2
+CHUNKS = 4
 
 
 def partner(block, axis, stride):
@@ -195,12 +195,15 @@
     chunks = CHUNKS
     block = reqs // chunks
 
-    def tick(k, carry):
-        incoming, finished = carry
+    incoming = jnp.zeros((steps, block, width), jnp.bfloat16)
+    finished = jnp.zeros((steps, reqs, width), jnp.bfloat16)
+    zero = jnp.zeros((), jnp.int32)
+    for k in range(chunks + count - 1):
         item = k - section
         live = jnp.logical_and(item >= 0, item < chunks)
         start = jnp.clip(item, 0, chunks - 1) * block
-        zero = jnp.zeros((), jnp.int32)
+        if k > 0:
+            start, incoming = lax.optimization_barrier((start, incoming))
         first = lax.dynamic_slice_in_dim(inputs, start, block, 1)
         rows = jnp.where(section == 0, first, incoming)
         result = layer_paged(rows, pool, table, lens_used, start, gain, scale)
@@ -208,14 +211,9 @@
         finished = lax.dynamic_update_slice(
             finished, jnp.where(live, result, previous), (zero, start, zero)
         )
-        passed = passed_along(result, "section", 1)
-        return (passed, finished)
-
-    start_carry = (
-        jnp.zeros((steps, block, width), jnp.bfloat16),
-        jnp.zeros((steps, reqs, width), jnp.bfloat16),
-    )
-    _, finished = lax.fori_loop(0, chunks + count - 1, tick, start_carry)
+        pairs = [(s, s + 1) for s in range(count - 1) if 0 <= k - s < chunks]
+        if pairs:
+            incoming = lax.ppermute(result, "section", pairs)
     handed = partner(finished[:, moving], "inst", 0)
     finished = finished.at[:, moving].set(handed)
     return (finished[None, None], received[None, None])

time: 208 us -> 193 us (0.928)
  waiting for transfers between devices: 66.8 us -> 45.2 us
  local copies, waits for them, and re-layouts: 43.3 us -> 56.8 us
  other arithmetic: 12.2 us -> 22.9 us
  Pallas kernels: 62.4 us -> 52.2 us
  starting transfers between devices: 19.5 us -> 12.2 us
    ppermute x9 -> x10, waiting for transfers between devices: 65.5 us -> 43.8 us  [per_device(): incoming = lax.ppermute(result, 'section', pairs)]
    pallas_call x9 -> x11, Pallas kernels: 62.4 us -> 52.2 us  [attend(): pl.pallas_call(attend_kernel, grid_spec=grid_spec, out_shape=jax.ShapeDty...]
    ppermute x9 -> x10, starting transfers between devices: 19.4 us -> 12.1 us  [per_device(): incoming = lax.ppermute(result, 'section', pairs)]
    unnamed x14 -> x27, local copies, waits for them, and re-layouts: 4.57 us -> 10.9 us
    reshape x9 -> x11, local copies, waits for them, and re-layouts: 1.83 us -> 7.72 us  [layer_paged(): jnp.transpose(attended, (2, 0, 1, 3, 4)).reshape(steps, reqs, width)]
    while x10 -> x0, local copies, waits for them, and re-layouts: 5.65 us -> none
    dynamic_update_slice x0 -> x11, other arithmetic: none -> 5.51 us  [per_device(): lax.dynamic_update_slice(finished, jnp.where(live, result, previous), (ze...]
    reshape x9 -> x10, local copies, waits for them, and re-layouts: 3.25 us -> 8.41 us  [layer_paged(): heads = normed.reshape(steps, reqs, kv_heads, group, head)]
  transfers between devices with their start and end apart: 11 -> 12, of which waited for: 10 -> 6; matrix products, arithmetic and copies ran while one was open for 21% -> 11% of each run, Pallas kernels for 30% -> 2%
where the time goes in v6:
time: 193 us; the launch traced here: 191 us
  local copies, waits for them, and re-layouts  56.8 us (29%)
  Pallas kernels  52.2 us (27%)
  waiting for transfers between devices  45.2 us (23%)
  other arithmetic  22.9 us (12%)
  starting transfers between devices  12.2 us (6%)
    pallas_call x11, Pallas kernels, attend(): pl.pallas_call(attend_kernel, grid_spec=grid_spec, out_shape=jax.ShapeDty...  52.2 us
    ppermute x10, waiting for transfers between devices, per_device(): incoming = lax.ppermute(result, 'section', pairs)  43.8 us
    transpose x11, local copies, waits for them, and re-layouts, layer_paged(): jnp.transpose(attended, (2, 0, 1, 3, 4)).reshape(steps, reqs, width)  13.5 us
    ppermute x10, starting transfers between devices, per_device(): incoming = lax.ppermute(result, 'section', pairs)  12.1 us
    unnamed x27, local copies, waits for them, and re-layouts  10.9 us
    reshape x10, local copies, waits for them, and re-layouts, layer_paged(): heads = normed.reshape(steps, reqs, kv_heads, group, head)  8.41 us
    reshape x11, local copies, waits for them, and re-layouts, layer_paged(): jnp.transpose(attended, (2, 0, 1, 3, 4)).reshape(steps, reqs, width)  7.72 us
    transpose x10, local copies, waits for them, and re-layouts, layer_paged(): query = jnp.transpose(heads.astype(jnp.bfloat16), (1, 2, 0, 3, 4))  6.76 us
  transfers between devices with their start and end apart: 12, of which 6 were waited for; matrix products, arithmetic and copies ran while one was open for 11% of the time, Pallas kernels for 2%

profile of v6, /device:TPU:26, one launch (start us, length us, event | category | flops | bytes accessed | tf_op | source)
XLA Modules:
  0.0 190.6 jit_solution(18328164199101207735)
XLA Ops:
  6.0 4.9 %shard_map.86 = f32[2,8,32,128]{3,2,1,0:T(8,128)} custom-call(s32[16]{0:T(128)} %reshape_squeeze.2.table_ref, s32[8]{0:T(128)} %bitcast.299, s32[1]{0:T(128)} %bitcast.3.start_ref, bf16[2,8,32,128]{3,2,1,0:T(8,128)(2,1)} %get-tuple-element.91.q_ref, bf16[2,8,4,128]{3,2,1,0:T(4,128)(2,1)} %fusion.39.f_ref, bf16[16,2,8,128,128]{4,3,2,1,0:T(8,128)(2,1)} %bitcast.254, ...), custom_call_target="tpu_custom_call" | custom-call | tf_op jit(solution)/shard_map/pallas_call | solution.py:151
  15.2 4.7 %shard_map.87 = f32[2,8,32,128]{3,2,1,0:T(8,128)} custom-call(s32[16]{0:T(128)} %reshape_squeeze.2.table_ref, s32[8]{0:T(128)} %bitcast.300, s32[1]{0:T(128)} %bitcast.12.start_ref, bf16[2,8,32,128]{3,2,1,0:T(8,128)(2,1)} %bitcast.348, bf16[2,8,4,128]{3,2,1,0:T(4,128)(2,1)} %bitcast.360, bf16[16,2,8,128,128]{4,3,2,1,0:T(8,128)(2,1)} %bitcast.258, ...), custom_call_target="tpu_custom_call" | custom-call | tf_op jit(solution)/shard_map/pallas_call | solution.py:151
  24.0 4.7 %shard_map.88 = f32[2,8,32,128]{3,2,1,0:T(8,128)} custom-call(s32[16]{0:T(128)} %reshape_squeeze.2.table_ref, s32[8]{0:T(128)} %bitcast.301, s32[1]{0:T(128)} %bitcast.20.start_ref, bf16[2,8,32,128]{3,2,1,0:T(8,128)(2,1)} %bitcast.349, bf16[2,8,4,128]{3,2,1,0:T(4,128)(2,1)} %bitcast.361, bf16[16,2,8,128,128]{4,3,2,1,0:T(8,128)(2,1)} %bitcast.262, ...), custom_call_target="tpu_custom_call" | custom-call | tf_op jit(solution)/shard_map/pallas_call | solution.py:151
  32.8 4.7 %shard_map.89 = f32[2,8,32,128]{3,2,1,0:T(8,128)} custom-call(s32[16]{0:T(128)} %reshape_squeeze.2.table_ref, s32[8]{0:T(128)} %bitcast.302, s32[1]{0:T(128)} %bitcast.27.start_ref, bf16[2,8,32,128]{3,2,1,0:T(8,128)(2,1)} %bitcast.350, bf16[2,8,4,128]{3,2,1,0:T(4,128)(2,1)} %bitcast.362, bf16[16,2,8,128,128]{4,3,2,1,0:T(8,128)(2,1)} %bitcast.266, ...), custom_call_target="tpu_custom_call" | custom-call | tf_op jit(solution)/shard_map/pallas_call | solution.py:151
  41.6 4.9 %shard_map.90 = f32[2,8,32,128]{3,2,1,0:T(8,128)} custom-call(s32[16]{0:T(128)} %reshape_squeeze.2.table_ref, s32[8]{0:T(128)} %bitcast.303, s32[1]{0:T(128)} %bitcast.34.start_ref, bf16[2,8,32,128]{3,2,1,0:T(8,128)(2,1)} %bitcast.351, bf16[2,8,4,128]{3,2,1,0:T(4,128)(2,1)} %bitcast.363, bf16[16,2,8,128,128]{4,3,2,1,0:T(8,128)(2,1)} %bitcast.270, ...), custom_call_target="tpu_custom_call" | custom-call | tf_op jit(solution)/shard_map/pallas_call | solution.py:151
  51.4 4.7 %shard_map.91 = f32[2,8,32,128]{3,2,1,0:T(8,128)} custom-call(s32[16]{0:T(128)} %reshape_squeeze.2.table_ref, s32[8]{0:T(128)} %bitcast.304, s32[1]{0:T(128)} %bitcast.41.start_ref, bf16[2,8,32,128]{3,2,1,0:T(8,128)(2,1)} %bitcast.352, bf16[2,8,4,128]{3,2,1,0:T(4,128)(2,1)} %bitcast.364, bf16[16,2,8,128,128]{4,3,2,1,0:T(8,128)(2,1)} %bitcast.276, ...), custom_call_target="tpu_custom_call" | custom-call | tf_op jit(solution)/shard_map/pallas_call | solution.py:151
  58.7 30.8 %collective-permute-done.5 = bf16[4,2,8192]{2,0,1:T(4,128)(2,1)S(1)} collective-permute-done((bf16[4,2,8192]{2,0,1:T(4,128)(2,1)S(1)}, bf16[4,2,8192]{2,0,1:T(4,128)(2,1)S(1)}, u32[]{:S(2)}, u32[]{:S(2)}) %collective-permute-start.5) | collective-permute-done | bytes 131104 | tf_op jit(solution)/shard_map/ppermute | solution.py:216
  91.7 4.7 %shard_map.92 = f32[2,8,32,128]{3,2,1,0:T(8,128)} custom-call(s32[16]{0:T(128)} %reshape_squeeze.2.table_ref, s32[8]{0:T(128)} %bitcast.305, s32[1]{0:T(128)} %bitcast.48.start_ref, bf16[2,8,32,128]{3,2,1,0:T(8,128)(2,1)} %bitcast.353, bf16[2,8,4,128]{3,2,1,0:T(4,128)(2,1)} %bitcast.365, bf16[16,2,8,128,128]{4,3,2,1,0:T(8,128)(2,1)} %bitcast.278, ...), custom_call_target="tpu_custom_call" | custom-call | tf_op jit(solution)/shard_map/pallas_call | solution.py:151
  97.7 1.9 %collective-permute-start.6 = (bf16[4,2,8192]{2,0,1:T(4,128)(2,1)S(1)}, bf16[4,2,8192]{2,0,1:T(4,128)(2,1)S(1)}, u32[]{:S(2)}, u32[]{:S(2)}) collective-permute-start(bf16[4,2,8192]{2,0,1:T(4,128)(2,1)S(1)} %get-tuple-element.65), channel_id=1, source_target_pairs={{3,4},{4,5},{5,6},{6,7},{11,12},{12,13},{13,14},{14,15},{19,20},{2... | collective-permute-start | bytes 393224 | tf_op jit(solution)/shard_map/ppermute | solution.py:216
  100.3 4.3 %gather_fusion.3 = bf16[4,2,8,128,128]{4,3,2,1,0:T(8,128)(2,1)S(1)} fusion(bf16[16,2,8,128,128]{4,3,2,1,0:T(8,128)(2,1)} %bitcast.282, s32[1024]{0:T(1024)S(1)} %pad_clamp_fusion), kind=kCustom, calls=%fused_computation.3 | custom fusion | bytes 4194320 | tf_op jit(solution)/shard_map/gather | solution.py:187
  106.7 1.8 reshape.387
  111.0 4.7 %shard_map.93 = f32[2,8,32,128]{3,2,1,0:T(8,128)} custom-call(s32[16]{0:T(128)} %reshape_squeeze.2.table_ref, s32[8]{0:T(128)} %bitcast.306, s32[1]{0:T(128)} %bitcast.55.start_ref, bf16[2,8,32,128]{3,2,1,0:T(8,128)(2,1)} %bitcast.354, bf16[2,8,4,128]{3,2,1,0:T(4,128)(2,1)} %bitcast.366, bf16[16,2,8,128,128]{4,3,2,1,0:T(8,128)(2,1)} %bitcast.283, ...), custom_call_target="tpu_custom_call" | custom-call | tf_op jit(solution)/shard_map/pallas_call | solution.py:151
  117.4 1.8 reshape.390
  120.2 1.9 %collective-permute-start.7 = (bf16[4,2,8192]{2,0,1:T(4,128)(2,1)S(1)}, bf16[4,2,8192]{2,0,1:T(4,128)(2,1)S(1)}, u32[]{:S(2)}, u32[]{:S(2)}) collective-permute-start(bf16[4,2,8192]{2,0,1:T(4,128)(2,1)S(1)} %get-tuple-element.61), channel_id=1, source_target_pairs={{4,5},{5,6},{6,7},{12,13},{13,14},{14,15},{20,21},{21,22},{22,23},... | collective-permute-start | bytes 393224 | tf_op jit(solution)/shard_map/ppermute | solution.py:216
  122.2 5.8 %collective-permute-done.7 = bf16[4,2,8192]{2,0,1:T(4,128)(2,1)S(1)} collective-permute-done((bf16[4,2,8192]{2,0,1:T(4,128)(2,1)S(1)}, bf16[4,2,8192]{2,0,1:T(4,128)(2,1)S(1)}, u32[]{:S(2)}, u32[]{:S(2)}) %collective-permute-start.7) | collective-permute-done | bytes 131104 | tf_op jit(solution)/shard_map/ppermute | solution.py:216
  129.3 1.8 reshape.392
  133.6 4.7 %shard_map.94 = f32[2,8,32,128]{3,2,1,0:T(8,128)} custom-call(s32[16]{0:T(128)} %reshape_squeeze.2.table_ref, s32[8]{0:T(128)} %bitcast.307, s32[1]{0:T(128)} %bitcast.62.start_ref, bf16[2,8,32,128]{3,2,1,0:T(8,128)(2,1)} %bitcast.355, bf16[2,8,4,128]{3,2,1,0:T(4,128)(2,1)} %bitcast.367, bf16[16,2,8,128,128]{4,3,2,1,0:T(8,128)(2,1)} %bitcast.287, ...), custom_call_target="tpu_custom_call" | custom-call | tf_op jit(solution)/shard_map/pallas_call | solution.py:151
  139.9 1.8 reshape.395
  142.8 1.9 %collective-permute-start.8 = (bf16[4,2,8192]{2,0,1:T(4,128)(2,1)S(1)}, bf16[4,2,8192]{2,0,1:T(4,128)(2,1)S(1)}, u32[]{:S(2)}, u32[]{:S(2)}) collective-permute-start(bf16[4,2,8192]{2,0,1:T(4,128)(2,1)S(1)} %get-tuple-element.57), channel_id=1, source_target_pairs={{5,6},{6,7},{13,14},{14,15},{21,22},{22,23},{29,30},{30,31}} | collective-permute-start | bytes 393224 | tf_op jit(solution)/shard_map/ppermute | solution.py:216
  144.8 5.8 %collective-permute-done.8 = bf16[4,2,8192]{2,0,1:T(4,128)(2,1)S(1)} collective-permute-done((bf16[4,2,8192]{2,0,1:T(4,128)(2,1)S(1)}, bf16[4,2,8192]{2,0,1:T(4,128)(2,1)S(1)}, u32[]{:S(2)}, u32[]{:S(2)}) %collective-permute-start.8) | collective-permute-done | bytes 131104 | tf_op jit(solution)/shard_map/ppermute | solution.py:216
  151.8 1.8 reshape.397
  156.1 4.7 %shard_map.95 = f32[2,8,32,128]{3,2,1,0:T(8,128)} custom-call(s32[16]{0:T(128)} %reshape_squeeze.2.table_ref, s32[8]{0:T(128)} %bitcast.308, s32[1]{0:T(128)} %bitcast.69.start_ref, bf16[2,8,32,128]{3,2,1,0:T(8,128)(2,1)} %bitcast.356, bf16[2,8,4,128]{3,2,1,0:T(4,128)(2,1)} %bitcast.368, bf16[16,2,8,128,128]{4,3,2,1,0:T(8,128)(2,1)} %bitcast.291, ...), custom_call_target="tpu_custom_call" | custom-call | tf_op jit(solution)/shard_map/pallas_call | solution.py:151
  172.0 1.8 reshape.402
  176.2 4.7 %shard_map.96 = f32[2,8,32,128]{3,2,1,0:T(8,128)} custom-call(s32[16]{0:T(128)} %reshape_squeeze.2.table_ref, s32[8]{0:T(128)} %bitcast.309, s32[1]{0:T(128)} %bitcast.76.start_ref, bf16[2,8,32,128]{3,2,1,0:T(8,128)(2,1)} %bitcast.347, bf16[2,8,4,128]{3,2,1,0:T(4,128)(2,1)} %bitcast.359, bf16[16,2,8,128,128]{4,3,2,1,0:T(8,128)(2,1)} %bitcast.295, ...), custom_call_target="tpu_custom_call" | custom-call | tf_op jit(solution)/shard_map/pallas_call | solution.py:151
  (175 shorter events, 73.7 us)
Async XLA Ops:
  0.6 1.0 copy-start
  6.0 6.1 %copy-start.2 = (f32[1,8192]{1,0:T(1,128)S(1)}, f32[1,8192]{1,0:T(1,128)}, u32[]{:S(2)}) copy-start(f32[1,8192]{1,0:T(1,128)} %param.13) | copy-start | bytes 98308
  10.9 2.6 %copy-start.3 = (f32[1,8192]{1,0:T(1,128)S(1)}, f32[1,8192]{1,0:T(1,128)}, u32[]{:S(2)}) copy-start(f32[1,8192]{1,0:T(1,128)} %param.12) | copy-start | bytes 98308
  12.3 0.7 collective-permute-start
  21.1 0.7 collective-permute-start.1
  29.9 0.7 collective-permute-start.2
  38.7 0.7 collective-permute-start.3
  41.6 7.0 %copy-start.6 = (s32[1,2]{1,0:T(1,128)S(1)}, s32[1,2]{1,0:T(1,128)}, u32[]{:S(2)}) copy-start(s32[1,2]{1,0:T(1,128)} %param.11) | copy-start | bytes 28
  41.6 7.0 %copy-start.5 = (s32[1,8,2]{1,2,0:T(2,128)S(1)}, s32[1,8,2]{1,2,0:T(2,128)}, u32[]{:S(2)}) copy-start(s32[1,8,2]{1,2,0:T(2,128)} %param.9) | copy-start | bytes 196
  47.7 1.6 collective-permute-start.4
  57.3 32.2 %collective-permute-start.5 = (bf16[4,2,8192]{2,0,1:T(4,128)(2,1)S(1)}, bf16[4,2,8192]{2,0,1:T(4,128)(2,1)S(1)}, u32[]{:S(2)}, u32[]{:S(2)}) collective-permute-start(bf16[4,2,8192]{2,0,1:T(4,128)(2,1)S(1)} %get-tuple-element.69), channel_id=1, source_target_pairs={{2,3},{3,4},{4,5},{5,6},{10,11},{11,12},{12,13},{13,14},{18,19},{1... | collective-permute-start | bytes 393224 | tf_op jit(solution)/shard_map/ppermute | solution.py:216
  96.4 3.2 %copy-start.1 = (s32[1,8]{1,0:T(1,128)S(1)}, s32[1,8]{1,0:T(1,128)}, u32[]{:S(2)}) copy-start(s32[1,8]{1,0:T(1,128)} %param.10) | copy-start | bytes 100
  97.7 7.8 %collective-permute-start.6 = (bf16[4,2,8192]{2,0,1:T(4,128)(2,1)S(1)}, bf16[4,2,8192]{2,0,1:T(4,128)(2,1)S(1)}, u32[]{:S(2)}, u32[]{:S(2)}) collective-permute-start(bf16[4,2,8192]{2,0,1:T(4,128)(2,1)S(1)} %get-tuple-element.65), channel_id=1, source_target_pairs={{3,4},{4,5},{5,6},{6,7},{11,12},{12,13},{13,14},{14,15},{19,20},{2... | collective-permute-start | bytes 393224 | tf_op jit(solution)/shard_map/ppermute | solution.py:216
  120.2 7.8 %collective-permute-start.7 = (bf16[4,2,8192]{2,0,1:T(4,128)(2,1)S(1)}, bf16[4,2,8192]{2,0,1:T(4,128)(2,1)S(1)}, u32[]{:S(2)}, u32[]{:S(2)}) collective-permute-start(bf16[4,2,8192]{2,0,1:T(4,128)(2,1)S(1)} %get-tuple-element.61), channel_id=1, source_target_pairs={{4,5},{5,6},{6,7},{12,13},{13,14},{14,15},{20,21},{21,22},{22,23},... | collective-permute-start | bytes 393224 | tf_op jit(solution)/shard_map/ppermute | solution.py:216
  142.8 7.8 %collective-permute-start.8 = (bf16[4,2,8192]{2,0,1:T(4,128)(2,1)S(1)}, bf16[4,2,8192]{2,0,1:T(4,128)(2,1)S(1)}, u32[]{:S(2)}, u32[]{:S(2)}) collective-permute-start(bf16[4,2,8192]{2,0,1:T(4,128)(2,1)S(1)} %get-tuple-element.57), channel_id=1, source_target_pairs={{5,6},{6,7},{13,14},{14,15},{21,22},{22,23},{29,30},{30,31}} | collective-permute-start | bytes 393224 | tf_op jit(solution)/shard_map/ppermute | solution.py:216
  165.4 3.8 %collective-permute-start.9 = (bf16[4,2,8192]{2,0,1:T(4,128)(2,1)S(1)}, bf16[4,2,8192]{2,0,1:T(4,128)(2,1)S(1)}, u32[]{:S(2)}, u32[]{:S(2)}) collective-permute-start(bf16[4,2,8192]{2,0,1:T(4,128)(2,1)S(1)} %get-tuple-element.53), channel_id=1, source_target_pairs={{6,7},{14,15},{22,23},{30,31}} | collective-permute-start | bytes 393224 | tf_op jit(solution)/shard_map/ppermute | solution.py:216
  168.5 20.8 %collective-permute-start.11 = (bf16[2,2,2,8,128,128]{5,4,3,2,1,0:T(8,128)(2,1)}, bf16[2,2,2,8,128,128]{5,4,3,2,1,0:T(8,128)(2,1)S(1)}, u32[]{:S(2)}, u32[]{:S(2)}) collective-permute-start(bf16[2,2,2,8,128,128]{5,4,3,2,1,0:T(8,128)(2,1)} %broadcast_select_fusion), channel_id=1, source_target_pairs={{0,8},{8,0},{1,9},{9,1},{2,10},{10,2},{3,11},{11,3},{4,12},{12,4},... | collective-permute-start | bytes 6291464 | tf_op jit(solution)/shard_map/ppermute | solution.py:20
  169.2 0.7 copy-start.4
  186.1 1.4 collective-permute-start.10
